TPU v7x, 512 devices: a whole 4x8x8 slice. The times are simulated.
512 devices in a mesh: spec: 32 (over x, y), tile: 16 (over z, core).
Axes of the slice: x: 4, y: 8, z: 8, core: 2. Of those that a mesh axis runs over, the one named last changes fastest.
Arguments:
- spectrum: float32 [1152, 64, 2048], P('spec', None, 'tile'), may hold values from 0.1 to 2
- depth_speed: float32 [64, 2048], P(None, 'tile'), may hold values from 0.5 to 1
- turning: float32 [64, 2048], P(None, 'tile'), may hold values from -0.5 to 0.5
- drift: float32 [1152], replicated, may hold values from -0.4 to 0.4
- partners: int32 [2, 1152], replicated, may hold values from 0 to 1151, as said below
- sea_slots: int32 [32, 16, 192], P(None, 'tile'), may hold values from 0 to 255, as said below
- sea_counts: int32 [32, 16], P(None, 'tile'), may hold values from 64 to 192
Outputs:
- new_spectrum: float32 [1152, 64, 2048], P(None, 'spec', 'tile')
Inputs may be any that keep to these rules, and one draw needn't show every extreme that they name: partners[0, k] and partners[1, k] for k = f * 36 + d are components of frequency min(f + a_f, 31) and max(f - b_f, 0) and directions (d + c_f) and (d - e_f) modulo 36, with a_f, b_f, c_f, e_f between 1 and 3 and fixed for each frequency. sea_slots[j, t] names 192 distinct cells of block (j, t); its first sea_counts[j, t] entries are the block's sea cells, the others are land cells.
All inputs are finite; a program needn't handle non-finite values.
Results may differ from a plain program's by a relative error of at most 0.000075.
Values sent between devices are 32-bit elements; how exact they have to be, the bound alone decides.
No kernel may reach another device: no remote copies, remote signals or barrier semaphores. Data moves between devices by JAX's collectives and lax.ppermute only.
A program may use at most 64 MiB of HBM per device.

v0:
```python
import jax
import jax.numpy as jnp
from jax import lax
from jax.sharding import PartitionSpec as P

ND = 36
NF = 32


speed_top = 0.6
decline = 0.0953102
dia_coeff = 0.25


def extended(cells, sides, width):
    for axis, dim in sides:
        count = lax.axis_size(axis)
        head = lax.slice_in_dim(cells, 0, width, axis=dim)
        tail = lax.slice_in_dim(cells, cells.shape[dim] - width, cells.shape[dim], axis=dim)
        cells = jnp.concatenate(
            [
                lax.ppermute(tail, axis, [(i, (i + 1) % count) for i in range(count)]),
                cells,
                lax.ppermute(head, axis, [((i + 1) % count, i) for i in range(count)]),
            ],
            axis=dim,
        )
    return cells


def sea_cells(sea_list, sea_total, per_block):
    cell_ids = jnp.arange(per_block, dtype=jnp.int32)
    slot_rank = jnp.arange(sea_list.shape[1], dtype=jnp.int32)
    is_live = slot_rank[None, :] < sea_total[:, None]
    matches = (sea_list[:, :, None] == cell_ids[None, None, :]) & is_live[:, :, None]
    return jnp.any(matches, axis=1).astype(jnp.float32)


def advect_space(energy_ext, depth_ext, speeds, cosines, sine_part, sea_mask):
    east_rate = (speeds * cosines)[:, None, None] * depth_ext[None]
    north_rate = (speeds * sine_part)[:, None, None] * depth_ext[None, :, 1:-1]
    centre = energy_ext[:, :, 1:-1]
    east_mid = east_rate[:, :, 1:-1]
    inflow = (
        jnp.maximum(east_rate[:, :, :-2], 0.0) * energy_ext[:, :, :-2]
        + jnp.maximum(-east_rate[:, :, 2:], 0.0) * energy_ext[:, :, 2:]
    )
    empty_row = jnp.zeros_like(centre[:, :1])
    from_south = jnp.concatenate(
        [empty_row, (jnp.maximum(north_rate, 0.0) * centre)[:, :-1]], axis=1
    )
    from_north = jnp.concatenate(
        [(jnp.maximum(-north_rate, 0.0) * centre)[:, 1:], empty_row], axis=1
    )
    updated = (
        centre
        - (jnp.abs(east_mid) + jnp.abs(north_rate)) * centre
        + inflow
        + from_south
        + from_north
    )
    return updated * sea_mask


def advect_direction(energy, turning):
    turn_plus = jnp.maximum(turning, 0.0)
    behind = jnp.maximum(-turning, 0.0)
    return (
        energy
        - jnp.abs(turning) * energy
        + turn_plus * jnp.roll(energy, 1, axis=1)
        + behind * jnp.roll(energy, -1, axis=1)
    )


def advect_frequency(energy, drift, n_freq, n_dir):
    shaped = energy.reshape(n_freq, n_dir, -1)
    drift_rate = drift.reshape(n_freq, n_dir, 1)
    upward = jnp.maximum(drift_rate, 0.0) * shaped
    downward = jnp.maximum(-drift_rate, 0.0) * shaped
    empty_row = jnp.zeros_like(shaped[:1])
    from_below = jnp.concatenate([empty_row, upward[:-1]], axis=0)
    from_above = jnp.concatenate([downward[1:], empty_row], axis=0)
    return (shaped - jnp.abs(drift_rate) * shaped + from_below + from_above).reshape(energy.shape)


def pick_rows(lookup_ids, values):
    columns = jnp.arange(values.shape[0], dtype=jnp.int32)

    def pick_one_block(wanted):
        one_hot = (wanted[:, None] == columns[None, :]).astype(jnp.float32)
        return jnp.dot(
            one_hot, values, precision=lax.Precision.HIGHEST, preferred_element_type=jnp.float32
        )

    return lax.map(pick_one_block, lookup_ids.reshape(3, -1)).reshape(values.shape)


def spread_rows(lookup_ids, values):
    targets = jnp.arange(values.shape[0], dtype=jnp.int32).reshape(3, -1)

    def spread_one_block(target_rows):
        one_hot = (target_rows[:, None] == lookup_ids[None, :]).astype(jnp.float32)
        return jnp.dot(
            one_hot, values, precision=lax.Precision.HIGHEST, preferred_element_type=jnp.float32
        )

    return lax.map(spread_one_block, targets).reshape(values.shape)


def shards(spectrum, depth_speed, turning, drift, partners, sea_slots, sea_counts):
    channels, grid_rows, grid_cols = spectrum.shape
    n_spec = lax.axis_size("spec")
    sub_rows = grid_rows // n_spec
    per_block = sub_rows * grid_cols
    sea_list = sea_slots[:, 0, :]
    sea_mask = sea_cells(sea_list, sea_counts[:, 0], per_block).reshape(grid_rows, grid_cols)
    energy = spectrum * sea_mask
    stacked = jnp.concatenate([energy, depth_speed[None]], axis=0)
    padded = extended(stacked, (("tile", 2),), 1)
    local_freq = channels // ND
    freq_ids = (
        lax.axis_index("spec") * local_freq + jnp.arange(local_freq, dtype=jnp.int32)
    ).astype(jnp.float32)
    speeds = jnp.repeat(speed_top * jnp.exp(-decline * freq_ids), ND)
    angles = 2.0 * jnp.pi * jnp.arange(ND, dtype=jnp.float32) / ND
    cosines = jnp.tile(jnp.cos(angles), local_freq)
    sine_part = jnp.tile(jnp.sin(angles), local_freq)
    spaced = advect_space(padded[:channels], padded[channels], speeds, cosines, sine_part, sea_mask)
    turned = advect_direction(spaced.reshape(local_freq, ND, grid_rows, grid_cols), turning)
    turned = turned.reshape(channels, grid_rows, grid_cols)
    points = lax.all_to_all(turned, "spec", split_axis=1, concat_axis=0, tiled=True)
    n_comps, point_rows, item_count = points.shape
    flattened = points.reshape(n_comps, point_rows * item_count)
    shifted = advect_frequency(flattened, drift, NF, ND)
    plus_values = pick_rows(partners[0], shifted)
    minus_values = pick_rows(partners[1], shifted)
    quartet = (
        shifted * shifted * (plus_values + minus_values)
        - 2.0 * shifted * plus_values * minus_values
    )
    source = spread_rows(partners[0], quartet) + spread_rows(partners[1], quartet) - 2.0 * quartet
    return (shifted + dia_coeff * source).reshape(n_comps, point_rows, item_count)


def solution(mesh):
    return jax.shard_map(
        shards,
        mesh=mesh,
        in_specs=(
            P("spec", None, "tile"),
            P(None, "tile"),
            P(None, "tile"),
            P(),
            P(),
            P(None, "tile", None),
            P(None, "tile"),
        ),
        out_specs=P(None, "spec", "tile"),
        check_vma=False,
    )
```

profile of v0, /device:TPU:201, one launch (start us, length us, event | category | flops | bytes accessed | tf_op | source)
XLA Modules:
  0.0 109.3 jit_solution(11014818217788500441)
XLA Ops:
  0.0 0.8 copy.62
  0.8 0.7 iota_compare_fusion.13
  1.5 2.3 %fusion.33 = pred[32,256]{1,0:T(8,128)(4,1)S(1)} fusion(s32[32,192]{1,0:T(8,128)S(1)} %bitcast.80, pred[32,192]{1,0:T(8,128)(4,1)S(1)} %iota_compare_fusion.13), kind=kLoop, calls=%fused_computation.30 | loop fusion | flops 4710400 | bytes 38912 | tf_op jit(solution)/shard_map/reduce_or | solution.py:36
  3.9 1.4 %broadcast_multiply_fusion.2 = f32[36,64,128]{2,1,0:T(8,128)S(1)} fusion(f32[36,64,128]{2,1,0:T(8,128)} %param.15, f32[64,128]{1,0:T(8,128)S(1)} %reshape.164), kind=kLoop, calls=%fused_computation.76 | loop fusion | flops 294912 | bytes 2392064 | tf_op jit(solution)/shard_map/mul | solution.py:118
  5.2 1.5 %slice_maximum_fusion = (f32[37,64,1]{2,1,0:T(8,128)}, f32[37,64,1]{2,1,0:T(8,128)S(1)}) fusion(f32[1,64,128]{2,1,0:T(8,128)S(1)} %bitcast.77, f32[36,64,128]{2,1,0:T(8,128)S(1)} %broadcast_multiply_fusion.2), kind=kLoop, calls=%fused_computation.35 | loop fusion | flops 4736 | bytes 1231360 | tf_op jit(solution)/shard_map/concatenate | solution.py:119
  6.7 1.7 %copy.43 = f32[37,64,1]{1,0,2:T(8,128)S(1)} copy(f32[37,64,1]{2,1,0:T(8,128)} %get-tuple-element.177) | data formatting | bytes 18944 | tf_op jit(solution)/shard_map/slice | solution.py:19
  8.4 3.9 %collective-permute-start = (f32[37,64,1]{1,0,2:T(8,128)S(1)}, f32[37,64,1]{1,0,2:T(8,128)S(1)}, u32[]{:S(2)}, u32[]{:S(2)}) collective-permute-start(f32[37,64,1]{1,0,2:T(8,128)S(1)} %copy.43), channel_id=1, source_target_pairs={{0,1},{1,2},{2,3},{3,4},{4,5},{5,6},{6,7},{7,8},{8,9},{9,10},{10,1... | collective-permute-start | bytes 28424 | tf_op jit(solution)/shard_map/ppermute | solution.py:22
  13.7 3.5 %collective-permute-done.1 = f32[37,64,1]{1,0,2:T(8,128)S(1)} collective-permute-done((f32[37,64,1]{1,0,2:T(8,128)S(1)}, f32[37,64,1]{1,0,2:T(8,128)S(1)}, u32[]{:S(2)}, u32[]{:S(2)}) %collective-permute-start.1) | collective-permute-done | bytes 9504 | tf_op jit(solution)/shard_map/ppermute | solution.py:24
  17.2 1.5 %copy.46 = f32[37,64,1]{2,1,0:T(8,128)} copy(f32[37,64,1]{1,0,2:T(8,128)S(1)} %collective-permute-done.1) | data formatting | bytes 18944 | tf_op jit(solution)/shard_map/ppermute | solution.py:24
  18.6 0.8 fusion.50
  20.5 1.0 copy-done.1
  21.6 1.6 %fusion.37 = f32[36,64,128]{2,1,0:T(8,128)S(1)} fusion(f32[36,64,128]{2,1,0:T(8,128)S(1)} %broadcast_multiply_fusion.2, f32[37,64,1]{2,1,0:T(8,128)S(1)} %copy-done.1, f32[1,64,128]{2,1,0:T(8,128)S(1)} %bitcast.79, f32[36,64,130]{2,1,0:T(8,128)S(1)} %broadcast_multiply_fusion, f32[37,64,1]{2,1,0:T(8,128)S(1)} %copy.45, ...), kind=kLoop, calls=%fused_computation.39 | loop fusion | flops 5898240 | bytes 8338064 | tf_op jit(solution)/shard_map/mul | solution.py:62
  24.0 1.8 %copy.49 = f32[36,64,128]{2,0,1:T(8,128)} copy(f32[36,64,128]{2,1,0:T(8,128)S(1)} %fusion.39) | data formatting | bytes 2359296 | tf_op jit(solution)/shard_map/add | solution.py:69
  25.8 9.7 %all-to-all-start = ((f32[36,64,128]{2,0,1:T(8,128)}), f32[36,64,128]{2,0,1:T(8,128)S(1)}, u32[]{:S(2)}, u32[]{:S(2)}) async-start(f32[36,64,128]{2,0,1:T(8,128)} %copy.49), calls=%async_computation | async-start | bytes 2621440 | tf_op jit(solution)/shard_map/all_to_all | solution.py:132
  38.0 29.4 %all-to-all-done = f32[36,64,128]{2,0,1:T(8,128)S(1)} async-done(((f32[36,64,128]{2,0,1:T(8,128)}), f32[36,64,128]{2,0,1:T(8,128)S(1)}, u32[]{:S(2)}, u32[]{:S(2)}) %all-to-all-start) | async-done | bytes 1179680 | tf_op jit(solution)/shard_map/all_to_all | solution.py:132
  68.0 0.9 reshape_reshape.3
  69.7 1.8 %copy.54 = f32[32,36,256]{2,1,0:T(8,128)} copy(f32[32,36,256]{2,0,1:T(8,128)S(1)} %fusion.41) | data formatting | bytes 2359296 | tf_op jit(solution)/shard_map/add | solution.py:84
  71.4 1.4 %reshape.159 = f32[1152,256]{1,0:T(8,128)S(1)} reshape(f32[32,36,256]{2,1,0:T(8,128)} %copy.54) | data formatting | bytes 2359296 | tf_op jit(solution)/shard_map/reshape | solution.py:84
  73.0 5.7 %while.44 = (s32[]{:T(128)}, f32[3,384,256]{2,1,0:T(8,128)S(1)}, s32[3,384]{1,0:T(4,128)}, f32[1152,256]{1,0:T(8,128)S(1)}, s32[]{:T(128)}) while((s32[]{:T(128)}, f32[3,384,256]{2,1,0:T(8,128)S(1)}, s32[3,384]{1,0:T(4,128)}, f32[1152,256]{1,0:T(8,128)S(1)}, s32[]{:T(128)}) %tuple.78), condition=%wide.region_2.3_spmd.clone, body=%wide.region_1.2_spmd.clone.sunk | while | flops 1359396864 | bytes 1578053 | solution.py:96
  73.0 0.7 dynamic-slice_reduce_fusion.10
  73.7 1.2 %fusion.74 = f32[3,384,256]{2,1,0:T(8,128)S(1)} fusion(f32[3,384,256]{2,1,0:T(8,128)S(1)} %get-tuple-element.326, s32[]{:T(128)} %get-tuple-element.325, f32[1152,256]{1,0:T(8,128)S(1)} %get-tuple-element.333, s32[384]{0:T(512)S(1)} %dynamic-slice_reduce_fusion.10), kind=kOutput, calls=%fused_computation.19.clone.1 | convolution fusion | flops 1359396864 | bytes 1574916 | tf_op jit(solution)/shard_map/while/body/eval_jaxpr/dot_general | solution.py:92
  74.9 0.7 dynamic-slice_reduce_fusion.10
  75.6 1.2 %fusion.74 = f32[3,384,256]{2,1,0:T(8,128)S(1)} fusion(f32[3,384,256]{2,1,0:T(8,128)S(1)} %get-tuple-element.326, s32[]{:T(128)} %get-tuple-element.325, f32[1152,256]{1,0:T(8,128)S(1)} %get-tuple-element.333, s32[384]{0:T(512)S(1)} %dynamic-slice_reduce_fusion.10), kind=kOutput, calls=%fused_computation.19.clone.1 | convolution fusion | flops 1359396864 | bytes 1574916 | tf_op jit(solution)/shard_map/while/body/eval_jaxpr/dot_general | solution.py:92
  76.8 0.7 dynamic-slice_reduce_fusion.10
  77.5 1.2 %fusion.74 = f32[3,384,256]{2,1,0:T(8,128)S(1)} fusion(f32[3,384,256]{2,1,0:T(8,128)S(1)} %get-tuple-element.326, s32[]{:T(128)} %get-tuple-element.325, f32[1152,256]{1,0:T(8,128)S(1)} %get-tuple-element.333, s32[384]{0:T(512)S(1)} %dynamic-slice_reduce_fusion.10), kind=kOutput, calls=%fused_computation.19.clone.1 | convolution fusion | flops 1359396864 | bytes 1574916 | tf_op jit(solution)/shard_map/while/body/eval_jaxpr/dot_general | solution.py:92
  78.7 3.6 %while.45 = (s32[]{:T(128)}, f32[3,384,256]{2,1,0:T(8,128)S(1)}, s32[3,384]{1,0:T(4,128)S(1)}, f32[1152,256]{1,0:T(8,128)S(1)}, s32[]{:T(128)}) while((s32[]{:T(128)}, f32[3,384,256]{2,1,0:T(8,128)S(1)}, s32[3,384]{1,0:T(4,128)S(1)}, f32[1152,256]{1,0:T(8,128)S(1)}, s32[]{:T(128)}) %tuple.87), condition=%wide.region_4.5_spmd.clone, body=%wide.region_3.4_spmd.clone.sunk | while | flops 1359396864 | bytes 1578053 | solution.py:96
  78.8 1.2 %fusion.76 = f32[3,384,256]{2,1,0:T(8,128)S(1)} fusion(f32[3,384,256]{2,1,0:T(8,128)S(1)} %get-tuple-element.311, s32[]{:T(128)} %get-tuple-element.310, f32[1152,256]{1,0:T(8,128)S(1)} %get-tuple-element.318, s32[384]{0:T(512)S(1)} %dynamic-slice_reduce_fusion.11), kind=kOutput, calls=%fused_computation.25.clone.1 | convolution fusion | flops 1359396864 | bytes 1574916 | tf_op jit(solution)/shard_map/while/body/eval_jaxpr/dot_general | solution.py:92
  80.0 1.2 %fusion.76 = f32[3,384,256]{2,1,0:T(8,128)S(1)} fusion(f32[3,384,256]{2,1,0:T(8,128)S(1)} %get-tuple-element.311, s32[]{:T(128)} %get-tuple-element.310, f32[1152,256]{1,0:T(8,128)S(1)} %get-tuple-element.318, s32[384]{0:T(512)S(1)} %dynamic-slice_reduce_fusion.11), kind=kOutput, calls=%fused_computation.25.clone.1 | convolution fusion | flops 1359396864 | bytes 1574916 | tf_op jit(solution)/shard_map/while/body/eval_jaxpr/dot_general | solution.py:92
  81.2 1.2 %fusion.76 = f32[3,384,256]{2,1,0:T(8,128)S(1)} fusion(f32[3,384,256]{2,1,0:T(8,128)S(1)} %get-tuple-element.311, s32[]{:T(128)} %get-tuple-element.310, f32[1152,256]{1,0:T(8,128)S(1)} %get-tuple-element.318, s32[384]{0:T(512)S(1)} %dynamic-slice_reduce_fusion.11), kind=kOutput, calls=%fused_computation.25.clone.1 | convolution fusion | flops 1359396864 | bytes 1574916 | tf_op jit(solution)/shard_map/while/body/eval_jaxpr/dot_general | solution.py:92
  82.4 1.6 %reshape.162 = f32[1152,2,128]{2,1,0:T(2,128)} reshape(f32[3,384,256]{2,1,0:T(8,128)S(1)} %get-tuple-element.113) | data formatting | bytes 2359296 | tf_op jit(solution)/shard_map/reshape | solution.py:96
  84.0 1.5 %fusion.49 = f32[1152,256]{1,0:T(8,128)S(1)} fusion(f32[3,384,256]{2,1,0:T(8,128)} %copy-done.2, f32[3,384,256]{2,1,0:T(8,128)S(1)} %get-tuple-element.113, f32[1152,256]{1,0:T(8,128)S(1)} %get-tuple-element.378), kind=kLoop, calls=%fused_computation.68 | loop fusion | flops 2064384 | bytes 4718592 | tf_op jit(solution)/shard_map/sub | solution.py:139
  85.5 2.9 %reshape.163 = f32[1152,2,128]{2,1,0:T(2,128)} reshape(f32[3,384,256]{2,1,0:T(8,128)} %copy-done.2) | data formatting | bytes 2359296 | tf_op jit(solution)/shard_map/reshape | solution.py:96
  88.4 1.6 %reshape.155 = f32[1152,2,128]{2,1,0:T(2,128)} reshape(f32[32,36,256]{2,1,0:T(8,128)S(1)} %copy-done) | data formatting | bytes 2359296 | tf_op jit(solution)/shard_map/reshape | solution.py:84
  90.1 5.6 %while.43 = (s32[]{:T(128)}, f32[3,384,256]{2,1,0:T(8,128)S(1)}, s32[3,384]{1,0:T(4,128)}, s32[1,1152]{1,0:T(1,128)S(1)}, f32[1152,256]{1,0:T(8,128)S(1)}, /*index=5*/s32[]{:T(128)}, s32[]{:T(128)}) while((s32[]{:T(128)}, f32[3,384,256]{2,1,0:T(8,128)S(1)}, s32[3,384]{1,0:T(4,128)}, s32[1,1152]{1,0:T(1,128)S(1)}, f32[1152,256]{1,0:T(8,128)S(1)}, ...), condition=%wide.region_8.9_spmd, body=%wide.region_7.8_spmd.sunk | while | flops 1359396864 | bytes 1595481 | solution.py:108
  90.2 0.7 dynamic-slice_reduce_fusion.9
  90.9 1.1 %fusion.72 = f32[3,384,256]{2,1,0:T(8,128)S(1)} fusion(f32[3,384,256]{2,1,0:T(8,128)S(1)} %get-tuple-element.364, s32[]{:T(128)} %get-tuple-element.363, f32[1152,256]{1,0:T(8,128)S(1)} %get-tuple-element.374, s32[1152]{0:T(1024)S(1)} %reduce.23, s32[384]{0:T(512)S(1)} %dynamic-slice_reduce_fusion.9), kind=kOutput, calls=%fused_computation.12.clone.1 | convolution fusion | flops 1359396864 | bytes 1583108 | tf_op jit(solution)/shard_map/while/body/eval_jaxpr/dot_general | solution.py:104
  92.0 0.7 dynamic-slice_reduce_fusion.9
  92.8 1.1 %fusion.72 = f32[3,384,256]{2,1,0:T(8,128)S(1)} fusion(f32[3,384,256]{2,1,0:T(8,128)S(1)} %get-tuple-element.364, s32[]{:T(128)} %get-tuple-element.363, f32[1152,256]{1,0:T(8,128)S(1)} %get-tuple-element.374, s32[1152]{0:T(1024)S(1)} %reduce.23, s32[384]{0:T(512)S(1)} %dynamic-slice_reduce_fusion.9), kind=kOutput, calls=%fused_computation.12.clone.1 | convolution fusion | flops 1359396864 | bytes 1583108 | tf_op jit(solution)/shard_map/while/body/eval_jaxpr/dot_general | solution.py:104
  93.9 0.7 dynamic-slice_reduce_fusion.9
  94.6 1.1 %fusion.72 = f32[3,384,256]{2,1,0:T(8,128)S(1)} fusion(f32[3,384,256]{2,1,0:T(8,128)S(1)} %get-tuple-element.364, s32[]{:T(128)} %get-tuple-element.363, f32[1152,256]{1,0:T(8,128)S(1)} %get-tuple-element.374, s32[1152]{0:T(1024)S(1)} %reduce.23, s32[384]{0:T(512)S(1)} %dynamic-slice_reduce_fusion.9), kind=kOutput, calls=%fused_computation.12.clone.1 | convolution fusion | flops 1359396864 | bytes 1583108 | tf_op jit(solution)/shard_map/while/body/eval_jaxpr/dot_general | solution.py:104
  95.8 7.7 %while.42 = (s32[]{:T(128)}, f32[3,384,256]{2,1,0:T(8,128)S(1)}, s32[3,384]{1,0:T(4,128)}, s32[1,1152]{1,0:T(1,128)}, f32[1152,256]{1,0:T(8,128)S(1)}, /*index=5*/s32[]{:T(128)}, s32[]{:T(128)}) while((s32[]{:T(128)}, f32[3,384,256]{2,1,0:T(8,128)S(1)}, s32[3,384]{1,0:T(4,128)}, s32[1,1152]{1,0:T(1,128)}, f32[1152,256]{1,0:T(8,128)S(1)}, ...), condition=%wide.region_6.7_spmd, body=%wide.region_5.6_spmd.sunk | while | flops 1359396864 | bytes 1595481 | solution.py:108
  95.9 0.7 dynamic-slice_reduce_fusion.8
  97.3 1.1 %fusion.69 = f32[3,384,256]{2,1,0:T(8,128)S(1)} fusion(f32[3,384,256]{2,1,0:T(8,128)S(1)} %get-tuple-element.343, s32[]{:T(128)} %get-tuple-element.342, f32[1152,256]{1,0:T(8,128)S(1)} %get-tuple-element.353, s32[1152]{0:T(1024)S(1)} %reduce.21, s32[384]{0:T(512)S(1)} %dynamic-slice_reduce_fusion.8), kind=kOutput, calls=%fused_computation.5.clone.1 | convolution fusion | flops 1359396864 | bytes 1583108 | tf_op jit(solution)/shard_map/while/body/eval_jaxpr/dot_general | solution.py:104
  99.8 1.1 %fusion.69 = f32[3,384,256]{2,1,0:T(8,128)S(1)} fusion(f32[3,384,256]{2,1,0:T(8,128)S(1)} %get-tuple-element.343, s32[]{:T(128)} %get-tuple-element.342, f32[1152,256]{1,0:T(8,128)S(1)} %get-tuple-element.353, s32[1152]{0:T(1024)S(1)} %reduce.21, s32[384]{0:T(512)S(1)} %dynamic-slice_reduce_fusion.8), kind=kOutput, calls=%fused_computation.5.clone.1 | convolution fusion | flops 1359396864 | bytes 1583108 | tf_op jit(solution)/shard_map/while/body/eval_jaxpr/dot_general | solution.py:104
  101.0 0.7 dynamic-slice_reduce_fusion.8
  102.4 1.1 %fusion.69 = f32[3,384,256]{2,1,0:T(8,128)S(1)} fusion(f32[3,384,256]{2,1,0:T(8,128)S(1)} %get-tuple-element.343, s32[]{:T(128)} %get-tuple-element.342, f32[1152,256]{1,0:T(8,128)S(1)} %get-tuple-element.353, s32[1152]{0:T(1024)S(1)} %reduce.21, s32[384]{0:T(512)S(1)} %dynamic-slice_reduce_fusion.8), kind=kOutput, calls=%fused_computation.5.clone.1 | convolution fusion | flops 1359396864 | bytes 1583108 | tf_op jit(solution)/shard_map/while/body/eval_jaxpr/dot_general | solution.py:104
  103.7 1.6 %add.79 = f32[1152,2,128]{2,1,0:T(2,128)} reshape(f32[3,384,256]{2,1,0:T(8,128)S(1)} %add.78) | data formatting | bytes 2359296 | tf_op jit(solution)/shard_map/add | solution.py:142
  105.5 3.8 %multiply_add_fusion = f32[1152,2,128]{2,1,0:T(2,128)} fusion(f32[1152,2,128]{2,1,0:T(2,128)} %reshape.155, f32[1152,2,128]{2,1,0:T(2,128)} %add.79, f32[1152,2,128]{2,1,0:T(2,128)S(1)} %copy-done.4, f32[1152,2,128]{2,1,0:T(2,128)S(1)} %copy-done.3), kind=kLoop, calls=%fused_computation.71 | loop fusion | flops 3244032 | bytes 5898240 | tf_op jit(solution)/shard_map/add | solution.py:143
  (63 shorter events, 10.5 us)
Async XLA Ops:
  3.8 1.4 %copy-start.5 = (f32[64,128]{1,0:T(8,128)S(1)}, f32[64,128]{1,0:T(8,128)}, u32[]{:S(2)}) copy-start(f32[64,128]{1,0:T(8,128)} %param.16) | copy-start | bytes 98308
  6.7 6.2 %copy-start.6 = (f32[64,128]{1,0:T(8,128)S(1)}, f32[64,128]{1,0:T(8,128)}, u32[]{:S(2)}) copy-start(f32[64,128]{1,0:T(8,128)} %param.17) | copy-start | bytes 98308
  8.4 4.8 %collective-permute-start = (f32[37,64,1]{1,0,2:T(8,128)S(1)}, f32[37,64,1]{1,0,2:T(8,128)S(1)}, u32[]{:S(2)}, u32[]{:S(2)}) collective-permute-start(f32[37,64,1]{1,0,2:T(8,128)S(1)} %copy.43), channel_id=1, source_target_pairs={{0,1},{1,2},{2,3},{3,4},{4,5},{5,6},{6,7},{7,8},{8,9},{9,10},{10,1... | collective-permute-start | bytes 28424 | tf_op jit(solution)/shard_map/ppermute | solution.py:22
  12.7 4.4 %collective-permute-start.1 = (f32[37,64,1]{1,0,2:T(8,128)S(1)}, f32[37,64,1]{1,0,2:T(8,128)S(1)}, u32[]{:S(2)}, u32[]{:S(2)}) collective-permute-start(f32[37,64,1]{1,0,2:T(8,128)S(1)} %copy.44), channel_id=1, source_target_pairs={{1,0},{2,1},{3,2},{4,3},{5,4},{6,5},{7,6},{8,7},{9,8},{10,9},{11,1... | collective-permute-start | bytes 28424 | tf_op jit(solution)/shard_map/ppermute | solution.py:24
  20.3 1.3 %copy-start.1 = (f32[37,64,1]{2,1,0:T(8,128)S(1)}, f32[37,64,1]{2,1,0:T(8,128)}, u32[]{:S(2)}) copy-start(f32[37,64,1]{2,1,0:T(8,128)} %copy.46) | copy-start | bytes 28420
  25.8 9.8 %copy-start.8 = (f32[1152]{0:T(1024)S(1)}, f32[1152]{0:T(1024)}, u32[]{:S(2)}) copy-start(f32[1152]{0:T(1024)} %param.18) | copy-start | bytes 13828
  25.8 10.4 %copy-start.7 = (s32[2,1152]{1,0:T(2,128)S(1)}, s32[2,1152]{1,0:T(2,128)}, u32[]{:S(2)}) copy-start(s32[2,1152]{1,0:T(2,128)} %param.19) | copy-start | bytes 27652
  25.8 41.6 %all-to-all-start = ((f32[36,64,128]{2,0,1:T(8,128)}), f32[36,64,128]{2,0,1:T(8,128)S(1)}, u32[]{:S(2)}, u32[]{:S(2)}) async-start(f32[36,64,128]{2,0,1:T(8,128)} %copy.49), calls=%async_computation | async-start | bytes 2621440 | tf_op jit(solution)/shard_map/all_to_all | solution.py:132
  82.3 1.6 %copy-start.2 = (f32[3,384,256]{2,1,0:T(8,128)}, f32[3,384,256]{2,1,0:T(8,128)S(1)}, u32[]{:S(2)}) copy-start(f32[3,384,256]{2,1,0:T(8,128)S(1)} %get-tuple-element.114) | copy-start | bytes 3538948
  85.5 2.9 %copy-start = (f32[32,36,256]{2,1,0:T(8,128)S(1)}, f32[32,36,256]{2,1,0:T(8,128)}, u32[]{:S(2)}) copy-start(f32[32,36,256]{2,1,0:T(8,128)} %copy.54) | copy-start | bytes 3538948
  103.7 1.6 %copy-start.3 = (f32[1152,2,128]{2,1,0:T(2,128)S(1)}, f32[1152,2,128]{2,1,0:T(2,128)}, u32[]{:S(2)}) copy-start(f32[1152,2,128]{2,1,0:T(2,128)} %reshape.162) | copy-start | bytes 3538948
  103.7 1.9 %copy-start.4 = (f32[1152,2,128]{2,1,0:T(2,128)S(1)}, f32[1152,2,128]{2,1,0:T(2,128)}, u32[]{:S(2)}) copy-start(f32[1152,2,128]{2,1,0:T(2,128)} %reshape.163) | copy-start | bytes 3538948
where the time goes:
time: 111 us; the launch traced here: 109 us
  waiting for transfers between devices  33.2 us (30%)
  local copies, waits for them, and re-layouts  29.5 us (27%)
  other arithmetic  18.8 us (17%)
  starting transfers between devices  13.6 us (12%)
  matrix products  13.6 us (12%)
    all_to_all x1, waiting for transfers between devices, shards(): lax.all_to_all(turned, 'spec', split_axis=1, concat_axis=0, tiled=True)  29.4 us
    all_to_all x1, starting transfers between devices, shards(): lax.all_to_all(turned, 'spec', split_axis=1, concat_axis=0, tiled=True)  9.74 us
    dot_general x6, matrix products, pick_one_block(): jnp.dot(one_hot, values, precision=lax.Precision.HIGHEST, preferred_eleme...  6.92 us
    dot_general x6, matrix products, spread_one_block(): jnp.dot(one_hot, values, precision=lax.Precision.HIGHEST, preferred_eleme...  6.66 us
    dynamic_slice x12, local copies, waits for them, and re-layouts, pick_rows(): lax.map(pick_one_block, lookup_ids.reshape(3, -1)).reshape(values.shape)  6.5 us
    reshape x2, local copies, waits for them, and re-layouts, pick_rows(): lax.map(pick_one_block, lookup_ids.reshape(3, -1)).reshape(values.shape)  4.51 us
    ppermute x1, starting transfers between devices, extended(): lax.ppermute(tail, axis, [(i, (i + 1) % count) for i in range(count)])  3.88 us
    add x1, other arithmetic, shards(): shifted + dia_coeff * source  3.76 us
  transfers between devices with their start and end apart: 3, of which 3 were waited for; matrix products, arithmetic and copies ran while one was open for 3% of the time, Pallas kernels for 0%

commit v1 on v0

--- a/solution.py
+++ b/solution.py
@@ -84,28 +84,74 @@
     return (shaped - jnp.abs(drift_rate) * shaped + from_below + from_above).reshape(energy.shape)
 
 
-def pick_rows(lookup_ids, values):
-    columns = jnp.arange(values.shape[0], dtype=jnp.int32)
-
-    def pick_one_block(wanted):
-        one_hot = (wanted[:, None] == columns[None, :]).astype(jnp.float32)
-        return jnp.dot(
-            one_hot, values, precision=lax.Precision.HIGHEST, preferred_element_type=jnp.float32
-        )
-
-    return lax.map(pick_one_block, lookup_ids.reshape(3, -1)).reshape(values.shape)
+def shift_freq(x, s, up):
+    if s == 0:
+        return x
+    n = x.shape[0]
+    if up:
+        return jnp.concatenate([x[s:], jnp.repeat(x[n - 1 :], s, axis=0)], axis=0)
+    return jnp.concatenate([jnp.repeat(x[:1], s, axis=0), x[: n - s]], axis=0)
 
 
-def spread_rows(lookup_ids, values):
-    targets = jnp.arange(values.shape[0], dtype=jnp.int32).reshape(3, -1)
+def pad_freq(x, s, up):
+    if s == 0:
+        return x
+    n = x.shape[0]
+    zeros = jnp.zeros_like(x[:s])
+    if up:
+        return jnp.concatenate([x[s:], zeros], axis=0)
+    return jnp.concatenate([zeros, x[: n - s]], axis=0)
 
-    def spread_one_block(target_rows):
-        one_hot = (target_rows[:, None] == lookup_ids[None, :]).astype(jnp.float32)
-        return jnp.dot(
-            one_hot, values, precision=lax.Precision.HIGHEST, preferred_element_type=jnp.float32
-        )
 
-    return lax.map(spread_one_block, targets).reshape(values.shape)
+def pick_shift(choice, options):
+    out = options[-1]
+    for i in range(len(options) - 2, -1, -1):
+        out = jnp.where(choice == i + 1, options[i], out)
+    return out
+
+
+def settle(points, drift, partners):
+    n_freq = NF
+    shape = points.shape
+    grid = points.reshape(n_freq, ND, -1)
+    shifted = advect_frequency(grid, drift, NF, ND).reshape(n_freq, ND, -1)
+    freq_ids = jnp.arange(n_freq, dtype=jnp.int32)
+    up_ids = partners[0].reshape(n_freq, ND)[:, 0]
+    down_ids = partners[1].reshape(n_freq, ND)[:, 0]
+    up_freq = up_ids // ND
+    down_freq = down_ids // ND
+    up_turn = (up_ids % ND)[:, None, None]
+    down_turn = (ND - down_ids % ND)[:, None, None]
+    up_step = (up_freq - freq_ids)[:, None, None]
+    down_step = (freq_ids - down_freq)[:, None, None]
+
+    def by_freq(step, up):
+        out = shifted
+        for s in (1, 2, 3):
+            out = jnp.where(step == s, shift_freq(shifted, s, up), out)
+        return out
+
+    up_src = by_freq(up_step, True)
+    down_src = by_freq(down_step, False)
+    plus_values = pick_shift(up_turn, [jnp.roll(up_src, -r, axis=1) for r in (1, 2, 3)])
+    minus_values = pick_shift(down_turn, [jnp.roll(down_src, r, axis=1) for r in (1, 2, 3)])
+    quartet = (
+        shifted * shifted * (plus_values + minus_values)
+        - 2.0 * shifted * plus_values * minus_values
+    )
+    back_up = pick_shift(up_turn, [jnp.roll(quartet, r, axis=1) for r in (1, 2, 3)])
+    back_down = pick_shift(down_turn, [jnp.roll(quartet, -r, axis=1) for r in (1, 2, 3)])
+    to_up = jnp.zeros_like(quartet)
+    to_down = jnp.zeros_like(quartet)
+    for s in (0, 1, 2, 3):
+        src_up = pad_freq(up_freq, s, False)
+        hit_up = (src_up == freq_ids) & (freq_ids >= s)
+        to_up = to_up + jnp.where(hit_up[:, None, None], pad_freq(back_up, s, False), 0.0)
+        src_down = pad_freq(down_freq, s, True)
+        hit_down = (src_down == freq_ids) & (freq_ids + s < n_freq)
+        to_down = to_down + jnp.where(hit_down[:, None, None], pad_freq(back_down, s, True), 0.0)
+    source = to_up + to_down - 2.0 * quartet
+    return (shifted + dia_coeff * source).reshape(shape)
 
 
 def shards(spectrum, depth_speed, turning, drift, partners, sea_slots, sea_counts):
@@ -130,17 +176,7 @@
     turned = advect_direction(spaced.reshape(local_freq, ND, grid_rows, grid_cols), turning)
     turned = turned.reshape(channels, grid_rows, grid_cols)
     points = lax.all_to_all(turned, "spec", split_axis=1, concat_axis=0, tiled=True)
-    n_comps, point_rows, item_count = points.shape
-    flattened = points.reshape(n_comps, point_rows * item_count)
-    shifted = advect_frequency(flattened, drift, NF, ND)
-    plus_values = pick_rows(partners[0], shifted)
-    minus_values = pick_rows(partners[1], shifted)
-    quartet = (
-        shifted * shifted * (plus_values + minus_values)
-        - 2.0 * shifted * plus_values * minus_values
-    )
-    source = spread_rows(partners[0], quartet) + spread_rows(partners[1], quartet) - 2.0 * quartet
-    return (shifted + dia_coeff * source).reshape(n_comps, point_rows, item_count)
+    return settle(points, drift, partners)
 
 
 def solution(mesh):

time: 111 us -> 80.8 us (0.73)
  the two profiles are of different devices: /device:TPU:201 before, /device:TPU:193 now
where the time goes in v1:
time: 80.8 us; the launch traced here: 80.3 us
  waiting for transfers between devices  34.2 us (42%)
  local copies, waits for them, and re-layouts  16 us (20%)
  other arithmetic  15.7 us (19%)
  starting transfers between devices  13.9 us (17%)
    all_to_all x1, waiting for transfers between devices, shards(): lax.all_to_all(turned, 'spec', split_axis=1, concat_axis=0, tiled=True)  30.4 us
    all_to_all x1, starting transfers between devices, shards(): lax.all_to_all(turned, 'spec', split_axis=1, concat_axis=0, tiled=True)  9.98 us
    ppermute x1, starting transfers between devices, extended(): lax.ppermute(tail, axis, [(i, (i + 1) % count) for i in range(count)])  3.88 us
    ppermute x1, waiting for transfers between devices, extended(): lax.ppermute(head, axis, [((i + 1) % count, i) for i in range(count)])  3.53 us
    reduce_or x1, other arithmetic, sea_cells(): return jnp.any(matches, axis=1).astype(jnp.float32)  2.32 us
    unnamed x16, local copies, waits for them, and re-layouts  2.18 us
    add x1, local copies, waits for them, and re-layouts, advect_direction(): energy - jnp.abs(turning) * energy + turn_plus * jnp.roll(energy, 1, axis=1)  1.76 us
    slice x1, local copies, waits for them, and re-layouts, extended(): lax.slice_in_dim(cells, cells.shape[dim] - width, cells.shape[dim], axis=...  1.73 us
  transfers between devices with their start and end apart: 3, of which 3 were waited for; matrix products, arithmetic and copies ran while one was open for 3% of the time, Pallas kernels for 0%

profile of v1, /device:TPU:193, one launch (start us, length us, event | category | flops | bytes accessed | tf_op | source)
XLA Modules:
  0.0 80.3 jit_solution(14151663270430954927)
XLA Ops:
  0.0 0.8 copy.75
  0.8 0.7 iota_compare_fusion.1
  1.5 2.3 %fusion.1 = pred[32,256]{1,0:T(8,128)(4,1)S(1)} fusion(s32[32,192]{1,0:T(8,128)S(1)} %bitcast.71, pred[32,192]{1,0:T(8,128)(4,1)S(1)} %iota_compare_fusion.1), kind=kLoop, calls=%fused_computation.2 | loop fusion | flops 4710400 | bytes 38912 | tf_op jit(solution)/shard_map/reduce_or | solution.py:36
  3.9 1.4 %broadcast_multiply_fusion.2 = f32[36,64,128]{2,1,0:T(8,128)S(1)} fusion(f32[36,64,128]{2,1,0:T(8,128)} %param.7, f32[64,128]{1,0:T(8,128)S(1)} %reshape.342), kind=kLoop, calls=%fused_computation.58 | loop fusion | flops 294912 | bytes 2392064 | tf_op jit(solution)/shard_map/mul | solution.py:164
  5.2 1.5 %slice_maximum_fusion = (f32[37,64,1]{2,1,0:T(8,128)}, f32[37,64,1]{2,1,0:T(8,128)S(1)}) fusion(f32[1,64,128]{2,1,0:T(8,128)S(1)} %bitcast.68, f32[36,64,128]{2,1,0:T(8,128)S(1)} %broadcast_multiply_fusion.2), kind=kLoop, calls=%fused_computation.7 | loop fusion | flops 4736 | bytes 1231360 | tf_op jit(solution)/shard_map/concatenate | solution.py:165
  6.7 1.7 %copy.49 = f32[37,64,1]{1,0,2:T(8,128)S(1)} copy(f32[37,64,1]{2,1,0:T(8,128)} %get-tuple-element.17) | data formatting | bytes 18944 | tf_op jit(solution)/shard_map/slice | solution.py:19
  8.4 3.9 %collective-permute-start = (f32[37,64,1]{1,0,2:T(8,128)S(1)}, f32[37,64,1]{1,0,2:T(8,128)S(1)}, u32[]{:S(2)}, u32[]{:S(2)}) collective-permute-start(f32[37,64,1]{1,0,2:T(8,128)S(1)} %copy.49), channel_id=1, source_target_pairs={{0,1},{1,2},{2,3},{3,4},{4,5},{5,6},{6,7},{7,8},{8,9},{9,10},{10,1... | collective-permute-start | bytes 28424 | tf_op jit(solution)/shard_map/ppermute | solution.py:22
  12.3 0.4 copy.50
  13.0 0.3 collective-permute-done
  13.2 0.4 copy.51
  13.7 3.5 %collective-permute-done.1 = f32[37,64,1]{1,0,2:T(8,128)S(1)} collective-permute-done((f32[37,64,1]{1,0,2:T(8,128)S(1)}, f32[37,64,1]{1,0,2:T(8,128)S(1)}, u32[]{:S(2)}, u32[]{:S(2)}) %collective-permute-start.1) | collective-permute-done | bytes 9504 | tf_op jit(solution)/shard_map/ppermute | solution.py:24
  17.2 1.5 %copy.52 = f32[37,64,1]{2,1,0:T(8,128)} copy(f32[37,64,1]{1,0,2:T(8,128)S(1)} %collective-permute-done.1) | data formatting | bytes 18944 | tf_op jit(solution)/shard_map/ppermute | solution.py:24
  18.7 0.8 %fusion.16 = f32[64,130]{1,0:T(8,128)S(1)} fusion(f32[37,64,1]{2,1,0:T(8,128)} %copy.52, f32[37,64,1]{2,1,0:T(8,128)S(1)} %copy.51, f32[1,64,128]{2,1,0:T(8,128)S(1)} %bitcast.69, f32[36,64,128]{2,1,0:T(8,128)S(1)} %broadcast_multiply_fusion.2), kind=kLoop, calls=%fused_computation.60 | loop fusion | flops 24960 | bytes 1264640 | tf_op jit(solution)/shard_map/mul | solution.py:40
  19.6 0.1 broadcast_multiply_fusion.1
  19.8 0.6 slice_multiply_fusion.3
  20.4 0.2 broadcast_multiply_fusion
  20.6 1.0 %copy-done = f32[37,64,1]{2,1,0:T(8,128)S(1)} copy-done((f32[37,64,1]{2,1,0:T(8,128)S(1)}, f32[37,64,1]{2,1,0:T(8,128)}, u32[]{:S(2)}) %copy-start) | copy-done | bytes 9496
  21.7 1.6 %fusion.5 = f32[36,64,128]{2,1,0:T(8,128)S(1)} fusion(f32[36,64,128]{2,1,0:T(8,128)S(1)} %broadcast_multiply_fusion.2, f32[37,64,1]{2,1,0:T(8,128)S(1)} %copy-done, f32[1,64,128]{2,1,0:T(8,128)S(1)} %bitcast.70, f32[36,64,130]{2,1,0:T(8,128)S(1)} %broadcast_multiply_fusion, f32[37,64,1]{2,1,0:T(8,128)S(1)} %copy.51, ...), kind=kLoop, calls=%fused_computation.11 | loop fusion | flops 5898240 | bytes 8338064 | tf_op jit(solution)/shard_map/mul | solution.py:62
  23.3 0.3 slice_bitcast_fusion
  23.7 0.4 fusion.7
  24.1 1.8 %copy.55 = f32[36,64,128]{2,0,1:T(8,128)} copy(f32[36,64,128]{2,1,0:T(8,128)S(1)} %fusion.7) | data formatting | bytes 2359296 | tf_op jit(solution)/shard_map/add | solution.py:69
  25.8 10.0 %all-to-all-start = ((f32[36,64,128]{2,0,1:T(8,128)}), f32[36,64,128]{2,0,1:T(8,128)S(1)}, u32[]{:S(2)}, u32[]{:S(2)}) async-start(f32[36,64,128]{2,0,1:T(8,128)} %copy.55), calls=%async_computation | async-start | bytes 2621440 | tf_op jit(solution)/shard_map/all_to_all | solution.py:178
  35.9 0.1 reshape_squeeze.7
  36.3 0.1 max.49
  36.5 0.1 max.47
  36.7 0.1 abs.24
  36.9 0.1 reshape_squeeze.6
  37.3 30.4 %all-to-all-done = f32[36,64,128]{2,0,1:T(8,128)S(1)} async-done(((f32[36,64,128]{2,0,1:T(8,128)}), f32[36,64,128]{2,0,1:T(8,128)S(1)}, u32[]{:S(2)}, u32[]{:S(2)}) %all-to-all-start) | async-done | bytes 1179680 | tf_op jit(solution)/shard_map/all_to_all | solution.py:178
  67.7 0.6 copy.74
  68.3 0.9 %reshape.336 = f32[32,36,256]{2,0,1:T(8,128)S(1)} reshape(f32[32,36,2,128]{3,2,0,1:T(2,128)S(1)} %bitcast.67) | data formatting | bytes 2359296 | tf_op jit(solution)/shard_map/reshape | solution.py:116
  69.2 0.4 slice_multiply_fusion.1
  69.6 0.4 fusion.9
  70.0 0.3 fusion.29
  70.3 0.3 fusion.30
  70.6 0.3 fusion.31
  71.1 1.4 %maximum_select_fusion = (f32[32,36,256]{2,0,1:T(8,128)S(1)}, f32[32,36,256]{2,0,1:T(8,128)S(1)}) fusion(f32[3,36,256]{2,0,1:T(4,128)S(1)} %reshape.337, f32[29,36,256]{2,0,1:T(8,128)S(1)} %get-tuple-element.37, f32[2,36,256]{2,0,1:T(2,128)S(1)} %reshape.338, f32[30,36,256]{2,0,1:T(8,128)S(1)} %get-tuple-element.35, f32[32,36,256]{2,0,1:T(8,128)S(1)} %fusion.9, ...), kind=kLoop, calls=%fused_computation.37 | loop fusion | flops 3538944 | bytes 10617024 | tf_op jit(solution)/shard_map/jit(_where)/select_n | solution.py:131
  73.0 1.0 %multiply_subtract_fusion.3 = f32[32,36,256]{2,0,1:T(8,128)S(1)} fusion(f32[32,36,256]{2,0,1:T(8,128)S(1)} %fusion.9, f32[32,33,256]{2,0,1:T(8,128)S(1)} %slice.333, f32[32,3,256]{2,0,1:T(8,128)S(1)} %slice.332, f32[32,34,256]{2,0,1:T(8,128)S(1)} %slice.331, f32[32,2,256]{2,0,1:T(8,128)S(1)} %slice.330, f32[32,35,256]{2,0,1:T(8,128)S(1)} %slice.329, ...), kind=kLoop, calls=%fused_computation.53 | loop fusion | flops 5013504 | bytes 9437312 | tf_op jit(solution)/shard_map/sub | solution.py:139
  74.1 0.3 fusion.28
  74.4 0.3 fusion.26
  74.7 0.3 fusion.24
  75.0 0.4 maximum_select_fusion.12
  75.5 0.1 slice.349
  75.6 0.1 slice.350
  75.8 0.1 slice.351
  75.9 0.4 maximum_select_fusion.10
  76.4 1.6 %multiply_add_fusion = f32[32,36,256]{2,0,1:T(8,128)S(1)} fusion(f32[32,36,256]{2,0,1:T(8,128)S(1)} %fusion.9, f32[32,36,256]{2,0,1:T(8,128)S(1)} %multiply_subtract_fusion.3, f32[29,36,256]{2,0,1:T(8,128)S(1)} %slice.351, f32[30,36,256]{2,0,1:T(8,128)S(1)} %slice.350, f32[31,36,256]{2,0,1:T(8,128)S(1)} %slice.349, ...), kind=kLoop, calls=%fused_computation.52 | loop fusion | flops 5603328 | bytes 12534016 | tf_op jit(solution)/shard_map/add | solution.py:154
  78.0 0.7 copy.62
  78.7 1.6 %reshape.341 = f32[1152,2,128]{2,1,0:T(2,128)} reshape(f32[32,36,256]{2,1,0:T(8,128)S(1)} %copy.62) | data formatting | bytes 2359296 | tf_op jit(solution)/shard_map/reshape | solution.py:154
  (56 shorter events, 1.8 us)
Async XLA Ops:
  3.8 1.4 %copy-start.1 = (f32[64,128]{1,0:T(8,128)S(1)}, f32[64,128]{1,0:T(8,128)}, u32[]{:S(2)}) copy-start(f32[64,128]{1,0:T(8,128)} %param.8) | copy-start | bytes 98308
  6.7 6.2 %copy-start.2 = (f32[64,128]{1,0:T(8,128)S(1)}, f32[64,128]{1,0:T(8,128)}, u32[]{:S(2)}) copy-start(f32[64,128]{1,0:T(8,128)} %param.9) | copy-start | bytes 98308
  8.4 4.8 %collective-permute-start = (f32[37,64,1]{1,0,2:T(8,128)S(1)}, f32[37,64,1]{1,0,2:T(8,128)S(1)}, u32[]{:S(2)}, u32[]{:S(2)}) collective-permute-start(f32[37,64,1]{1,0,2:T(8,128)S(1)} %copy.49), channel_id=1, source_target_pairs={{0,1},{1,2},{2,3},{3,4},{4,5},{5,6},{6,7},{7,8},{8,9},{9,10},{10,1... | collective-permute-start | bytes 28424 | tf_op jit(solution)/shard_map/ppermute | solution.py:22
  12.8 4.4 %collective-permute-start.1 = (f32[37,64,1]{1,0,2:T(8,128)S(1)}, f32[37,64,1]{1,0,2:T(8,128)S(1)}, u32[]{:S(2)}, u32[]{:S(2)}) collective-permute-start(f32[37,64,1]{1,0,2:T(8,128)S(1)} %copy.50), channel_id=1, source_target_pairs={{1,0},{2,1},{3,2},{4,3},{5,4},{6,5},{7,6},{8,7},{9,8},{10,9},{11,1... | collective-permute-start | bytes 28424 | tf_op jit(solution)/shard_map/ppermute | solution.py:24
  20.4 1.3 %copy-start = (f32[37,64,1]{2,1,0:T(8,128)S(1)}, f32[37,64,1]{2,1,0:T(8,128)}, u32[]{:S(2)}) copy-start(f32[37,64,1]{2,1,0:T(8,128)} %copy.52) | copy-start | bytes 28420
  25.8 10.0 %copy-start.3 = (s32[2,1152]{1,0:T(2,128)S(1)}, s32[2,1152]{1,0:T(2,128)}, u32[]{:S(2)}) copy-start(s32[2,1152]{1,0:T(2,128)} %param.11) | copy-start | bytes 27652
  25.8 10.5 %copy-start.4 = (f32[1152]{0:T(1024)S(1)}, f32[1152]{0:T(1024)}, u32[]{:S(2)}) copy-start(f32[1152]{0:T(1024)} %param.10) | copy-start | bytes 13828
  25.8 41.9 %all-to-all-start = ((f32[36,64,128]{2,0,1:T(8,128)}), f32[36,64,128]{2,0,1:T(8,128)S(1)}, u32[]{:S(2)}, u32[]{:S(2)}) async-start(f32[36,64,128]{2,0,1:T(8,128)} %copy.55), calls=%async_computation | async-start | bytes 2621440 | tf_op jit(solution)/shard_map/all_to_all | solution.py:178

commit v2 on v1

--- a/solution.py
+++ b/solution.py
@@ -154,6 +154,46 @@
     return (shifted + dia_coeff * source).reshape(shape)
 
 
+def neighbours(edges_first, edges_last):
+    count = lax.axis_size("tile")
+    from_west = lax.ppermute(edges_last, "tile", [(i, (i + 1) % count) for i in range(count)])
+    from_east = lax.ppermute(edges_first, "tile", [((i + 1) % count, i) for i in range(count)])
+    return from_west, from_east
+
+
+def propagate(energy, depth, sea_mask, turning, from_west, from_east, speeds, cosines, sine_part):
+    channels, grid_rows, grid_cols = energy.shape
+    col = lax.broadcasted_iota(jnp.int32, (grid_rows, grid_cols), 1)
+    row = lax.broadcasted_iota(jnp.int32, (grid_rows, grid_cols), 0)
+    first_col = col == 0
+    last_col = col == grid_cols - 1
+    west_energy = jnp.where(first_col, from_west[:channels, :, None], jnp.roll(energy, 1, axis=2))
+    east_energy = jnp.where(last_col, from_east[:channels, :, None], jnp.roll(energy, -1, axis=2))
+    west_depth = jnp.where(first_col, from_west[channels][:, None], jnp.roll(depth, 1, axis=1))
+    east_depth = jnp.where(last_col, from_east[channels][:, None], jnp.roll(depth, -1, axis=1))
+    east_coef = (speeds * cosines)[:, None, None]
+    north_coef = (speeds * sine_part)[:, None, None]
+    east_mid = east_coef * depth[None]
+    north_rate = north_coef * depth[None]
+    inflow = (
+        jnp.maximum(east_coef * west_depth[None], 0.0) * west_energy
+        + jnp.maximum(-(east_coef * east_depth[None]), 0.0) * east_energy
+    )
+    south_flux = jnp.maximum(north_rate, 0.0) * energy
+    north_flux = jnp.maximum(-north_rate, 0.0) * energy
+    from_south = jnp.where(row == 0, 0.0, jnp.roll(south_flux, 1, axis=1))
+    from_north = jnp.where(row == grid_rows - 1, 0.0, jnp.roll(north_flux, -1, axis=1))
+    updated = (
+        energy
+        - (jnp.abs(east_mid) + jnp.abs(north_rate)) * energy
+        + inflow
+        + from_south
+        + from_north
+    )
+    spaced = updated * sea_mask
+    return advect_direction(spaced[None], turning)[0]
+
+
 def shards(spectrum, depth_speed, turning, drift, partners, sea_slots, sea_counts):
     channels, grid_rows, grid_cols = spectrum.shape
     n_spec = lax.axis_size("spec")
@@ -162,8 +202,9 @@
     sea_list = sea_slots[:, 0, :]
     sea_mask = sea_cells(sea_list, sea_counts[:, 0], per_block).reshape(grid_rows, grid_cols)
     energy = spectrum * sea_mask
-    stacked = jnp.concatenate([energy, depth_speed[None]], axis=0)
-    padded = extended(stacked, (("tile", 2),), 1)
+    edges_first = jnp.concatenate([energy[:, :, 0], depth_speed[None, :, 0]], axis=0)
+    edges_last = jnp.concatenate([energy[:, :, -1], depth_speed[None, :, -1]], axis=0)
+    from_west, from_east = neighbours(edges_first, edges_last)
     local_freq = channels // ND
     freq_ids = (
         lax.axis_index("spec") * local_freq + jnp.arange(local_freq, dtype=jnp.int32)
@@ -172,9 +213,9 @@
     angles = 2.0 * jnp.pi * jnp.arange(ND, dtype=jnp.float32) / ND
     cosines = jnp.tile(jnp.cos(angles), local_freq)
     sine_part = jnp.tile(jnp.sin(angles), local_freq)
-    spaced = advect_space(padded[:channels], padded[channels], speeds, cosines, sine_part, sea_mask)
-    turned = advect_direction(spaced.reshape(local_freq, ND, grid_rows, grid_cols), turning)
-    turned = turned.reshape(channels, grid_rows, grid_cols)
+    turned = propagate(
+        energy, depth_speed, sea_mask, turning, from_west, from_east, speeds, cosines, sine_part
+    )
     points = lax.all_to_all(turned, "spec", split_axis=1, concat_axis=0, tiled=True)
     return settle(points, drift, partners)
 

time: 80.8 us -> 92.8 us (1.15)
  local copies, waits for them, and re-layouts: 16 us -> 24.2 us
  other arithmetic: 15.7 us -> 21.7 us
  waiting for transfers between devices: 34.2 us -> 31.9 us
    slice x3 -> x5, local copies, waits for them, and re-layouts: 2.25 us -> 8.69 us  [the longest x1 2.96 us: propagate(): jnp.roll(energy, -1, axis=2)]
    mul x8 -> x5, other arithmetic: 4.87 us -> 11 us  [the longest x1 8.28 us: propagate(): spaced = updated * sea_mask]
    ppermute x2, waiting for transfers between devices: 3.8 us -> 0.01 us  [the longest x1 0.01 us: neighbours(): lax.ppermute(edges_last, 'tile', [(i, (i + 1) % count) for i in range(cou...]
    unnamed x16 -> x21, local copies, waits for them, and re-layouts: 2.18 us -> 5.39 us
    ppermute x2 -> x0, local copies, waits for them, and re-layouts: 1.94 us -> none  [the longest x1 1.5 us: extended(): lax.ppermute(head, axis, [((i + 1) % count, i) for i in range(count)])]
    all_to_all x1, waiting for transfers between devices: 30.4 us -> 31.9 us  [shards(): lax.all_to_all(turned, 'spec', split_axis=1, concat_axis=0, tiled=True)]
    concatenate x1 -> x2, other arithmetic: 1.49 us -> 0.02 us  [the longest x1 0.01 us: shards(): jnp.concatenate([energy[:, :, -1], depth_speed[None, :, -1]], axis=0)]
    add x1, other arithmetic: 0.39 us -> 1.48 us  [advect_direction(): energy - jnp.abs(turning) * energy + turn_plus * jnp.roll(energy, 1, axis=1)]
  transfers between devices with their start and end apart: 3 -> 3, of which waited for: 3 -> 1; matrix products, arithmetic and copies ran while one was open for 3% -> 11% of each run, Pallas kernels for 0% -> 0%
where the time goes in v2:
time: 92.8 us; the launch traced here: 92.3 us
  waiting for transfers between devices  31.9 us (34%)
  local copies, waits for them, and re-layouts  24.2 us (26%)
  other arithmetic  21.7 us (23%)
  starting transfers between devices  13.9 us (15%)
    all_to_all x1, waiting for transfers between devices, shards(): lax.all_to_all(turned, 'spec', split_axis=1, concat_axis=0, tiled=True)  31.9 us
    all_to_all x1, starting transfers between devices, shards(): lax.all_to_all(turned, 'spec', split_axis=1, concat_axis=0, tiled=True)  9.98 us
    mul x1, other arithmetic, propagate(): spaced = updated * sea_mask  8.28 us
    unnamed x21, local copies, waits for them, and re-layouts  5.39 us
    ppermute x1, starting transfers between devices, neighbours(): lax.ppermute(edges_last, 'tile', [(i, (i + 1) % count) for i in range(cou...  3.88 us
    slice x1, local copies, waits for them, and re-layouts, propagate(): jnp.roll(energy, -1, axis=2)  2.96 us
    slice x1, local copies, waits for them, and re-layouts, propagate(): jnp.roll(north_flux, -1, axis=1)  2.33 us
    reduce_or x1, other arithmetic, sea_cells(): return jnp.any(matches, axis=1).astype(jnp.float32)  2.32 us
  transfers between devices with their start and end apart: 3, of which 1 were waited for; matrix products, arithmetic and copies ran while one was open for 11% of the time, Pallas kernels for 0%

profile of v2, /device:TPU:193, one launch (start us, length us, event | category | flops | bytes accessed | tf_op | source)
XLA Modules:
  0.0 92.3 jit_solution(9500344232677622728)
XLA Ops:
  0.0 0.8 copy.77
  0.9 1.0 %slice_reduce_fusion.3 = (f32[64]{0:T(128)S(1)}, f32[64]{0:T(128)S(1)}, f32[64,1]{1,0:T(8,128)S(1)}, f32[64,1]{1,0:T(8,128)S(1)}) fusion(f32[64,128]{1,0:T(8,128)} %param.8), kind=kLoop, calls=%fused_computation.106 | loop fusion | bytes 1536 | tf_op jit(solution)/shard_map/slice | solution.py:206
  2.0 0.8 copy.106
  2.7 0.7 iota_compare_fusion.1
  3.5 2.3 %fusion.1 = pred[32,256]{1,0:T(8,128)(4,1)S(1)} fusion(s32[32,192]{1,0:T(8,128)S(1)} %bitcast.89, pred[32,192]{1,0:T(8,128)(4,1)S(1)} %iota_compare_fusion.1), kind=kLoop, calls=%fused_computation.2 | loop fusion | flops 4710400 | bytes 38912 | tf_op jit(solution)/shard_map/reduce_or | solution.py:36
  5.9 3.2 %copy.76 = f32[36,64,128]{1,0,2:T(8,128)} copy(f32[36,64,128]{2,1,0:T(8,128)} %param.7) | data formatting | bytes 2359296 | tf_op args[0]
  9.2 2.3 %fusion.11 = (f32[36,64,128]{1,0,2:T(8,128)S(1)}, f32[36,64,128]{1,0,2:T(8,128)S(1)}) fusion(f32[36]{0:T(128)S(1)} %sine_multiply_fusion, f32[64,128]{0,1:T(8,128)S(1)} %copy.77, f32[36,64,128]{1,0,2:T(8,128)} %copy.76, f32[64,128]{0,1:T(8,128)S(1)} %copy.75), kind=kLoop, calls=%fused_computation.17 | loop fusion | flops 1474560 | bytes 3604624 | tf_op jit(solution)/shard_map/mul | solution.py:183
  11.5 3.9 %collective-permute-start = (f32[37,64]{1,0:T(8,128)S(1)}, f32[37,64]{1,0:T(8,128)S(1)}, u32[]{:S(2)}, u32[]{:S(2)}) collective-permute-start(f32[37,64]{1,0:T(8,128)S(1)} %pad_maximum_fusion), channel_id=1, source_target_pairs={{0,1},{1,2},{2,3},{3,4},{4,5},{5,6},{6,7},{7,8},{8,9},{9,10},{10,1... | collective-permute-start | bytes 28424 | tf_op jit(solution)/shard_map/ppermute | solution.py:159
  15.5 0.4 fusion.9
  15.9 3.0 %fusion.23 = (f32[36,64,127]{1,0,2:T(8,128)}, f32[36,64,127]{1,0,2:T(8,128)}) fusion(f32[36,64,128]{1,0,2:T(8,128)S(1)} %get-tuple-element.18), kind=kLoop, calls=%fused_computation.107 | loop fusion | bytes 4681728 | tf_op jit(solution)/shard_map/jit(_roll_static)/slice | solution.py:171
  18.9 0.2 copy-done.1
  19.1 2.3 %slice.330 = f32[36,1,128]{1,0,2:T(8,128)} slice(f32[36,64,128]{1,0,2:T(8,128)S(1)} %fusion.9), slice={[0:36], [63:64], [0:128]} | slice | bytes 36864 | tf_op jit(solution)/shard_map/jit(_roll_static)/slice | solution.py:184
  21.4 2.3 %slice.332 = f32[36,63,128]{1,0,2:T(8,128)} slice(f32[36,64,128]{1,0,2:T(8,128)S(1)} %get-tuple-element.17), slice={[0:36], [1:64], [0:128]} | slice | bytes 2322432 | tf_op jit(solution)/shard_map/jit(_roll_static)/slice | solution.py:185
  23.8 0.1 copy.81
  23.9 0.1 copy.83
  24.4 8.3 %fusion.5 = f32[36,64,128]{1,0,2:T(8,128)S(1)} fusion(f32[36,64,128]{1,0,2:T(8,128)S(1)} %get-tuple-element.18, f32[36,64,127]{1,0,2:T(8,128)} %get-tuple-element.28, f32[36,64,1]{1,0,2:T(8,128)S(1)} %get-tuple-element.26, f32[36,64,1]{1,0,2:T(8,128)S(1)} %get-tuple-element.25, f32[36,64,127]{1,0,2:T(8,128)} %get-tuple-element.27, ...), kind=kLoop, calls=%fused_computation.11 | loop fusion | flops 7962624 | bytes 7228064 | tf_op jit(solution)/shard_map/mul | solution.py:193
  32.7 0.4 slice_bitcast_fusion
  33.2 1.5 %fusion.7 = f32[36,64,128]{1,0,2:T(8,128)S(1)} fusion(f32[36,64,128]{1,0,2:T(8,128)S(1)} %fusion.5, f32[35,64,128]{1,0,2:T(8,128)S(1)} %get-tuple-element.20, f32[1,64,128]{1,0,2:T(1,128)S(1)} %get-tuple-element.22, f32[1,64,128]{1,0,2:T(1,128)S(1)} %get-tuple-element.21, f32[35,64,128]{1,0,2:T(8,128)S(1)} %get-tuple-element.19, f32[64,128]{0,1:T(8,128)S(1)} %copy.83, ...), kind=kLoop, calls=%fused_computation.13 | loop fusion | flops 2359296 | bytes 4816896 | tf_op jit(solution)/shard_map/add | solution.py:69
  34.7 2.0 %copy.85 = f32[36,64,128]{2,0,1:T(8,128)} copy(f32[36,64,128]{1,0,2:T(8,128)S(1)} %fusion.7) | data formatting | bytes 2359296 | tf_op jit(solution)/shard_map/add | solution.py:69
  36.7 10.0 %all-to-all-start = ((f32[36,64,128]{2,0,1:T(8,128)}), f32[36,64,128]{2,0,1:T(8,128)S(1)}, u32[]{:S(2)}, u32[]{:S(2)}) async-start(f32[36,64,128]{2,0,1:T(8,128)} %copy.85), calls=%async_computation | async-start | bytes 2621440 | tf_op jit(solution)/shard_map/all_to_all | solution.py:219
  46.7 0.1 reshape_squeeze.7
  47.2 0.1 max.49
  47.3 0.1 copy.102
  47.4 0.1 max.47
  47.5 0.1 copy.103
  47.6 0.1 abs.24
  47.8 0.1 reshape_squeeze.6
  48.2 31.9 %all-to-all-done = f32[36,64,128]{2,0,1:T(8,128)S(1)} async-done(((f32[36,64,128]{2,0,1:T(8,128)}), f32[36,64,128]{2,0,1:T(8,128)S(1)}, u32[]{:S(2)}, u32[]{:S(2)}) %all-to-all-start) | async-done | bytes 1179680 | tf_op jit(solution)/shard_map/all_to_all | solution.py:219
  80.0 0.2 copy.86
  80.3 0.9 %reshape.415 = f32[32,36,256]{2,0,1:T(8,128)S(1)} reshape(f32[32,36,2,128]{3,2,0,1:T(2,128)S(1)} %bitcast.84) | data formatting | bytes 2359296 | tf_op jit(solution)/shard_map/reshape | solution.py:116
  81.2 0.4 slice_multiply_fusion.1
  81.6 0.4 fusion.16
  82.0 0.3 fusion.30
  82.3 0.3 fusion.31
  82.5 0.3 fusion.32
  83.0 1.4 %maximum_select_fusion.4 = (f32[32,36,256]{2,0,1:T(8,128)S(1)}, f32[32,36,256]{2,0,1:T(8,128)S(1)}) fusion(f32[3,36,256]{2,0,1:T(4,128)S(1)} %reshape.416, f32[29,36,256]{2,0,1:T(8,128)S(1)} %get-tuple-element.47, f32[2,36,256]{2,0,1:T(2,128)S(1)} %reshape.417, f32[30,36,256]{2,0,1:T(8,128)S(1)} %get-tuple-element.45, f32[32,36,256]{2,0,1:T(8,128)S(1)} %fusion.16, ...), kind=kLoop, calls=%fused_computation.35 | loop fusion | flops 3538944 | bytes 10617024 | tf_op jit(solution)/shard_map/jit(_where)/select_n | solution.py:131
  85.0 1.0 %multiply_subtract_fusion.3 = f32[32,36,256]{2,0,1:T(8,128)S(1)} fusion(f32[32,36,256]{2,0,1:T(8,128)S(1)} %fusion.16, f32[32,33,256]{2,0,1:T(8,128)S(1)} %slice.363, f32[32,3,256]{2,0,1:T(8,128)S(1)} %slice.362, f32[32,34,256]{2,0,1:T(8,128)S(1)} %slice.361, f32[32,2,256]{2,0,1:T(8,128)S(1)} %slice.360, f32[32,35,256]{2,0,1:T(8,128)S(1)} %slice.359, ...), kind=kLoop, calls=%fused_computation.50 | loop fusion | flops 5013504 | bytes 9437312 | tf_op jit(solution)/shard_map/sub | solution.py:139
  86.1 0.3 fusion.29
  86.4 0.3 fusion.27
  86.7 0.3 fusion.25
  87.0 0.4 maximum_select_fusion.16
  87.4 0.1 slice.379
  87.6 0.1 slice.380
  87.7 0.1 slice.381
  87.9 0.4 maximum_select_fusion.14
  88.3 1.6 %multiply_add_fusion = f32[32,36,256]{2,0,1:T(8,128)S(1)} fusion(f32[32,36,256]{2,0,1:T(8,128)S(1)} %fusion.16, f32[32,36,256]{2,0,1:T(8,128)S(1)} %multiply_subtract_fusion.3, f32[29,36,256]{2,0,1:T(8,128)S(1)} %slice.381, f32[30,36,256]{2,0,1:T(8,128)S(1)} %slice.380, f32[31,36,256]{2,0,1:T(8,128)S(1)} %slice.379, ...), kind=kLoop, calls=%fused_computation.49 | loop fusion | flops 5603328 | bytes 12534016 | tf_op jit(solution)/shard_map/add | solution.py:154
  90.0 0.7 copy.92
  90.7 1.6 %reshape.420 = f32[1152,2,128]{2,1,0:T(2,128)} reshape(f32[32,36,256]{2,1,0:T(8,128)S(1)} %copy.92) | data formatting | bytes 2359296 | tf_op jit(solution)/shard_map/reshape | solution.py:154
  (72 shorter events, 2.3 us)
Async XLA Ops:
  9.2 6.3 %copy-start.2 = (f32[64,128]{1,0:T(8,128)S(1)}, f32[64,128]{1,0:T(8,128)}, u32[]{:S(2)}) copy-start(f32[64,128]{1,0:T(8,128)} %param.8) | copy-start | bytes 98308
  11.5 9.9 %copy-start = (f32[36,64,128]{1,0,2:T(8,128)}, f32[36,64,128]{1,0,2:T(8,128)S(1)}, u32[]{:S(2)}) copy-start(f32[36,64,128]{1,0,2:T(8,128)S(1)} %get-tuple-element.17) | copy-start | bytes 3538948
  11.5 12.5 %collective-permute-start = (f32[37,64]{1,0:T(8,128)S(1)}, f32[37,64]{1,0:T(8,128)S(1)}, u32[]{:S(2)}, u32[]{:S(2)}) collective-permute-start(f32[37,64]{1,0:T(8,128)S(1)} %pad_maximum_fusion), channel_id=1, source_target_pairs={{0,1},{1,2},{2,3},{3,4},{4,5},{5,6},{6,7},{7,8},{8,9},{9,10},{10,1... | collective-permute-start | bytes 28424 | tf_op jit(solution)/shard_map/ppermute | solution.py:159
  15.4 8.9 %collective-permute-start.1 = (f32[37,64]{1,0:T(8,128)S(1)}, f32[37,64]{1,0:T(8,128)S(1)}, u32[]{:S(2)}, u32[]{:S(2)}) collective-permute-start(f32[37,64]{1,0:T(8,128)S(1)} %pad_maximum_fusion.1), channel_id=1, source_target_pairs={{1,0},{2,1},{3,2},{4,3},{5,4},{6,5},{7,6},{8,7},{9,8},{10,9},{11,1... | collective-permute-start | bytes 28424 | tf_op jit(solution)/shard_map/ppermute | solution.py:160
  15.9 3.2 %copy-start.1 = (f32[36,64,128]{1,0,2:T(8,128)}, f32[36,64,128]{1,0,2:T(8,128)S(1)}, u32[]{:S(2)}) copy-start(f32[36,64,128]{1,0,2:T(8,128)S(1)} %fusion.9) | copy-start | bytes 3538948
  15.9 3.0 %copy-start.3 = (f32[64,128]{1,0:T(8,128)S(1)}, f32[64,128]{1,0:T(8,128)}, u32[]{:S(2)}) copy-start(f32[64,128]{1,0:T(8,128)} %param.9) | copy-start | bytes 98308
  36.7 10.0 %copy-start.4 = (s32[2,1152]{1,0:T(2,128)S(1)}, s32[2,1152]{1,0:T(2,128)}, u32[]{:S(2)}) copy-start(s32[2,1152]{1,0:T(2,128)} %param.11) | copy-start | bytes 27652
  36.7 10.5 %copy-start.5 = (f32[1152]{0:T(1024)S(1)}, f32[1152]{0:T(1024)}, u32[]{:S(2)}) copy-start(f32[1152]{0:T(1024)} %param.10) | copy-start | bytes 13828
  36.7 43.3 %all-to-all-start = ((f32[36,64,128]{2,0,1:T(8,128)}), f32[36,64,128]{2,0,1:T(8,128)S(1)}, u32[]{:S(2)}, u32[]{:S(2)}) async-start(f32[36,64,128]{2,0,1:T(8,128)} %copy.85), calls=%async_computation | async-start | bytes 2621440 | tf_op jit(solution)/shard_map/all_to_all | solution.py:219

commit v3 on v1

--- a/solution.py
+++ b/solution.py
@@ -2,6 +2,8 @@
 import jax.numpy as jnp
 from jax import lax
 from jax.sharding import PartitionSpec as P
+from jax.experimental import pallas as pl
+from jax.experimental.pallas import tpu as pltpu
 
 ND = 36
 NF = 32
@@ -154,6 +156,76 @@
     return (shifted + dia_coeff * source).reshape(shape)
 
 
+def neighbours(edges_first, edges_last):
+    count = lax.axis_size("tile")
+    from_west = lax.ppermute(edges_last, "tile", [(i, (i + 1) % count) for i in range(count)])
+    from_east = lax.ppermute(edges_first, "tile", [((i + 1) % count, i) for i in range(count)])
+    return from_west, from_east
+
+
+def propagate_kernel(coef_ref, spec_ref, mask_ref, depth_ref, turn_ref, west_ref, east_ref, out_ref, spaced_ref):
+    channels, grid_rows, grid_cols = spec_ref.shape
+    mask = mask_ref[...]
+    depth = depth_ref[...]
+    west = west_ref[...]
+    east = east_ref[...]
+    col = lax.broadcasted_iota(jnp.int32, (grid_rows, grid_cols), 1)
+    row = lax.broadcasted_iota(jnp.int32, (grid_rows, grid_cols), 0)
+    first_col = col == 0
+    last_col = col == grid_cols - 1
+    first_row = row == 0
+    last_row = row == grid_rows - 1
+    west_depth = jnp.where(first_col, west[:, channels : channels + 1], pltpu.roll(depth, 1, 1))
+    east_depth = jnp.where(last_col, east[:, channels : channels + 1], pltpu.roll(depth, grid_cols - 1, 1))
+    for d in range(channels):
+        energy = spec_ref[d] * mask
+        west_energy = jnp.where(first_col, west[:, d : d + 1], pltpu.roll(energy, 1, 1))
+        east_energy = jnp.where(last_col, east[:, d : d + 1], pltpu.roll(energy, grid_cols - 1, 1))
+        east_coef = coef_ref[0, d]
+        north_coef = coef_ref[1, d]
+        east_mid = east_coef * depth
+        north_rate = north_coef * depth
+        inflow = (
+            jnp.maximum(east_coef * west_depth, 0.0) * west_energy
+            + jnp.maximum(-(east_coef * east_depth), 0.0) * east_energy
+        )
+        south_flux = jnp.maximum(north_rate, 0.0) * energy
+        north_flux = jnp.maximum(-north_rate, 0.0) * energy
+        from_south = jnp.where(first_row, 0.0, pltpu.roll(south_flux, 1, 0))
+        from_north = jnp.where(last_row, 0.0, pltpu.roll(north_flux, grid_rows - 1, 0))
+        updated = (
+            energy
+            - (jnp.abs(east_mid) + jnp.abs(north_rate)) * energy
+            + inflow
+            + from_south
+            + from_north
+        )
+        spaced_ref[d] = updated * mask
+    turning = turn_ref[...]
+    turn_plus = jnp.maximum(turning, 0.0)
+    behind = jnp.maximum(-turning, 0.0)
+    turn_abs = jnp.abs(turning)
+    for d in range(channels):
+        here = spaced_ref[d]
+        out_ref[d] = (
+            here
+            - turn_abs * here
+            + turn_plus * spaced_ref[(d - 1) % channels]
+            + behind * spaced_ref[(d + 1) % channels]
+        )
+
+
+def propagate(spectrum, depth, sea_mask, turning, from_west, from_east, coef):
+    vmem = pl.BlockSpec(memory_space=pltpu.VMEM)
+    return pl.pallas_call(
+        propagate_kernel,
+        out_shape=jax.ShapeDtypeStruct(spectrum.shape, jnp.float32),
+        in_specs=[pl.BlockSpec(memory_space=pltpu.SMEM)] + [vmem] * 6,
+        out_specs=vmem,
+        scratch_shapes=[pltpu.VMEM(spectrum.shape, jnp.float32)],
+    )(coef, spectrum, sea_mask, depth, turning, from_west, from_east)
+
+
 def shards(spectrum, depth_speed, turning, drift, partners, sea_slots, sea_counts):
     channels, grid_rows, grid_cols = spectrum.shape
     n_spec = lax.axis_size("spec")
@@ -161,9 +233,14 @@
     per_block = sub_rows * grid_cols
     sea_list = sea_slots[:, 0, :]
     sea_mask = sea_cells(sea_list, sea_counts[:, 0], per_block).reshape(grid_rows, grid_cols)
-    energy = spectrum * sea_mask
-    stacked = jnp.concatenate([energy, depth_speed[None]], axis=0)
-    padded = extended(stacked, (("tile", 2),), 1)
+    edge_mask = sea_mask[:, ::grid_cols - 1]
+    edges_first = jnp.concatenate(
+        [(spectrum[:, :, 0] * edge_mask[None, :, 0]).T, depth_speed[:, :1]], axis=1
+    )
+    edges_last = jnp.concatenate(
+        [(spectrum[:, :, -1] * edge_mask[None, :, 1]).T, depth_speed[:, -1:]], axis=1
+    )
+    from_west, from_east = neighbours(edges_first, edges_last)
     local_freq = channels // ND
     freq_ids = (
         lax.axis_index("spec") * local_freq + jnp.arange(local_freq, dtype=jnp.int32)
@@ -172,9 +249,8 @@
     angles = 2.0 * jnp.pi * jnp.arange(ND, dtype=jnp.float32) / ND
     cosines = jnp.tile(jnp.cos(angles), local_freq)
     sine_part = jnp.tile(jnp.sin(angles), local_freq)
-    spaced = advect_space(padded[:channels], padded[channels], speeds, cosines, sine_part, sea_mask)
-    turned = advect_direction(spaced.reshape(local_freq, ND, grid_rows, grid_cols), turning)
-    turned = turned.reshape(channels, grid_rows, grid_cols)
+    coef = jnp.stack([speeds * cosines, speeds * sine_part])
+    turned = propagate(spectrum, depth_speed, sea_mask, turning, from_west, from_east, coef)
     points = lax.all_to_all(turned, "spec", split_axis=1, concat_axis=0, tiled=True)
     return settle(points, drift, partners)
 

time: 80.8 us -> 79.2 us (0.980)
  the two profiles are of different devices: /device:TPU:193 before, /device:TPU:8 now
where the time goes in v3:
time: 79.2 us; the launch traced here: 78.7 us
  waiting for transfers between devices  29.2 us (37%)
  starting transfers between devices  18.8 us (24%)
  local copies, waits for them, and re-layouts  16.2 us (20%)
  other arithmetic  9.92 us (13%)
  Pallas kernels  4.02 us (5%)
    all_to_all x1, waiting for transfers between devices, shards(): lax.all_to_all(turned, 'spec', split_axis=1, concat_axis=0, tiled=True)  28.3 us
    all_to_all x1, starting transfers between devices, shards(): lax.all_to_all(turned, 'spec', split_axis=1, concat_axis=0, tiled=True)  10.3 us
    ppermute x1, starting transfers between devices, neighbours(): lax.ppermute(edges_first, 'tile', [((i + 1) % count, i) for i in range(co...  8.49 us
    pallas_call x1, Pallas kernels, propagate(): pl.pallas_call(propagate_kernel, out_shape=jax.ShapeDtypeStruct(spectrum....  4.02 us
    unnamed x21, local copies, waits for them, and re-layouts  3.33 us
    pallas_call x1, local copies, waits for them, and re-layouts, propagate(): pl.pallas_call(propagate_kernel, out_shape=jax.ShapeDtypeStruct(spectrum....  3.04 us
    reduce_or x1, other arithmetic, sea_cells(): return jnp.any(matches, axis=1).astype(jnp.float32)  2.32 us
    slice x1, local copies, waits for them, and re-layouts, shards(): spectrum[:, :, 0] * edge_mask[None, :, 0]  2.06 us
  transfers between devices with their start and end apart: 3, of which 2 were waited for; matrix products, arithmetic and copies ran while one was open for 4% of the time, Pallas kernels for 0%

profile of v3, /device:TPU:8, one launch (start us, length us, event | category | flops | bytes accessed | tf_op | source)
XLA Modules:
  0.0 78.7 jit_solution(14182947347468242437)
XLA Ops:
  0.0 0.8 copy.70
  0.8 0.7 iota_compare_fusion.1
  1.5 2.3 %fusion.1 = pred[32,256]{1,0:T(8,128)(4,1)S(1)} fusion(s32[32,192]{1,0:T(8,128)S(1)} %bitcast.72, pred[32,192]{1,0:T(8,128)(4,1)S(1)} %iota_compare_fusion.1), kind=kLoop, calls=%fused_computation.2 | loop fusion | flops 4710400 | bytes 38912 | tf_op jit(solution)/shard_map/reduce_or | solution.py:38
  3.9 0.1 slice.192
  3.9 0.2 slice_reduce_fusion
  4.1 2.1 %fusion.22 = (f32[36,64,1]{2,1,0:T(8,128)S(1)}, f32[36,64,1]{2,1,0:T(8,128)S(1)}) fusion(f32[36,64,128]{2,1,0:T(8,128)} %spec_ref.1), kind=kLoop, calls=%fused_computation.82 | loop fusion | bytes 36864 | tf_op jit(solution)/shard_map/slice | solution.py:238
  6.2 0.8 copy.57
  7.1 0.1 pad_maximum_fusion
  7.2 0.8 %copy.58 = f32[36,64,1]{0,1,2:T(8,128)S(1)} copy(f32[36,64,1]{2,1,0:T(8,128)S(1)} %get-tuple-element.41) | data formatting | bytes 18432
  8.1 0.1 pad_maximum_fusion.1
  8.2 8.5 %collective-permute-start.1 = (f32[64,37]{1,0:T(8,128)S(1)}, f32[64,37]{1,0:T(8,128)S(1)}, u32[]{:S(2)}, u32[]{:S(2)}) collective-permute-start(f32[64,37]{1,0:T(8,128)S(1)} %pad_maximum_fusion.1), channel_id=1, source_target_pairs={{1,0},{2,1},{3,2},{4,3},{5,4},{6,5},{7,6},{8,7},{9,8},{10,9},{11,1... | collective-permute-start | bytes 28424 | tf_op jit(solution)/shard_map/ppermute | solution.py:162
  16.8 0.6 pad_maximum_fusion.2.coef_ref
  17.4 0.9 %collective-permute-done.1.east_ref = f32[64,37]{1,0:T(8,128)S(1)} collective-permute-done((f32[64,37]{1,0:T(8,128)S(1)}, f32[64,37]{1,0:T(8,128)S(1)}, u32[]{:S(2)}, u32[]{:S(2)}) %collective-permute-start.1) | collective-permute-done | bytes 9504 | tf_op jit(solution)/shard_map/ppermute | solution.py:162
  18.3 0.6 copy-done.3
  18.9 4.0 %shard_map.76 = f32[36,64,128]{2,1,0:T(8,128)} custom-call(f32[2,36]{1,0:T(2,128)} %pad_maximum_fusion.2.coef_ref, f32[36,64,128]{2,1,0:T(8,128)} %spec_ref.1, f32[64,128]{1,0:T(8,128)} %copy-done.1, f32[64,128]{1,0:T(8,128)} %depth_ref.1, f32[64,128]{1,0:T(8,128)} %turn_ref.1, f32[64,37]{1,0:T(8,128)} %copy-done.2, f32[64,37]{1,0:T(8,128)} %copy-done.3), custom_call_target="tpu_custom_call" | custom-call | tf_op jit(solution)/shard_map/pallas_call | solution.py:220
  22.9 3.0 %copy.46 = f32[36,64,128]{2,0,1:T(8,128)} copy(f32[36,64,128]{2,1,0:T(8,128)} %shard_map.76) | data formatting | bytes 2359296 | tf_op jit(solution)/shard_map/pallas_call | solution.py:220
  26.0 10.3 %all-to-all-start = ((f32[36,64,128]{2,0,1:T(8,128)}), f32[36,64,128]{2,0,1:T(8,128)S(1)}, u32[]{:S(2)}, u32[]{:S(2)}) async-start(f32[36,64,128]{2,0,1:T(8,128)} %copy.46), calls=%async_computation | async-start | bytes 2621440 | tf_op jit(solution)/shard_map/all_to_all | solution.py:254
  36.3 0.1 reshape_squeeze.7
  36.7 0.1 max.25
  36.9 0.1 copy.65
  37.0 0.1 max.23
  37.1 0.1 copy.66
  37.2 0.1 abs.12
  37.3 0.1 copy.48
  37.4 0.1 reshape_squeeze.6
  37.6 0.1 compare_and_fusion.4
  37.8 28.3 %all-to-all-done = f32[36,64,128]{2,0,1:T(8,128)S(1)} async-done(((f32[36,64,128]{2,0,1:T(8,128)}), f32[36,64,128]{2,0,1:T(8,128)S(1)}, u32[]{:S(2)}, u32[]{:S(2)}) %all-to-all-start) | async-done | bytes 1179680 | tf_op jit(solution)/shard_map/all_to_all | solution.py:254
  66.1 0.6 copy.67
  66.7 0.9 %reshape.319 = f32[32,36,256]{2,0,1:T(8,128)S(1)} reshape(f32[32,36,2,128]{3,2,0,1:T(2,128)S(1)} %bitcast.67) | data formatting | bytes 2359296 | tf_op jit(solution)/shard_map/reshape | solution.py:118
  67.7 0.4 slice_multiply_fusion.1
  68.0 0.4 fusion.3
  68.5 0.3 fusion.18
  68.8 0.3 fusion.19
  69.0 0.3 fusion.20
  69.5 1.4 %maximum_select_fusion = (f32[32,36,256]{2,0,1:T(8,128)S(1)}, f32[32,36,256]{2,0,1:T(8,128)S(1)}) fusion(f32[3,36,256]{2,0,1:T(4,128)S(1)} %reshape.320, f32[29,36,256]{2,0,1:T(8,128)S(1)} %get-tuple-element.35, f32[2,36,256]{2,0,1:T(2,128)S(1)} %reshape.321, f32[30,36,256]{2,0,1:T(8,128)S(1)} %get-tuple-element.33, f32[32,36,256]{2,0,1:T(8,128)S(1)} %fusion.3, ...), kind=kLoop, calls=%fused_computation.8 | loop fusion | flops 3538944 | bytes 10617024 | tf_op jit(solution)/shard_map/jit(_where)/select_n | solution.py:133
  70.9 0.1 slice.261
  71.5 1.0 %multiply_subtract_fusion.1 = f32[32,36,256]{2,0,1:T(8,128)S(1)} fusion(f32[32,36,256]{2,0,1:T(8,128)S(1)} %fusion.3, f32[32,33,256]{2,0,1:T(8,128)S(1)} %slice.277, f32[32,3,256]{2,0,1:T(8,128)S(1)} %slice.276, f32[32,34,256]{2,0,1:T(8,128)S(1)} %slice.275, f32[32,2,256]{2,0,1:T(8,128)S(1)} %slice.274, f32[32,35,256]{2,0,1:T(8,128)S(1)} %slice.273, ...), kind=kLoop, calls=%fused_computation.24 | loop fusion | flops 5013504 | bytes 9437312 | tf_op jit(solution)/shard_map/sub | solution.py:141
  72.5 0.3 fusion.17
  72.8 0.3 fusion.15
  73.1 0.3 fusion.13
  73.4 0.4 maximum_select_fusion.12
  73.9 0.1 slice.293
  74.0 0.1 slice.294
  74.2 0.1 slice.295
  74.3 0.4 maximum_select_fusion.10
  74.8 1.6 %multiply_add_fusion = f32[32,36,256]{2,0,1:T(8,128)S(1)} fusion(f32[32,36,256]{2,0,1:T(8,128)S(1)} %fusion.3, f32[32,36,256]{2,0,1:T(8,128)S(1)} %multiply_subtract_fusion.1, f32[29,36,256]{2,0,1:T(8,128)S(1)} %slice.295, f32[30,36,256]{2,0,1:T(8,128)S(1)} %slice.294, f32[31,36,256]{2,0,1:T(8,128)S(1)} %slice.293, ...), kind=kLoop, calls=%fused_computation.23 | loop fusion | flops 5603328 | bytes 12534016 | tf_op jit(solution)/shard_map/add | solution.py:156
  76.4 0.7 copy.53
  77.1 1.6 %reshape.324 = f32[1152,2,128]{2,1,0:T(2,128)} reshape(f32[32,36,256]{2,1,0:T(8,128)S(1)} %copy.53) | data formatting | bytes 2359296 | tf_op jit(solution)/shard_map/reshape | solution.py:156
  (54 shorter events, 1.5 us)
Async XLA Ops:
  3.8 2.3 %copy-start.1 = (f32[64,128]{1,0:T(8,128)}, f32[64,128]{1,0:T(8,128)S(1)}, u32[]{:S(2)}) copy-start(f32[64,128]{1,0:T(8,128)S(1)} %reshape.325.mask_ref) | copy-start | bytes 98308
  6.2 0.8 %copy-start = (f32[64,128]{1,0:T(8,128)S(1)}, f32[64,128]{1,0:T(8,128)}, u32[]{:S(2)}) copy-start(f32[64,128]{1,0:T(8,128)} %depth_ref.1) | copy-start | bytes 98308
  7.2 10.1 %collective-permute-start = (f32[64,37]{1,0:T(8,128)S(1)}, f32[64,37]{1,0:T(8,128)S(1)}, u32[]{:S(2)}, u32[]{:S(2)}) collective-permute-start(f32[64,37]{1,0:T(8,128)S(1)} %pad_maximum_fusion), channel_id=1, source_target_pairs={{0,1},{1,2},{2,3},{3,4},{4,5},{5,6},{6,7},{7,8},{8,9},{9,10},{10,1... | collective-permute-start | bytes 28424 | tf_op jit(solution)/shard_map/ppermute | solution.py:161
  8.2 10.1 %collective-permute-start.1 = (f32[64,37]{1,0:T(8,128)S(1)}, f32[64,37]{1,0:T(8,128)S(1)}, u32[]{:S(2)}, u32[]{:S(2)}) collective-permute-start(f32[64,37]{1,0:T(8,128)S(1)} %pad_maximum_fusion.1), channel_id=1, source_target_pairs={{1,0},{2,1},{3,2},{4,3},{5,4},{6,5},{7,6},{8,7},{9,8},{10,9},{11,1... | collective-permute-start | bytes 28424 | tf_op jit(solution)/shard_map/ppermute | solution.py:162
  17.4 0.9 %copy-start.2 = (f32[64,37]{1,0:T(8,128)}, f32[64,37]{1,0:T(8,128)S(1)}, u32[]{:S(2)}) copy-start(f32[64,37]{1,0:T(8,128)S(1)} %collective-permute-done.west_ref) | copy-start | bytes 28420
  18.3 0.6 copy-start.3
  26.0 10.3 %copy-start.4 = (s32[2,1152]{1,0:T(2,128)S(1)}, s32[2,1152]{1,0:T(2,128)}, u32[]{:S(2)}) copy-start(s32[2,1152]{1,0:T(2,128)} %param.11) | copy-start | bytes 27652
  26.0 10.8 %copy-start.5 = (f32[1152]{0:T(1024)S(1)}, f32[1152]{0:T(1024)}, u32[]{:S(2)}) copy-start(f32[1152]{0:T(1024)} %param.10) | copy-start | bytes 13828
  26.0 40.1 %all-to-all-start = ((f32[36,64,128]{2,0,1:T(8,128)}), f32[36,64,128]{2,0,1:T(8,128)S(1)}, u32[]{:S(2)}, u32[]{:S(2)}) async-start(f32[36,64,128]{2,0,1:T(8,128)} %copy.46), calls=%async_computation | async-start | bytes 2621440 | tf_op jit(solution)/shard_map/all_to_all | solution.py:254

commit v4 on v3

--- a/solution.py
+++ b/solution.py
@@ -112,20 +112,25 @@
     return out
 
 
-def settle(points, drift, partners):
-    n_freq = NF
-    shape = points.shape
-    grid = points.reshape(n_freq, ND, -1)
-    shifted = advect_frequency(grid, drift, NF, ND).reshape(n_freq, ND, -1)
+def settle(grid, drift, partners):
+    n_freq = grid.shape[0]
+    drift_rate = drift.reshape(n_freq, 1, ND, 1)
+    upward = jnp.maximum(drift_rate, 0.0) * grid
+    downward = jnp.maximum(-drift_rate, 0.0) * grid
+    empty_row = jnp.zeros_like(grid[:1])
+    from_below = jnp.concatenate([empty_row, upward[:-1]], axis=0)
+    from_above = jnp.concatenate([downward[1:], empty_row], axis=0)
+    shifted = grid - jnp.abs(drift_rate) * grid + from_below + from_above
     freq_ids = jnp.arange(n_freq, dtype=jnp.int32)
     up_ids = partners[0].reshape(n_freq, ND)[:, 0]
     down_ids = partners[1].reshape(n_freq, ND)[:, 0]
     up_freq = up_ids // ND
     down_freq = down_ids // ND
-    up_turn = (up_ids % ND)[:, None, None]
-    down_turn = (ND - down_ids % ND)[:, None, None]
-    up_step = (up_freq - freq_ids)[:, None, None]
-    down_step = (freq_ids - down_freq)[:, None, None]
+    per_freq = (n_freq, 1, 1, 1)
+    up_turn = (up_ids % ND).reshape(per_freq)
+    down_turn = (ND - down_ids % ND).reshape(per_freq)
+    up_step = (up_freq - freq_ids).reshape(per_freq)
+    down_step = (freq_ids - down_freq).reshape(per_freq)
 
     def by_freq(step, up):
         out = shifted
@@ -135,25 +140,25 @@
 
     up_src = by_freq(up_step, True)
     down_src = by_freq(down_step, False)
-    plus_values = pick_shift(up_turn, [jnp.roll(up_src, -r, axis=1) for r in (1, 2, 3)])
-    minus_values = pick_shift(down_turn, [jnp.roll(down_src, r, axis=1) for r in (1, 2, 3)])
+    plus_values = pick_shift(up_turn, [jnp.roll(up_src, -r, axis=2) for r in (1, 2, 3)])
+    minus_values = pick_shift(down_turn, [jnp.roll(down_src, r, axis=2) for r in (1, 2, 3)])
     quartet = (
         shifted * shifted * (plus_values + minus_values)
         - 2.0 * shifted * plus_values * minus_values
     )
-    back_up = pick_shift(up_turn, [jnp.roll(quartet, r, axis=1) for r in (1, 2, 3)])
-    back_down = pick_shift(down_turn, [jnp.roll(quartet, -r, axis=1) for r in (1, 2, 3)])
+    back_up = pick_shift(up_turn, [jnp.roll(quartet, r, axis=2) for r in (1, 2, 3)])
+    back_down = pick_shift(down_turn, [jnp.roll(quartet, -r, axis=2) for r in (1, 2, 3)])
     to_up = jnp.zeros_like(quartet)
     to_down = jnp.zeros_like(quartet)
     for s in (0, 1, 2, 3):
         src_up = pad_freq(up_freq, s, False)
-        hit_up = (src_up == freq_ids) & (freq_ids >= s)
-        to_up = to_up + jnp.where(hit_up[:, None, None], pad_freq(back_up, s, False), 0.0)
+        hit_up = ((src_up == freq_ids) & (freq_ids >= s)).reshape(per_freq)
+        to_up = to_up + jnp.where(hit_up, pad_freq(back_up, s, False), 0.0)
         src_down = pad_freq(down_freq, s, True)
-        hit_down = (src_down == freq_ids) & (freq_ids + s < n_freq)
-        to_down = to_down + jnp.where(hit_down[:, None, None], pad_freq(back_down, s, True), 0.0)
+        hit_down = ((src_down == freq_ids) & (freq_ids + s < n_freq)).reshape(per_freq)
+        to_down = to_down + jnp.where(hit_down, pad_freq(back_down, s, True), 0.0)
     source = to_up + to_down - 2.0 * quartet
-    return (shifted + dia_coeff * source).reshape(shape)
+    return shifted + dia_coeff * source
 
 
 def neighbours(edges_first, edges_last):
@@ -251,8 +256,11 @@
     sine_part = jnp.tile(jnp.sin(angles), local_freq)
     coef = jnp.stack([speeds * cosines, speeds * sine_part])
     turned = propagate(spectrum, depth_speed, sea_mask, turning, from_west, from_east, coef)
-    points = lax.all_to_all(turned, "spec", split_axis=1, concat_axis=0, tiled=True)
-    return settle(points, drift, partners)
+    by_row = jnp.transpose(turned, (1, 0, 2))
+    points = lax.all_to_all(by_row, "spec", split_axis=0, concat_axis=0, tiled=True)
+    grid = points.reshape(NF, sub_rows, ND, grid_cols)
+    settled = settle(grid, drift, partners)
+    return jnp.transpose(settled, (0, 2, 1, 3)).reshape(NF * ND, sub_rows, grid_cols)
 
 
 def solution(mesh):

time: 79.2 us -> 80.3 us (1.014)
  the two profiles are of different devices: /device:TPU:8 before, /device:TPU:193 now
where the time goes in v4:
time: 80.3 us; the launch traced here: 79.6 us
  waiting for transfers between devices  34.3 us (43%)
  local copies, waits for them, and re-layouts  16 us (20%)
  starting transfers between devices  13.9 us (17%)
  other arithmetic  10.9 us (14%)
  Pallas kernels  4.02 us (5%)
    all_to_all x1, waiting for transfers between devices, shards(): lax.all_to_all(by_row, 'spec', split_axis=0, concat_axis=0, tiled=True)  30.4 us
    all_to_all x1, starting transfers between devices, shards(): lax.all_to_all(by_row, 'spec', split_axis=0, concat_axis=0, tiled=True)  9.98 us
    pallas_call x1, Pallas kernels, propagate(): pl.pallas_call(propagate_kernel, out_shape=jax.ShapeDtypeStruct(spectrum....  4.02 us
    ppermute x1, waiting for transfers between devices, neighbours(): lax.ppermute(edges_first, 'tile', [((i + 1) % count, i) for i in range(co...  3.89 us
    ppermute x1, starting transfers between devices, neighbours(): lax.ppermute(edges_last, 'tile', [(i, (i + 1) % count) for i in range(cou...  3.87 us
    unnamed x17, local copies, waits for them, and re-layouts  3.58 us
    transpose x1, local copies, waits for them, and re-layouts, shards(): by_row = jnp.transpose(turned, (1, 0, 2))  3.02 us
    transpose x1, other arithmetic, shards(): jnp.transpose(settled, (0, 2, 1, 3)).reshape(NF * ND, sub_rows, grid_cols)  2.47 us
  transfers between devices with their start and end apart: 3, of which 2 were waited for; matrix products, arithmetic and copies ran while one was open for 3% of the time, Pallas kernels for 0%

profile of v4, /device:TPU:193, one launch (start us, length us, event | category | flops | bytes accessed | tf_op | source)
XLA Modules:
  0.0 79.6 jit_solution(2865141705096939631)
XLA Ops:
  0.0 0.7 iota_compare_fusion.1
  0.7 0.8 copy.39
  1.5 2.3 %fusion.1 = pred[32,256]{1,0:T(8,128)(4,1)S(1)} fusion(s32[32,192]{1,0:T(8,128)S(1)} %bitcast.66, pred[32,192]{1,0:T(8,128)(4,1)S(1)} %iota_compare_fusion.1), kind=kLoop, calls=%fused_computation.2 | loop fusion | flops 4710400 | bytes 38912 | tf_op jit(solution)/shard_map/reduce_or | solution.py:38
  3.8 0.1 slice.192
  3.9 0.2 slice_reduce_fusion
  4.1 0.9 %fusion.23 = (f32[64,1]{1,0:T(8,128)S(1)}, f32[64,1]{1,0:T(8,128)S(1)}) fusion(f32[64,128]{1,0:T(8,128)} %depth_ref.1), kind=kLoop, calls=%fused_computation.82 | loop fusion | bytes 1024 | tf_op jit(solution)/shard_map/slice | solution.py:243
  5.0 2.1 %fusion.22 = (f32[36,64,1]{2,1,0:T(8,128)S(1)}, f32[36,64,1]{2,1,0:T(8,128)S(1)}) fusion(f32[36,64,128]{2,1,0:T(8,128)} %spec_ref.1), kind=kLoop, calls=%fused_computation.81 | loop fusion | bytes 36864 | tf_op jit(solution)/shard_map/slice | solution.py:243
  7.1 0.8 copy.34
  8.0 0.1 pad_maximum_fusion
  8.0 3.9 %collective-permute-start = (f32[64,37]{1,0:T(8,128)S(1)}, f32[64,37]{1,0:T(8,128)S(1)}, u32[]{:S(2)}, u32[]{:S(2)}) collective-permute-start(f32[64,37]{1,0:T(8,128)S(1)} %pad_maximum_fusion), channel_id=1, source_target_pairs={{0,1},{1,2},{2,3},{3,4},{4,5},{5,6},{6,7},{7,8},{8,9},{9,10},{10,1... | collective-permute-start | bytes 28424 | tf_op jit(solution)/shard_map/ppermute | solution.py:166
  11.9 0.8 copy.35
  12.8 0.1 pad_maximum_fusion.1
  13.0 0.6 pad_maximum_fusion.2.coef_ref
  13.5 3.9 %collective-permute-done.1.east_ref = f32[64,37]{1,0:T(8,128)S(1)} collective-permute-done((f32[64,37]{1,0:T(8,128)S(1)}, f32[64,37]{1,0:T(8,128)S(1)}, u32[]{:S(2)}, u32[]{:S(2)}) %collective-permute-start.1) | collective-permute-done | bytes 9504 | tf_op jit(solution)/shard_map/ppermute | solution.py:167
  17.4 0.6 copy-done.3
  18.0 4.0 %shard_map.76 = f32[36,64,128]{2,1,0:T(8,128)} custom-call(f32[2,36]{1,0:T(2,128)} %pad_maximum_fusion.2.coef_ref, f32[36,64,128]{2,1,0:T(8,128)} %spec_ref.1, f32[64,128]{1,0:T(8,128)} %copy-done.1, f32[64,128]{1,0:T(8,128)} %depth_ref.1, f32[64,128]{1,0:T(8,128)} %turn_ref.1, f32[64,37]{1,0:T(8,128)} %copy-done.2, f32[64,37]{1,0:T(8,128)} %copy-done.3), custom_call_target="tpu_custom_call" | custom-call | tf_op jit(solution)/shard_map/pallas_call | solution.py:225
  22.0 3.0 %copy.29 = f32[64,36,128]{2,1,0:T(8,128)} copy(f32[64,36,128]{2,0,1:T(8,128)} %bitcast.65) | data formatting | bytes 2359296 | tf_op jit(solution)/shard_map/transpose | solution.py:259
  25.1 10.0 %all-to-all-start = ((f32[64,36,128]{2,1,0:T(8,128)}), f32[64,36,128]{2,1,0:T(8,128)S(1)}, u32[]{:S(2)}, u32[]{:S(2)}) async-start(f32[64,36,128]{2,1,0:T(8,128)} %copy.29), calls=%async_computation | async-start | bytes 2621440 | tf_op jit(solution)/shard_map/all_to_all | solution.py:260
  35.1 0.1 reshape_squeeze.7
  35.5 0.1 reshape_squeeze.6
  35.7 0.1 abs.12
  35.8 0.1 max.25
  35.9 0.1 max.23
  36.1 0.1 compare_and_fusion.2
  36.3 30.4 %all-to-all-done = f32[64,36,128]{2,1,0:T(8,128)S(1)} async-done(((f32[64,36,128]{2,1,0:T(8,128)}), f32[64,36,128]{2,1,0:T(8,128)S(1)}, u32[]{:S(2)}, u32[]{:S(2)}) %all-to-all-start) | async-done | bytes 1179680 | tf_op jit(solution)/shard_map/all_to_all | solution.py:260
  66.7 0.4 slice_multiply_fusion.1
  67.1 0.4 fusion.3
  67.5 0.2 fusion.21
  67.6 0.2 fusion.20
  67.8 0.2 fusion.18
  68.1 1.3 %maximum_select_fusion = (f32[32,2,36,128]{3,2,1,0:T(8,128)S(1)}, f32[32,2,36,128]{3,2,1,0:T(8,128)S(1)}) fusion(f32[3,2,36,128]{3,2,1,0:T(8,128)S(1)} %reshape.331, f32[29,2,36,128]{3,2,1,0:T(8,128)S(1)} %get-tuple-element.39, f32[2,2,36,128]{3,2,1,0:T(8,128)S(1)} %reshape.332, f32[30,2,36,128]{3,2,1,0:T(8,128)S(1)} %get-tuple-element.37, ...), kind=kLoop, calls=%fused_computation.6 | loop fusion | flops 3538944 | bytes 10617024 | tf_op jit(solution)/shard_map/jit(_where)/select_n | solution.py:138
  69.6 0.1 slice.265
  69.7 0.1 slice.263
  69.8 0.1 slice.261
  69.9 1.3 %multiply_subtract_fusion.1 = f32[32,2,36,128]{3,2,1,0:T(8,128)S(1)} fusion(f32[32,2,36,128]{3,2,1,0:T(8,128)S(1)} %fusion.3, f32[32,2,33,128]{3,2,1,0:T(8,128)S(1)} %bitcast.60, f32[32,2,3,128]{3,2,1,0:T(4,128)S(1)} %slice.276, f32[32,2,34,128]{3,2,1,0:T(8,128)S(1)} %bitcast.61, f32[32,2,2,128]{3,2,1,0:T(2,128)S(1)} %slice.274, ...), kind=kLoop, calls=%fused_computation.21 | loop fusion | flops 5013504 | bytes 9437312 | tf_op jit(solution)/shard_map/sub | solution.py:146
  71.4 0.2 fusion.13
  71.7 0.2 fusion.15
  71.9 0.2 fusion.17
  72.1 0.5 maximum_select_fusion.10
  72.7 0.4 maximum_select_fusion.12
  73.1 0.1 slice.294
  73.2 0.5 copy-done
  73.7 0.1 slice.284
  73.8 0.1 slice.293
  73.9 1.2 %slice-done = f32[29,2,36,128]{3,2,1,0:T(8,128)S(1)} async-done(((f32[32,2,36,128]{3,2,1,0:T(8,128)}), f32[29,2,36,128]{3,2,1,0:T(8,128)S(1)}, s32[]{:S(2)}) %slice-start) | async-done | bytes 1069080 | tf_op jit(solution)/shard_map/slice | solution.py:105
  75.1 0.4 slice-done.1
  75.5 2.5 %add_bitcast_fusion = f32[32,36,2,128]{3,1,2,0:T(8,128)S(1)} fusion(f32[32,2,36,128]{3,2,1,0:T(8,128)S(1)} %fusion.3, f32[32,2,36,128]{3,2,1,0:T(8,128)S(1)} %multiply_subtract_fusion.1, f32[29,2,36,128]{3,2,1,0:T(8,128)S(1)} %slice.295, f32[30,2,36,128]{3,2,1,0:T(8,128)S(1)} %slice.294, f32[31,2,36,128]{3,2,1,0:T(8,128)S(1)} %slice.293, ...), kind=kLoop, calls=%fused_computation.20 | loop fusion | flops 5603328 | bytes 12534016 | tf_op jit(solution)/shard_map/transpose | solution.py:263
  78.0 1.6 %copy.32 = f32[32,36,2,128]{3,2,1,0:T(2,128)} copy(f32[32,36,2,128]{3,1,2,0:T(8,128)S(1)} %add_bitcast_fusion) | data formatting | bytes 2359296 | tf_op jit(solution)/shard_map/transpose | solution.py:263
  (48 shorter events, 1.2 us)
Async XLA Ops:
  3.8 3.3 %copy-start.1 = (f32[64,128]{1,0:T(8,128)}, f32[64,128]{1,0:T(8,128)S(1)}, u32[]{:S(2)}) copy-start(f32[64,128]{1,0:T(8,128)S(1)} %reshape.336.mask_ref) | copy-start | bytes 98308
  8.0 5.5 %collective-permute-start = (f32[64,37]{1,0:T(8,128)S(1)}, f32[64,37]{1,0:T(8,128)S(1)}, u32[]{:S(2)}, u32[]{:S(2)}) collective-permute-start(f32[64,37]{1,0:T(8,128)S(1)} %pad_maximum_fusion), channel_id=1, source_target_pairs={{0,1},{1,2},{2,3},{3,4},{4,5},{5,6},{6,7},{7,8},{8,9},{9,10},{10,1... | collective-permute-start | bytes 28424 | tf_op jit(solution)/shard_map/ppermute | solution.py:166
  12.8 4.6 %collective-permute-start.1 = (f32[64,37]{1,0:T(8,128)S(1)}, f32[64,37]{1,0:T(8,128)S(1)}, u32[]{:S(2)}, u32[]{:S(2)}) collective-permute-start(f32[64,37]{1,0:T(8,128)S(1)} %pad_maximum_fusion.1), channel_id=1, source_target_pairs={{1,0},{2,1},{3,2},{4,3},{5,4},{6,5},{7,6},{8,7},{9,8},{10,9},{11,1... | collective-permute-start | bytes 28424 | tf_op jit(solution)/shard_map/ppermute | solution.py:167
  13.5 3.9 %copy-start.2 = (f32[64,37]{1,0:T(8,128)}, f32[64,37]{1,0:T(8,128)S(1)}, u32[]{:S(2)}) copy-start(f32[64,37]{1,0:T(8,128)S(1)} %collective-permute-done.west_ref) | copy-start | bytes 28420
  17.4 0.6 copy-start.3
  25.1 10.0 %copy-start.4 = (s32[2,1152]{1,0:T(2,128)S(1)}, s32[2,1152]{1,0:T(2,128)}, u32[]{:S(2)}) copy-start(s32[2,1152]{1,0:T(2,128)} %param.11) | copy-start | bytes 27652
  25.1 10.6 %copy-start.5 = (f32[1152]{0:T(1024)S(1)}, f32[1152]{0:T(1024)}, u32[]{:S(2)}) copy-start(f32[1152]{0:T(1024)} %param.10) | copy-start | bytes 13828
  25.1 41.6 %all-to-all-start = ((f32[64,36,128]{2,1,0:T(8,128)}), f32[64,36,128]{2,1,0:T(8,128)S(1)}, u32[]{:S(2)}, u32[]{:S(2)}) async-start(f32[64,36,128]{2,1,0:T(8,128)} %copy.29), calls=%async_computation | async-start | bytes 2621440 | tf_op jit(solution)/shard_map/all_to_all | solution.py:260
  72.6 1.1 %copy-start = (f32[32,2,36,128]{3,2,1,0:T(8,128)}, f32[32,2,36,128]{3,2,1,0:T(8,128)S(1)}, u32[]{:S(2)}) copy-start(f32[32,2,36,128]{3,2,1,0:T(8,128)S(1)} %maximum_select_fusion.10) | copy-start | bytes 3538948
  73.8 1.3 %slice-start = ((f32[32,2,36,128]{3,2,1,0:T(8,128)}), f32[29,2,36,128]{3,2,1,0:T(8,128)S(1)}, s32[]{:S(2)}) async-start(f32[32,2,36,128]{3,2,1,0:T(8,128)} %copy-done), calls=%async_computation.1 | async-start | bytes 2375680 | tf_op jit(solution)/shard_map/slice | solution.py:105
  73.8 1.7 %slice-start.1 = ((f32[32,2,36,128]{3,2,1,0:T(8,128)}), f32[30,2,36,128]{3,2,1,0:T(8,128)S(1)}, s32[]{:S(2)}) async-start(f32[32,2,36,128]{3,2,1,0:T(8,128)} %copy-done), calls=%async_computation.2 | async-start | bytes 2457600 | tf_op jit(solution)/shard_map/slice | solution.py:105

commit v5 on v4

--- a/solution.py
+++ b/solution.py
@@ -212,7 +212,7 @@
     turn_abs = jnp.abs(turning)
     for d in range(channels):
         here = spaced_ref[d]
-        out_ref[d] = (
+        out_ref[:, d, :] = (
             here
             - turn_abs * here
             + turn_plus * spaced_ref[(d - 1) % channels]
@@ -220,11 +220,38 @@
         )
 
 
+def edges_kernel(spec_ref, mask_ref, depth_ref, first_ref, last_ref):
+    channels, grid_rows, grid_cols = spec_ref.shape
+    mask = mask_ref[...]
+    depth = depth_ref[...]
+    lane = lax.broadcasted_iota(jnp.int32, (grid_rows, grid_cols), 1)
+    first = jnp.where(lane == channels, depth[:, :1], 0.0)
+    last = jnp.where(lane == channels, depth[:, grid_cols - 1 :], 0.0)
+    for d in range(channels):
+        energy = spec_ref[d] * mask
+        first = jnp.where(lane == d, energy[:, :1], first)
+        last = jnp.where(lane == d, energy[:, grid_cols - 1 :], last)
+    first_ref[...] = first
+    last_ref[...] = last
+
+
+def edges(spectrum, sea_mask, depth):
+    vmem = pl.BlockSpec(memory_space=pltpu.VMEM)
+    plane = jax.ShapeDtypeStruct(depth.shape, jnp.float32)
+    return pl.pallas_call(
+        edges_kernel,
+        out_shape=(plane, plane),
+        in_specs=[vmem] * 3,
+        out_specs=(vmem, vmem),
+    )(spectrum, sea_mask, depth)
+
+
 def propagate(spectrum, depth, sea_mask, turning, from_west, from_east, coef):
+    channels, grid_rows, grid_cols = spectrum.shape
     vmem = pl.BlockSpec(memory_space=pltpu.VMEM)
     return pl.pallas_call(
         propagate_kernel,
-        out_shape=jax.ShapeDtypeStruct(spectrum.shape, jnp.float32),
+        out_shape=jax.ShapeDtypeStruct((grid_rows, channels, grid_cols), jnp.float32),
         in_specs=[pl.BlockSpec(memory_space=pltpu.SMEM)] + [vmem] * 6,
         out_specs=vmem,
         scratch_shapes=[pltpu.VMEM(spectrum.shape, jnp.float32)],
@@ -238,13 +265,7 @@
     per_block = sub_rows * grid_cols
     sea_list = sea_slots[:, 0, :]
     sea_mask = sea_cells(sea_list, sea_counts[:, 0], per_block).reshape(grid_rows, grid_cols)
-    edge_mask = sea_mask[:, ::grid_cols - 1]
-    edges_first = jnp.concatenate(
-        [(spectrum[:, :, 0] * edge_mask[None, :, 0]).T, depth_speed[:, :1]], axis=1
-    )
-    edges_last = jnp.concatenate(
-        [(spectrum[:, :, -1] * edge_mask[None, :, 1]).T, depth_speed[:, -1:]], axis=1
-    )
+    edges_first, edges_last = edges(spectrum, sea_mask, depth_speed)
     from_west, from_east = neighbours(edges_first, edges_last)
     local_freq = channels // ND
     freq_ids = (
@@ -256,8 +277,7 @@
     sine_part = jnp.tile(jnp.sin(angles), local_freq)
     coef = jnp.stack([speeds * cosines, speeds * sine_part])
     turned = propagate(spectrum, depth_speed, sea_mask, turning, from_west, from_east, coef)
-    by_row = jnp.transpose(turned, (1, 0, 2))
-    points = lax.all_to_all(by_row, "spec", split_axis=0, concat_axis=0, tiled=True)
+    points = lax.all_to_all(turned, "spec", split_axis=0, concat_axis=0, tiled=True)
     grid = points.reshape(NF, sub_rows, ND, grid_cols)
     settled = settle(grid, drift, partners)
     return jnp.transpose(settled, (0, 2, 1, 3)).reshape(NF * ND, sub_rows, grid_cols)

time: 80.3 us -> 76.2 us (0.949)
  local copies, waits for them, and re-layouts: 16 us -> 8.77 us
  Pallas kernels: 4.02 us -> 7.38 us
    pallas_call x1 -> x2, Pallas kernels: 4.02 us -> 7.38 us  [the longest x1 4.63 us: propagate(): pl.pallas_call(propagate_kernel, out_shape=jax.ShapeDtypeStruct((grid_row...]
    slice x4 -> x0, local copies, waits for them, and re-layouts: 3.23 us -> none  [the longest x1 2.06 us: shards(): spectrum[:, :, 0] * edge_mask[None, :, 0]]
    transpose x1 -> x0, local copies, waits for them, and re-layouts: 3.02 us -> none  [shards(): by_row = jnp.transpose(turned, (1, 0, 2))]
    unnamed x17 -> x13, local copies, waits for them, and re-layouts: 3.58 us -> 2.02 us
  transfers between devices with their start and end apart: 3 -> 3, of which waited for: 2 -> 3; matrix products, arithmetic and copies ran while one was open for 3% -> 2% of each run, Pallas kernels for 0% -> 0%
where the time goes in v5:
time: 76.2 us; the launch traced here: 75.6 us
  waiting for transfers between devices  34.7 us (46%)
  starting transfers between devices  13.7 us (18%)
  other arithmetic  10.7 us (14%)
  local copies, waits for them, and re-layouts  8.77 us (12%)
  Pallas kernels  7.38 us (10%)
    all_to_all x1, waiting for transfers between devices, shards(): lax.all_to_all(turned, 'spec', split_axis=0, concat_axis=0, tiled=True)  30.6 us
    all_to_all x1, starting transfers between devices, shards(): lax.all_to_all(turned, 'spec', split_axis=0, concat_axis=0, tiled=True)  9.8 us
    pallas_call x1, Pallas kernels, propagate(): pl.pallas_call(propagate_kernel, out_shape=jax.ShapeDtypeStruct((grid_row...  4.63 us
    ppermute x1, starting transfers between devices, neighbours(): lax.ppermute(edges_last, 'tile', [(i, (i + 1) % count) for i in range(cou...  3.86 us
    ppermute x1, waiting for transfers between devices, neighbours(): lax.ppermute(edges_first, 'tile', [((i + 1) % count, i) for i in range(co...  3.42 us
    pallas_call x1, Pallas kernels, edges(): pl.pallas_call(edges_kernel, out_shape=(plane, plane), in_specs=[vmem] *...  2.75 us
    transpose x1, other arithmetic, shards(): jnp.transpose(settled, (0, 2, 1, 3)).reshape(NF * ND, sub_rows, grid_cols)  2.47 us
    reduce_or x1, other arithmetic, sea_cells(): return jnp.any(matches, axis=1).astype(jnp.float32)  2.31 us
  transfers between devices with their start and end apart: 3, of which 3 were waited for; matrix products, arithmetic and copies ran while one was open for 2% of the time, Pallas kernels for 0%

profile of v5, /device:TPU:193, one launch (start us, length us, event | category | flops | bytes accessed | tf_op | source)
XLA Modules:
  0.0 75.6 jit_solution(18220175802976400809)
XLA Ops:
  0.0 0.7 iota_compare_fusion.1
  0.7 0.8 %copy.18 = s32[32,1,192]{2,0,1:T(8,128)S(1)} copy(s32[32,1,192]{2,1,0:T(1,128)} %param.12) | data formatting | bytes 49152
  1.5 2.3 %fusion.1 = pred[32,256]{1,0:T(8,128)(4,1)S(1)} fusion(s32[32,192]{1,0:T(8,128)S(1)} %bitcast.52, pred[32,192]{1,0:T(8,128)(4,1)S(1)} %iota_compare_fusion.1), kind=kLoop, calls=%fused_computation.2 | loop fusion | flops 4710400 | bytes 38912 | tf_op jit(solution)/shard_map/reduce_or | solution.py:38
  3.8 0.6 reshape.334.mask_ref
  4.4 2.7 %shard_map.76 = (f32[64,128]{1,0:T(8,128)}, f32[64,128]{1,0:T(8,128)}) custom-call(f32[36,64,128]{2,1,0:T(8,128)} %spec_ref.3, f32[64,128]{1,0:T(8,128)} %reshape.334.mask_ref, f32[64,128]{1,0:T(8,128)} %depth_ref.3), custom_call_target="tpu_custom_call" | custom-call | tf_op jit(solution)/shard_map/pallas_call | solution.py:241
  7.2 3.9 %collective-permute-start = (f32[64,128]{1,0:T(8,128)}, f32[64,128]{1,0:T(8,128)S(1)}, u32[]{:S(2)}, u32[]{:S(2)}) collective-permute-start(f32[64,128]{1,0:T(8,128)} %get-tuple-element.7), channel_id=1, source_target_pairs={{0,1},{1,2},{2,3},{3,4},{4,5},{5,6},{6,7},{7,8},{8,9},{9,10},{10,1... | collective-permute-start | bytes 98312 | tf_op jit(solution)/shard_map/ppermute | solution.py:166
  11.1 0.6 pad_maximum_fusion.coef_ref
  11.8 0.6 collective-permute-done.west_ref
  12.4 3.4 %collective-permute-done.1.east_ref = f32[64,128]{1,0:T(8,128)S(1)} collective-permute-done((f32[64,128]{1,0:T(8,128)}, f32[64,128]{1,0:T(8,128)S(1)}, u32[]{:S(2)}, u32[]{:S(2)}) %collective-permute-start.1) | collective-permute-done | bytes 32800 | tf_op jit(solution)/shard_map/ppermute | solution.py:167
  15.8 0.6 copy-done.2
  16.4 4.6 %shard_map.77 = f32[64,36,128]{2,1,0:T(8,128)} custom-call(f32[2,36]{1,0:T(2,128)} %pad_maximum_fusion.coef_ref, f32[36,64,128]{2,1,0:T(8,128)} %spec_ref.3, f32[64,128]{1,0:T(8,128)} %reshape.334.mask_ref, f32[64,128]{1,0:T(8,128)} %depth_ref.3, f32[64,128]{1,0:T(8,128)} %turn_ref.1, f32[64,128]{1,0:T(8,128)} %copy-done.1, f32[64,128]{1,0:T(8,128)} %copy-done.2), custom_call_target="tpu_custom_call" | custom-call | tf_op jit(solution)/shard_map/pallas_call | solution.py:252
  21.0 9.8 %all-to-all-start = ((f32[64,36,128]{2,1,0:T(8,128)}), f32[64,36,128]{2,1,0:T(8,128)S(1)}, u32[]{:S(2)}, u32[]{:S(2)}) async-start(f32[64,36,128]{2,1,0:T(8,128)} %shard_map.77), calls=%async_computation | async-start | bytes 2621440 | tf_op jit(solution)/shard_map/all_to_all | solution.py:280
  30.9 0.1 reshape_squeeze.7
  31.0 0.1 copy.16
  31.1 0.1 slice.216
  31.2 0.1 slice.218
  31.3 0.1 reshape_squeeze.6
  31.4 0.1 copy.15
  31.5 0.1 abs.12
  31.6 0.1 max.25
  31.7 0.1 max.23
  31.9 0.1 compare_and_fusion.4
  32.0 0.1 compare_and_fusion.2
  32.1 30.6 %all-to-all-done = f32[64,36,128]{2,1,0:T(8,128)S(1)} async-done(((f32[64,36,128]{2,1,0:T(8,128)}), f32[64,36,128]{2,1,0:T(8,128)S(1)}, u32[]{:S(2)}, u32[]{:S(2)}) %all-to-all-start) | async-done | bytes 1179680 | tf_op jit(solution)/shard_map/all_to_all | solution.py:280
  62.7 0.4 slice_multiply_fusion.1
  63.1 0.4 fusion.3
  63.5 0.2 fusion.19
  63.6 0.2 fusion.18
  63.8 0.2 fusion.16
  64.1 1.3 %maximum_select_fusion = (f32[32,2,36,128]{3,2,1,0:T(8,128)S(1)}, f32[32,2,36,128]{3,2,1,0:T(8,128)S(1)}) fusion(f32[3,2,36,128]{3,2,1,0:T(8,128)S(1)} %reshape.329, f32[29,2,36,128]{3,2,1,0:T(8,128)S(1)} %get-tuple-element.41, f32[2,2,36,128]{3,2,1,0:T(8,128)S(1)} %reshape.330, f32[30,2,36,128]{3,2,1,0:T(8,128)S(1)} %get-tuple-element.39, ...), kind=kLoop, calls=%fused_computation.6 | loop fusion | flops 3538944 | bytes 10617024 | tf_op jit(solution)/shard_map/jit(_where)/select_n | solution.py:138
  65.6 0.1 slice.235
  65.7 0.1 slice.233
  65.8 0.1 slice.231
  65.9 1.3 %multiply_subtract_fusion.1 = f32[32,2,36,128]{3,2,1,0:T(8,128)S(1)} fusion(f32[32,2,36,128]{3,2,1,0:T(8,128)S(1)} %fusion.3, f32[32,2,33,128]{3,2,1,0:T(8,128)S(1)} %bitcast.47, f32[32,2,3,128]{3,2,1,0:T(4,128)S(1)} %slice.246, f32[32,2,34,128]{3,2,1,0:T(8,128)S(1)} %bitcast.48, f32[32,2,2,128]{3,2,1,0:T(2,128)S(1)} %slice.244, ...), kind=kLoop, calls=%fused_computation.21 | loop fusion | flops 5013504 | bytes 9437312 | tf_op jit(solution)/shard_map/sub | solution.py:146
  67.4 0.2 fusion.11
  67.7 0.2 fusion.13
  67.9 0.2 fusion.15
  68.1 0.5 maximum_select_fusion.10
  68.6 0.4 maximum_select_fusion.12
  69.0 0.1 slice.265
  69.1 0.1 slice.264
  69.2 0.5 copy-done
  69.7 0.1 slice.254
  69.8 0.1 slice.263
  69.9 1.2 %slice-done = f32[29,2,36,128]{3,2,1,0:T(8,128)S(1)} async-done(((f32[32,2,36,128]{3,2,1,0:T(8,128)}), f32[29,2,36,128]{3,2,1,0:T(8,128)S(1)}, s32[]{:S(2)}) %slice-start) | async-done | bytes 1069080 | tf_op jit(solution)/shard_map/slice | solution.py:105
  71.1 0.4 slice-done.1
  71.5 2.5 %add_bitcast_fusion = f32[32,36,2,128]{3,1,2,0:T(8,128)S(1)} fusion(f32[32,2,36,128]{3,2,1,0:T(8,128)S(1)} %fusion.3, f32[32,2,36,128]{3,2,1,0:T(8,128)S(1)} %multiply_subtract_fusion.1, f32[29,2,36,128]{3,2,1,0:T(8,128)S(1)} %slice.265, f32[30,2,36,128]{3,2,1,0:T(8,128)S(1)} %slice.264, f32[31,2,36,128]{3,2,1,0:T(8,128)S(1)} %slice.263, ...), kind=kLoop, calls=%fused_computation.20 | loop fusion | flops 5603328 | bytes 12534016 | tf_op jit(solution)/shard_map/transpose | solution.py:283
  73.9 1.6 %copy.13 = f32[32,36,2,128]{3,2,1,0:T(2,128)} copy(f32[32,36,2,128]{3,1,2,0:T(8,128)S(1)} %add_bitcast_fusion) | data formatting | bytes 2359296 | tf_op jit(solution)/shard_map/transpose | solution.py:283
  (36 shorter events, 0.6 us)
Async XLA Ops:
  7.2 5.2 %collective-permute-start = (f32[64,128]{1,0:T(8,128)}, f32[64,128]{1,0:T(8,128)S(1)}, u32[]{:S(2)}, u32[]{:S(2)}) collective-permute-start(f32[64,128]{1,0:T(8,128)} %get-tuple-element.7), channel_id=1, source_target_pairs={{0,1},{1,2},{2,3},{3,4},{4,5},{5,6},{6,7},{7,8},{8,9},{9,10},{10,1... | collective-permute-start | bytes 98312 | tf_op jit(solution)/shard_map/ppermute | solution.py:166
  11.0 4.8 %collective-permute-start.1 = (f32[64,128]{1,0:T(8,128)}, f32[64,128]{1,0:T(8,128)S(1)}, u32[]{:S(2)}, u32[]{:S(2)}) collective-permute-start(f32[64,128]{1,0:T(8,128)} %get-tuple-element.8), channel_id=1, source_target_pairs={{1,0},{2,1},{3,2},{4,3},{5,4},{6,5},{7,6},{8,7},{9,8},{10,9},{11,1... | collective-permute-start | bytes 98312 | tf_op jit(solution)/shard_map/ppermute | solution.py:167
  12.4 3.4 %copy-start.1 = (f32[64,128]{1,0:T(8,128)}, f32[64,128]{1,0:T(8,128)S(1)}, u32[]{:S(2)}) copy-start(f32[64,128]{1,0:T(8,128)S(1)} %collective-permute-done.west_ref) | copy-start | bytes 98308
  15.8 0.6 copy-start.2
  21.0 9.8 %copy-start.3 = (s32[2,1152]{1,0:T(2,128)S(1)}, s32[2,1152]{1,0:T(2,128)}, u32[]{:S(2)}) copy-start(s32[2,1152]{1,0:T(2,128)} %param.11) | copy-start | bytes 27652
  21.0 10.5 %copy-start.4 = (f32[1152]{0:T(1024)S(1)}, f32[1152]{0:T(1024)}, u32[]{:S(2)}) copy-start(f32[1152]{0:T(1024)} %param.10) | copy-start | bytes 13828
  21.0 41.6 %all-to-all-start = ((f32[64,36,128]{2,1,0:T(8,128)}), f32[64,36,128]{2,1,0:T(8,128)S(1)}, u32[]{:S(2)}, u32[]{:S(2)}) async-start(f32[64,36,128]{2,1,0:T(8,128)} %shard_map.77), calls=%async_computation | async-start | bytes 2621440 | tf_op jit(solution)/shard_map/all_to_all | solution.py:280
  68.6 1.1 %copy-start = (f32[32,2,36,128]{3,2,1,0:T(8,128)}, f32[32,2,36,128]{3,2,1,0:T(8,128)S(1)}, u32[]{:S(2)}) copy-start(f32[32,2,36,128]{3,2,1,0:T(8,128)S(1)} %maximum_select_fusion.10) | copy-start | bytes 3538948
  69.8 1.3 %slice-start = ((f32[32,2,36,128]{3,2,1,0:T(8,128)}), f32[29,2,36,128]{3,2,1,0:T(8,128)S(1)}, s32[]{:S(2)}) async-start(f32[32,2,36,128]{3,2,1,0:T(8,128)} %copy-done), calls=%async_computation.1 | async-start | bytes 2375680 | tf_op jit(solution)/shard_map/slice | solution.py:105
  69.8 1.7 %slice-start.1 = ((f32[32,2,36,128]{3,2,1,0:T(8,128)}), f32[30,2,36,128]{3,2,1,0:T(8,128)S(1)}, s32[]{:S(2)}) async-start(f32[32,2,36,128]{3,2,1,0:T(8,128)} %copy-done), calls=%async_computation.2 | async-start | bytes 2457600 | tf_op jit(solution)/shard_map/slice | solution.py:105

commit v6 on v5

--- a/solution.py
+++ b/solution.py
@@ -7,6 +7,7 @@
 
 ND = 36
 NF = 32
+PAD_DIR = 40
 
 
 speed_top = 0.6
@@ -112,53 +113,84 @@
     return out
 
 
-def settle(grid, drift, partners):
-    n_freq = grid.shape[0]
-    drift_rate = drift.reshape(n_freq, 1, ND, 1)
-    upward = jnp.maximum(drift_rate, 0.0) * grid
-    downward = jnp.maximum(-drift_rate, 0.0) * grid
-    empty_row = jnp.zeros_like(grid[:1])
-    from_below = jnp.concatenate([empty_row, upward[:-1]], axis=0)
-    from_above = jnp.concatenate([downward[1:], empty_row], axis=0)
-    shifted = grid - jnp.abs(drift_rate) * grid + from_below + from_above
-    freq_ids = jnp.arange(n_freq, dtype=jnp.int32)
-    up_ids = partners[0].reshape(n_freq, ND)[:, 0]
-    down_ids = partners[1].reshape(n_freq, ND)[:, 0]
-    up_freq = up_ids // ND
-    down_freq = down_ids // ND
-    per_freq = (n_freq, 1, 1, 1)
-    up_turn = (up_ids % ND).reshape(per_freq)
-    down_turn = (ND - down_ids % ND).reshape(per_freq)
-    up_step = (up_freq - freq_ids).reshape(per_freq)
-    down_step = (freq_ids - down_freq).reshape(per_freq)
-
-    def by_freq(step, up):
-        out = shifted
-        for s in (1, 2, 3):
-            out = jnp.where(step == s, shift_freq(shifted, s, up), out)
-        return out
-
-    up_src = by_freq(up_step, True)
-    down_src = by_freq(down_step, False)
-    plus_values = pick_shift(up_turn, [jnp.roll(up_src, -r, axis=2) for r in (1, 2, 3)])
-    minus_values = pick_shift(down_turn, [jnp.roll(down_src, r, axis=2) for r in (1, 2, 3)])
-    quartet = (
-        shifted * shifted * (plus_values + minus_values)
-        - 2.0 * shifted * plus_values * minus_values
-    )
-    back_up = pick_shift(up_turn, [jnp.roll(quartet, r, axis=2) for r in (1, 2, 3)])
-    back_down = pick_shift(down_turn, [jnp.roll(quartet, -r, axis=2) for r in (1, 2, 3)])
-    to_up = jnp.zeros_like(quartet)
-    to_down = jnp.zeros_like(quartet)
-    for s in (0, 1, 2, 3):
-        src_up = pad_freq(up_freq, s, False)
-        hit_up = ((src_up == freq_ids) & (freq_ids >= s)).reshape(per_freq)
-        to_up = to_up + jnp.where(hit_up, pad_freq(back_up, s, False), 0.0)
-        src_down = pad_freq(down_freq, s, True)
-        hit_down = ((src_down == freq_ids) & (freq_ids + s < n_freq)).reshape(per_freq)
-        to_down = to_down + jnp.where(hit_down, pad_freq(back_down, s, True), 0.0)
-    source = to_up + to_down - 2.0 * quartet
-    return shifted + dia_coeff * source
+def turn_rows(x, k):
+    d = lax.broadcasted_iota(jnp.int32, x.shape, 0)
+    ahead = pltpu.roll(x, PAD_DIR - k, 0)
+    wrapped = pltpu.roll(x, ND - k, 0)
+    return jnp.where(d + k < ND, ahead, wrapped)
+
+
+def settle_kernel(table_ref, points_ref, drift_ref, out_ref, shifted_ref, quartet_ref, source_ref):
+    n_freq = drift_ref.shape[0]
+    sub_rows = points_ref.shape[0] // n_freq
+    grid_cols = points_ref.shape[2]
+    for r in range(sub_rows):
+
+        def advect(f, carry):
+            here = points_ref[f * sub_rows + r]
+            rate = drift_ref[f]
+            below = jnp.maximum(f - 1, 0)
+            above = jnp.minimum(f + 1, n_freq - 1)
+            from_below = jnp.where(
+                f > 0, jnp.maximum(drift_ref[below], 0.0) * points_ref[below * sub_rows + r], 0.0
+            )
+            from_above = jnp.where(
+                f < n_freq - 1,
+                jnp.maximum(-drift_ref[above], 0.0) * points_ref[above * sub_rows + r],
+                0.0,
+            )
+            shifted_ref[f] = here - jnp.abs(rate) * here + from_below + from_above
+            source_ref[f] = jnp.zeros_like(here)
+            return carry
+
+        lax.fori_loop(0, n_freq, advect, 0)
+
+        def interact(f, carry):
+            up_freq = table_ref[0, f]
+            down_freq = table_ref[1, f]
+            up_turn = table_ref[2, f]
+            down_turn = table_ref[3, f]
+            here = shifted_ref[f]
+            plus_values = turn_rows(shifted_ref[up_freq], up_turn)
+            minus_values = turn_rows(shifted_ref[down_freq], ND - down_turn)
+            quartet = (
+                here * here * (plus_values + minus_values)
+                - 2.0 * here * plus_values * minus_values
+            )
+            quartet_ref[f] = quartet
+            source_ref[up_freq] = source_ref[up_freq] + turn_rows(quartet, ND - up_turn)
+            source_ref[down_freq] = source_ref[down_freq] + turn_rows(quartet, down_turn)
+            return carry
+
+        lax.fori_loop(0, n_freq, interact, 0)
+
+        def finish(f, carry):
+            source = source_ref[f] - 2.0 * quartet_ref[f]
+            value = shifted_ref[f] + dia_coeff * source
+            out_ref[f, :, pl.ds(r * grid_cols, grid_cols)] = value[:ND]
+            return carry
+
+        lax.fori_loop(0, n_freq, finish, 0)
+
+
+def settle(points, drift, partners):
+    n_rows, _, grid_cols = points.shape
+    sub_rows = n_rows // NF
+    up_ids = partners[0].reshape(NF, ND)[:, 0]
+    down_ids = partners[1].reshape(NF, ND)[:, 0]
+    table = jnp.stack([up_ids // ND, down_ids // ND, up_ids % ND, ND - down_ids % ND])
+    rates = jnp.pad(drift.reshape(NF, ND), ((0, 0), (0, PAD_DIR - ND)))
+    rates = jnp.broadcast_to(rates[:, :, None], (NF, PAD_DIR, grid_cols))
+    vmem = pl.BlockSpec(memory_space=pltpu.VMEM)
+    block = pltpu.VMEM((NF, PAD_DIR, grid_cols), jnp.float32)
+    out = pl.pallas_call(
+        settle_kernel,
+        out_shape=jax.ShapeDtypeStruct((NF, ND, sub_rows * grid_cols), jnp.float32),
+        in_specs=[pl.BlockSpec(memory_space=pltpu.SMEM), vmem, vmem],
+        out_specs=vmem,
+        scratch_shapes=[block, block, block],
+    )(table, points, rates)
+    return out.reshape(NF * ND, sub_rows, grid_cols)
 
 
 def neighbours(edges_first, edges_last):
@@ -206,6 +238,7 @@
             + from_north
         )
         spaced_ref[d] = updated * mask
+    out_ref[:, channels:, :] = jnp.zeros((grid_rows, PAD_DIR - channels, grid_cols), jnp.float32)
     turning = turn_ref[...]
     turn_plus = jnp.maximum(turning, 0.0)
     behind = jnp.maximum(-turning, 0.0)
@@ -251,7 +284,7 @@
     vmem = pl.BlockSpec(memory_space=pltpu.VMEM)
     return pl.pallas_call(
         propagate_kernel,
-        out_shape=jax.ShapeDtypeStruct((grid_rows, channels, grid_cols), jnp.float32),
+        out_shape=jax.ShapeDtypeStruct((grid_rows, PAD_DIR, grid_cols), jnp.float32),
         in_specs=[pl.BlockSpec(memory_space=pltpu.SMEM)] + [vmem] * 6,
         out_specs=vmem,
         scratch_shapes=[pltpu.VMEM(spectrum.shape, jnp.float32)],
@@ -278,9 +311,7 @@
     coef = jnp.stack([speeds * cosines, speeds * sine_part])
     turned = propagate(spectrum, depth_speed, sea_mask, turning, from_west, from_east, coef)
     points = lax.all_to_all(turned, "spec", split_axis=0, concat_axis=0, tiled=True)
-    grid = points.reshape(NF, sub_rows, ND, grid_cols)
-    settled = settle(grid, drift, partners)
-    return jnp.transpose(settled, (0, 2, 1, 3)).reshape(NF * ND, sub_rows, grid_cols)
+    return settle(points, drift, partners)
 
 
 def solution(mesh):

time: 76.2 us -> 75.3 us (0.988)
  the two profiles are of different devices: /device:TPU:193 before, /device:TPU:8 now
where the time goes in v6:
time: 75.3 us; the launch traced here: 74.9 us
  waiting for transfers between devices  29.3 us (39%)
  starting transfers between devices  18.8 us (25%)
  Pallas kernels  15.3 us (20%)
  local copies, waits for them, and re-layouts  7.08 us (9%)
  other arithmetic  4.32 us (6%)
    all_to_all x1, waiting for transfers between devices, shards(): lax.all_to_all(turned, 'spec', split_axis=0, concat_axis=0, tiled=True)  28.1 us
    all_to_all x1, starting transfers between devices, shards(): lax.all_to_all(turned, 'spec', split_axis=0, concat_axis=0, tiled=True)  10.3 us
    ppermute x1, starting transfers between devices, neighbours(): lax.ppermute(edges_first, 'tile', [((i + 1) % count, i) for i in range(co...  8.48 us
    pallas_call x1, Pallas kernels, settle(): pl.pallas_call(settle_kernel, out_shape=jax.ShapeDtypeStruct((NF, ND, sub...  7.89 us
    pallas_call x1, Pallas kernels, propagate(): pl.pallas_call(propagate_kernel, out_shape=jax.ShapeDtypeStruct((grid_row...  4.64 us
    reshape x1, local copies, waits for them, and re-layouts, settle(): return out.reshape(NF * ND, sub_rows, grid_cols)  2.77 us
    pallas_call x1, Pallas kernels, edges(): pl.pallas_call(edges_kernel, out_shape=(plane, plane), in_specs=[vmem] *...  2.75 us
    reduce_or x1, other arithmetic, sea_cells(): return jnp.any(matches, axis=1).astype(jnp.float32)  2.32 us
  transfers between devices with their start and end apart: 3, of which 3 were waited for; matrix products, arithmetic and copies ran while one was open for 2% of the time, Pallas kernels for 0%

profile of v6, /device:TPU:8, one launch (start us, length us, event | category | flops | bytes accessed | tf_op | source)
XLA Modules:
  0.0 74.9 jit_solution(14850101969996707935)
XLA Ops:
  0.0 0.8 %copy.18 = s32[32,1,192]{2,0,1:T(8,128)S(1)} copy(s32[32,1,192]{2,1,0:T(1,128)} %param.12) | data formatting | bytes 49152
  0.8 0.7 iota_compare_fusion.1
  1.5 2.3 %fusion.1 = pred[32,256]{1,0:T(8,128)(4,1)S(1)} fusion(s32[32,192]{1,0:T(8,128)S(1)} %bitcast.24, pred[32,192]{1,0:T(8,128)(4,1)S(1)} %iota_compare_fusion.1), kind=kLoop, calls=%fused_computation.2 | loop fusion | flops 4710400 | bytes 38912 | tf_op jit(solution)/shard_map/reduce_or | solution.py:39
  3.8 0.6 reshape.203.mask_ref
  4.4 2.8 %shard_map.76 = (f32[64,128]{1,0:T(8,128)}, f32[64,128]{1,0:T(8,128)}) custom-call(f32[36,64,128]{2,1,0:T(8,128)} %spec_ref.3, f32[64,128]{1,0:T(8,128)} %reshape.203.mask_ref, f32[64,128]{1,0:T(8,128)} %depth_ref.3), custom_call_target="tpu_custom_call" | custom-call | tf_op jit(solution)/shard_map/pallas_call | solution.py:274
  7.2 0.0 collective-permute-start
  7.2 8.5 %collective-permute-start.1 = (f32[64,128]{1,0:T(8,128)}, f32[64,128]{1,0:T(8,128)S(1)}, u32[]{:S(2)}, u32[]{:S(2)}) collective-permute-start(f32[64,128]{1,0:T(8,128)} %get-tuple-element.8), channel_id=1, source_target_pairs={{1,0},{2,1},{3,2},{4,3},{5,4},{6,5},{7,6},{8,7},{9,8},{10,9},{11,1... | collective-permute-start | bytes 98312 | tf_op jit(solution)/shard_map/ppermute | solution.py:199
  15.8 0.6 pad_maximum_fusion.coef_ref
  16.4 1.1 %collective-permute-done.west_ref = f32[64,128]{1,0:T(8,128)S(1)} collective-permute-done((f32[64,128]{1,0:T(8,128)}, f32[64,128]{1,0:T(8,128)S(1)}, u32[]{:S(2)}, u32[]{:S(2)}) %collective-permute-start) | collective-permute-done | bytes 32800 | tf_op jit(solution)/shard_map/ppermute | solution.py:198
  17.5 0.0 copy-start.1
  17.5 0.1 collective-permute-done.1.east_ref
  17.6 0.5 copy-done.1
  18.1 0.0 copy-start.2
  18.1 0.6 copy-done.2
  18.7 4.6 %shard_map.77 = f32[64,40,128]{2,1,0:T(8,128)} custom-call(f32[2,36]{1,0:T(2,128)} %pad_maximum_fusion.coef_ref, f32[36,64,128]{2,1,0:T(8,128)} %spec_ref.3, f32[64,128]{1,0:T(8,128)} %reshape.203.mask_ref, f32[64,128]{1,0:T(8,128)} %depth_ref.3, f32[64,128]{1,0:T(8,128)} %turn_ref.1, f32[64,128]{1,0:T(8,128)} %copy-done.1, f32[64,128]{1,0:T(8,128)} %copy-done.2), custom_call_target="tpu_custom_call" | custom-call | tf_op jit(solution)/shard_map/pallas_call | solution.py:285
  23.4 0.0 copy-start.3
  23.4 0.0 copy-start.4
  23.4 10.3 %all-to-all-start = ((f32[64,40,128]{2,1,0:T(8,128)}), f32[64,40,128]{2,1,0:T(8,128)S(1)}, u32[]{:S(2)}, u32[]{:S(2)}) async-start(f32[64,40,128]{2,1,0:T(8,128)} %shard_map.77), calls=%async_computation | async-start | bytes 2621440 | tf_op jit(solution)/shard_map/all_to_all | solution.py:313
  33.7 0.0 copy-done.3
  33.7 0.1 reshape_squeeze.6
  33.8 0.1 copy.15
  33.9 0.1 reshape_squeeze.7
  34.0 0.1 copy.16
  34.1 0.0 copy-done.4
  34.1 0.1 reshape.201
  34.2 0.6 pad_add_fusion.table_ref
  34.8 28.1 %all-to-all-done.points_ref = f32[64,40,128]{2,1,0:T(8,128)S(1)} async-done(((f32[64,40,128]{2,1,0:T(8,128)}), f32[64,40,128]{2,1,0:T(8,128)S(1)}, u32[]{:S(2)}, u32[]{:S(2)}) %all-to-all-start) | async-done | bytes 1310752 | tf_op jit(solution)/shard_map/all_to_all | solution.py:313
  62.9 0.0 copy-start
  62.9 1.2 %broadcast_in_dim.2.drift_ref = f32[32,40,128]{2,1,0:T(8,128)} broadcast(f32[32,40]{1,0:T(8,128)S(1)} %pad.4), dimensions={0,1} | broadcast | bytes 660480 | tf_op jit(solution)/shard_map/broadcast_in_dim | solution.py:183
  64.2 0.1 copy-done
  64.3 7.9 %shard_map.78 = f32[32,36,256]{2,1,0:T(8,128)} custom-call(s32[4,32]{1,0:T(4,128)} %pad_add_fusion.table_ref, f32[64,40,128]{2,1,0:T(8,128)} %copy-done, f32[32,40,128]{2,1,0:T(8,128)} %broadcast_in_dim.2.drift_ref), custom_call_target="tpu_custom_call" | custom-call | tf_op jit(solution)/shard_map/pallas_call | solution.py:186
  72.1 2.8 %reshape.202 = f32[1152,2,128]{2,1,0:T(2,128)} reshape(f32[32,36,256]{2,1,0:T(8,128)} %shard_map.78) | data formatting | bytes 2359296 | tf_op jit(solution)/shard_map/reshape | solution.py:193
  (5 shorter events, 0.1 us)
Async XLA Ops:
  7.2 10.3 %collective-permute-start = (f32[64,128]{1,0:T(8,128)}, f32[64,128]{1,0:T(8,128)S(1)}, u32[]{:S(2)}, u32[]{:S(2)}) collective-permute-start(f32[64,128]{1,0:T(8,128)} %get-tuple-element.7), channel_id=1, source_target_pairs={{0,1},{1,2},{2,3},{3,4},{4,5},{5,6},{6,7},{7,8},{8,9},{9,10},{10,1... | collective-permute-start | bytes 98312 | tf_op jit(solution)/shard_map/ppermute | solution.py:198
  7.2 10.4 %collective-permute-start.1 = (f32[64,128]{1,0:T(8,128)}, f32[64,128]{1,0:T(8,128)S(1)}, u32[]{:S(2)}, u32[]{:S(2)}) collective-permute-start(f32[64,128]{1,0:T(8,128)} %get-tuple-element.8), channel_id=1, source_target_pairs={{1,0},{2,1},{3,2},{4,3},{5,4},{6,5},{7,6},{8,7},{9,8},{10,9},{11,1... | collective-permute-start | bytes 98312 | tf_op jit(solution)/shard_map/ppermute | solution.py:199
  17.5 0.6 copy-start.1
  18.1 0.6 copy-start.2
  23.4 10.3 %copy-start.3 = (s32[2,1152]{1,0:T(2,128)S(1)}, s32[2,1152]{1,0:T(2,128)}, u32[]{:S(2)}) copy-start(s32[2,1152]{1,0:T(2,128)} %param.11) | copy-start | bytes 27652
  23.4 10.7 %copy-start.4 = (f32[1152]{0:T(1024)S(1)}, f32[1152]{0:T(1024)}, u32[]{:S(2)}) copy-start(f32[1152]{0:T(1024)} %param.10) | copy-start | bytes 13828
  23.4 39.6 %all-to-all-start = ((f32[64,40,128]{2,1,0:T(8,128)}), f32[64,40,128]{2,1,0:T(8,128)S(1)}, u32[]{:S(2)}, u32[]{:S(2)}) async-start(f32[64,40,128]{2,1,0:T(8,128)} %shard_map.77), calls=%async_computation | async-start | bytes 2621440 | tf_op jit(solution)/shard_map/all_to_all | solution.py:313
  62.9 1.3 %copy-start = (f32[64,40,128]{2,1,0:T(8,128)}, f32[64,40,128]{2,1,0:T(8,128)S(1)}, u32[]{:S(2)}) copy-start(f32[64,40,128]{2,1,0:T(8,128)S(1)} %all-to-all-done.points_ref) | copy-start | bytes 3932164

commit v7 on v6

--- a/solution.py
+++ b/solution.py
@@ -123,7 +123,6 @@
 def settle_kernel(table_ref, points_ref, drift_ref, out_ref, shifted_ref, quartet_ref, source_ref):
     n_freq = drift_ref.shape[0]
     sub_rows = points_ref.shape[0] // n_freq
-    grid_cols = points_ref.shape[2]
     for r in range(sub_rows):
 
         def advect(f, carry):
@@ -143,7 +142,7 @@
             source_ref[f] = jnp.zeros_like(here)
             return carry
 
-        lax.fori_loop(0, n_freq, advect, 0)
+        lax.fori_loop(0, n_freq, advect, 0, unroll=True)
 
         def interact(f, carry):
             up_freq = table_ref[0, f]
@@ -162,15 +161,15 @@
             source_ref[down_freq] = source_ref[down_freq] + turn_rows(quartet, down_turn)
             return carry
 
-        lax.fori_loop(0, n_freq, interact, 0)
+        lax.fori_loop(0, n_freq, interact, 0, unroll=True)
 
         def finish(f, carry):
             source = source_ref[f] - 2.0 * quartet_ref[f]
             value = shifted_ref[f] + dia_coeff * source
-            out_ref[f, :, pl.ds(r * grid_cols, grid_cols)] = value[:ND]
+            out_ref[pl.ds(f * ND, ND), r, :] = value[:ND]
             return carry
 
-        lax.fori_loop(0, n_freq, finish, 0)
+        lax.fori_loop(0, n_freq, finish, 0, unroll=True)
 
 
 def settle(points, drift, partners):
@@ -185,12 +184,12 @@
     block = pltpu.VMEM((NF, PAD_DIR, grid_cols), jnp.float32)
     out = pl.pallas_call(
         settle_kernel,
-        out_shape=jax.ShapeDtypeStruct((NF, ND, sub_rows * grid_cols), jnp.float32),
+        out_shape=jax.ShapeDtypeStruct((NF * ND, sub_rows, grid_cols), jnp.float32),
         in_specs=[pl.BlockSpec(memory_space=pltpu.SMEM), vmem, vmem],
         out_specs=vmem,
         scratch_shapes=[block, block, block],
     )(table, points, rates)
-    return out.reshape(NF * ND, sub_rows, grid_cols)
+    return out
 
 
 def neighbours(edges_first, edges_last):

time: 75.3 us -> 71.8 us (0.954)
  local copies, waits for them, and re-layouts: 7.08 us -> 4.28 us
    reshape x1 -> x0, local copies, waits for them, and re-layouts: 2.77 us -> none  [settle(): return out.reshape(NF * ND, sub_rows, grid_cols)]
where the time goes in v7:
time: 71.8 us; the launch traced here: 71.4 us
  waiting for transfers between devices  29.3 us (41%)
  starting transfers between devices  18.8 us (26%)
  Pallas kernels  14.6 us (20%)
  other arithmetic  4.3 us (6%)
  local copies, waits for them, and re-layouts  4.28 us (6%)
    all_to_all x1, waiting for transfers between devices, shards(): lax.all_to_all(turned, 'spec', split_axis=0, concat_axis=0, tiled=True)  28.1 us
    all_to_all x1, starting transfers between devices, shards(): lax.all_to_all(turned, 'spec', split_axis=0, concat_axis=0, tiled=True)  10.3 us
    ppermute x1, starting transfers between devices, neighbours(): lax.ppermute(edges_first, 'tile', [((i + 1) % count, i) for i in range(co...  8.48 us
    pallas_call x1, Pallas kernels, settle(): pl.pallas_call(settle_kernel, out_shape=jax.ShapeDtypeStruct((NF * ND, su...  7.2 us
    pallas_call x1, Pallas kernels, propagate(): pl.pallas_call(propagate_kernel, out_shape=jax.ShapeDtypeStruct((grid_row...  4.64 us
    pallas_call x1, Pallas kernels, edges(): pl.pallas_call(edges_kernel, out_shape=(plane, plane), in_specs=[vmem] *...  2.75 us
    reduce_or x1, other arithmetic, sea_cells(): return jnp.any(matches, axis=1).astype(jnp.float32)  2.32 us
    unnamed x13, local copies, waits for them, and re-layouts  2.07 us
  transfers between devices with their start and end apart: 3, of which 3 were waited for; matrix products, arithmetic and copies ran while one was open for 2% of the time, Pallas kernels for 0%

profile of v7, /device:TPU:8, one launch (start us, length us, event | category | flops | bytes accessed | tf_op | source)
XLA Modules:
  0.0 71.4 jit_solution(17121604225199297054)
XLA Ops:
  0.0 0.8 %copy.16 = s32[32,1,192]{2,0,1:T(8,128)S(1)} copy(s32[32,1,192]{2,1,0:T(1,128)} %param.12) | data formatting | bytes 49152
  0.8 0.7 %iota_compare_fusion.1 = pred[32,192]{1,0:T(8,128)(4,1)S(1)} fusion(s32[32]{0:T(128)} %bitcast.27), kind=kLoop, calls=%fused_computation.4 | loop fusion | flops 6144 | bytes 6272 | tf_op jit(solution)/shard_map/lt | solution.py:37
  1.5 2.3 %fusion.1 = pred[32,256]{1,0:T(8,128)(4,1)S(1)} fusion(s32[32,192]{1,0:T(8,128)S(1)} %bitcast.24, pred[32,192]{1,0:T(8,128)(4,1)S(1)} %iota_compare_fusion.1), kind=kLoop, calls=%fused_computation.2 | loop fusion | flops 4710400 | bytes 38912 | tf_op jit(solution)/shard_map/reduce_or | solution.py:39
  3.8 0.6 reshape.199.mask_ref
  4.4 2.8 %shard_map.76 = (f32[64,128]{1,0:T(8,128)}, f32[64,128]{1,0:T(8,128)}) custom-call(f32[36,64,128]{2,1,0:T(8,128)} %spec_ref.3, f32[64,128]{1,0:T(8,128)} %reshape.199.mask_ref, f32[64,128]{1,0:T(8,128)} %depth_ref.3), custom_call_target="tpu_custom_call" | custom-call | tf_op jit(solution)/shard_map/pallas_call | solution.py:273
  7.2 0.0 collective-permute-start
  7.2 8.5 %collective-permute-start.1 = (f32[64,128]{1,0:T(8,128)}, f32[64,128]{1,0:T(8,128)S(1)}, u32[]{:S(2)}, u32[]{:S(2)}) collective-permute-start(f32[64,128]{1,0:T(8,128)} %get-tuple-element.8), channel_id=1, source_target_pairs={{1,0},{2,1},{3,2},{4,3},{5,4},{6,5},{7,6},{8,7},{9,8},{10,9},{11,1... | collective-permute-start | bytes 98312 | tf_op jit(solution)/shard_map/ppermute | solution.py:198
  15.8 0.6 pad_maximum_fusion.coef_ref
  16.4 1.1 %collective-permute-done.west_ref = f32[64,128]{1,0:T(8,128)S(1)} collective-permute-done((f32[64,128]{1,0:T(8,128)}, f32[64,128]{1,0:T(8,128)S(1)}, u32[]{:S(2)}, u32[]{:S(2)}) %collective-permute-start) | collective-permute-done | bytes 32800 | tf_op jit(solution)/shard_map/ppermute | solution.py:197
  17.5 0.0 copy-start.1
  17.5 0.1 collective-permute-done.1.east_ref
  17.6 0.5 copy-done.1
  18.1 0.0 copy-start.2
  18.1 0.6 copy-done.2
  18.7 4.6 %shard_map.77 = f32[64,40,128]{2,1,0:T(8,128)} custom-call(f32[2,36]{1,0:T(2,128)} %pad_maximum_fusion.coef_ref, f32[36,64,128]{2,1,0:T(8,128)} %spec_ref.3, f32[64,128]{1,0:T(8,128)} %reshape.199.mask_ref, f32[64,128]{1,0:T(8,128)} %depth_ref.3, f32[64,128]{1,0:T(8,128)} %turn_ref.1, f32[64,128]{1,0:T(8,128)} %copy-done.1, f32[64,128]{1,0:T(8,128)} %copy-done.2), custom_call_target="tpu_custom_call" | custom-call | tf_op jit(solution)/shard_map/pallas_call | solution.py:284
  23.4 0.0 copy-start.3
  23.4 0.0 copy-start.4
  23.4 10.3 %all-to-all-start = ((f32[64,40,128]{2,1,0:T(8,128)}), f32[64,40,128]{2,1,0:T(8,128)S(1)}, u32[]{:S(2)}, u32[]{:S(2)}) async-start(f32[64,40,128]{2,1,0:T(8,128)} %shard_map.77), calls=%async_computation | async-start | bytes 2621440 | tf_op jit(solution)/shard_map/all_to_all | solution.py:312
  33.7 0.0 copy-done.3
  33.7 0.1 reshape_squeeze.6
  33.8 0.1 copy.13
  33.9 0.1 reshape_squeeze.7
  34.0 0.1 copy.14
  34.1 0.0 copy-done.4
  34.1 0.1 reshape.198
  34.2 0.6 pad_add_fusion.table_ref
  34.8 28.1 %all-to-all-done.points_ref = f32[64,40,128]{2,1,0:T(8,128)S(1)} async-done(((f32[64,40,128]{2,1,0:T(8,128)}), f32[64,40,128]{2,1,0:T(8,128)S(1)}, u32[]{:S(2)}, u32[]{:S(2)}) %all-to-all-start) | async-done | bytes 1310752 | tf_op jit(solution)/shard_map/all_to_all | solution.py:312
  62.9 0.0 copy-start
  62.9 1.3 %broadcast_in_dim.2.drift_ref = f32[32,40,128]{2,1,0:T(8,128)} broadcast(f32[32,40]{1,0:T(8,128)S(1)} %pad.4), dimensions={0,1} | broadcast | bytes 660480 | tf_op jit(solution)/shard_map/broadcast_in_dim | solution.py:182
  64.2 0.0 copy-done
  64.2 7.2 %shard_map.78 = f32[1152,2,128]{2,1,0:T(2,128)} custom-call(s32[4,32]{1,0:T(4,128)} %pad_add_fusion.table_ref, f32[64,40,128]{2,1,0:T(8,128)} %copy-done, f32[32,40,128]{2,1,0:T(8,128)} %broadcast_in_dim.2.drift_ref), custom_call_target="tpu_custom_call" | custom-call | tf_op jit(solution)/shard_map/pallas_call | solution.py:185
  (5 shorter events, 0.1 us)
Async XLA Ops:
  7.2 10.3 %collective-permute-start = (f32[64,128]{1,0:T(8,128)}, f32[64,128]{1,0:T(8,128)S(1)}, u32[]{:S(2)}, u32[]{:S(2)}) collective-permute-start(f32[64,128]{1,0:T(8,128)} %get-tuple-element.7), channel_id=1, source_target_pairs={{0,1},{1,2},{2,3},{3,4},{4,5},{5,6},{6,7},{7,8},{8,9},{9,10},{10,1... | collective-permute-start | bytes 98312 | tf_op jit(solution)/shard_map/ppermute | solution.py:197
  7.2 10.4 %collective-permute-start.1 = (f32[64,128]{1,0:T(8,128)}, f32[64,128]{1,0:T(8,128)S(1)}, u32[]{:S(2)}, u32[]{:S(2)}) collective-permute-start(f32[64,128]{1,0:T(8,128)} %get-tuple-element.8), channel_id=1, source_target_pairs={{1,0},{2,1},{3,2},{4,3},{5,4},{6,5},{7,6},{8,7},{9,8},{10,9},{11,1... | collective-permute-start | bytes 98312 | tf_op jit(solution)/shard_map/ppermute | solution.py:198
  17.5 0.6 copy-start.1
  18.1 0.6 copy-start.2
  23.4 10.3 %copy-start.3 = (s32[2,1152]{1,0:T(2,128)S(1)}, s32[2,1152]{1,0:T(2,128)}, u32[]{:S(2)}) copy-start(s32[2,1152]{1,0:T(2,128)} %param.11) | copy-start | bytes 27652
  23.4 10.7 %copy-start.4 = (f32[1152]{0:T(1024)S(1)}, f32[1152]{0:T(1024)}, u32[]{:S(2)}) copy-start(f32[1152]{0:T(1024)} %param.10) | copy-start | bytes 13828
  23.4 39.6 %all-to-all-start = ((f32[64,40,128]{2,1,0:T(8,128)}), f32[64,40,128]{2,1,0:T(8,128)S(1)}, u32[]{:S(2)}, u32[]{:S(2)}) async-start(f32[64,40,128]{2,1,0:T(8,128)} %shard_map.77), calls=%async_computation | async-start | bytes 2621440 | tf_op jit(solution)/shard_map/all_to_all | solution.py:312
  62.9 1.3 %copy-start = (f32[64,40,128]{2,1,0:T(8,128)}, f32[64,40,128]{2,1,0:T(8,128)S(1)}, u32[]{:S(2)}) copy-start(f32[64,40,128]{2,1,0:T(8,128)S(1)} %all-to-all-done.points_ref) | copy-start | bytes 3932164

commit v8 on v7

--- a/solution.py
+++ b/solution.py
@@ -29,6 +29,15 @@
             axis=dim,
         )
     return cells
+
+
+def edge_cells(sea_list, sea_total, sub_rows, grid_cols):
+    slot_rank = jnp.arange(sea_list.shape[1], dtype=jnp.int32)
+    is_live = slot_rank[None, :] < sea_total[:, None]
+    rows = jnp.arange(sub_rows, dtype=jnp.int32)[:, None] * grid_cols
+    cells = rows + jnp.array([0, grid_cols - 1], dtype=jnp.int32)[None, :]
+    matches = (sea_list[:, None, None, :] == cells[None, :, :, None]) & is_live[:, None, None, :]
+    return jnp.any(matches, axis=3).astype(jnp.float32).reshape(-1, 2)
 
 
 def sea_cells(sea_list, sea_total, per_block):
@@ -254,20 +263,20 @@
 
 def edges_kernel(spec_ref, mask_ref, depth_ref, first_ref, last_ref):
     channels, grid_rows, grid_cols = spec_ref.shape
-    mask = mask_ref[...]
+    edge_mask = mask_ref[...]
     depth = depth_ref[...]
     lane = lax.broadcasted_iota(jnp.int32, (grid_rows, grid_cols), 1)
     first = jnp.where(lane == channels, depth[:, :1], 0.0)
     last = jnp.where(lane == channels, depth[:, grid_cols - 1 :], 0.0)
     for d in range(channels):
-        energy = spec_ref[d] * mask
-        first = jnp.where(lane == d, energy[:, :1], first)
-        last = jnp.where(lane == d, energy[:, grid_cols - 1 :], last)
+        plane = spec_ref[d]
+        first = jnp.where(lane == d, plane[:, :1] * edge_mask[:, :1], first)
+        last = jnp.where(lane == d, plane[:, grid_cols - 1 :] * edge_mask[:, 1:], last)
     first_ref[...] = first
     last_ref[...] = last
 
 
-def edges(spectrum, sea_mask, depth):
+def edges(spectrum, edge_mask, depth):
     vmem = pl.BlockSpec(memory_space=pltpu.VMEM)
     plane = jax.ShapeDtypeStruct(depth.shape, jnp.float32)
     return pl.pallas_call(
@@ -275,7 +284,7 @@
         out_shape=(plane, plane),
         in_specs=[vmem] * 3,
         out_specs=(vmem, vmem),
-    )(spectrum, sea_mask, depth)
+    )(spectrum, edge_mask, depth)
 
 
 def propagate(spectrum, depth, sea_mask, turning, from_west, from_east, coef):
@@ -297,7 +306,8 @@
     per_block = sub_rows * grid_cols
     sea_list = sea_slots[:, 0, :]
     sea_mask = sea_cells(sea_list, sea_counts[:, 0], per_block).reshape(grid_rows, grid_cols)
-    edges_first, edges_last = edges(spectrum, sea_mask, depth_speed)
+    edge_mask = edge_cells(sea_list, sea_counts[:, 0], sub_rows, grid_cols)
+    edges_first, edges_last = edges(spectrum, edge_mask, depth_speed)
     from_west, from_east = neighbours(edges_first, edges_last)
     local_freq = channels // ND
     freq_ids = (

time: 71.8 us -> 71 us (0.989)
  the two profiles are of different devices: /device:TPU:8 before, /device:TPU:193 now
where the time goes in v8:
time: 71 us; the launch traced here: 70.6 us
  waiting for transfers between devices  33.1 us (47%)
  Pallas kernels  14.6 us (21%)
  starting transfers between devices  13.7 us (19%)
  other arithmetic  4.58 us (6%)
  local copies, waits for them, and re-layouts  4.51 us (6%)
    all_to_all x1, waiting for transfers between devices, shards(): lax.all_to_all(turned, 'spec', split_axis=0, concat_axis=0, tiled=True)  31.9 us
    all_to_all x1, starting transfers between devices, shards(): lax.all_to_all(turned, 'spec', split_axis=0, concat_axis=0, tiled=True)  9.8 us
    pallas_call x1, Pallas kernels, settle(): pl.pallas_call(settle_kernel, out_shape=jax.ShapeDtypeStruct((NF * ND, su...  7.21 us
    pallas_call x1, Pallas kernels, propagate(): pl.pallas_call(propagate_kernel, out_shape=jax.ShapeDtypeStruct((grid_row...  4.63 us
    ppermute x1, starting transfers between devices, neighbours(): lax.ppermute(edges_last, 'tile', [(i, (i + 1) % count) for i in range(cou...  3.86 us
    pallas_call x1, Pallas kernels, edges(): pl.pallas_call(edges_kernel, out_shape=(plane, plane), in_specs=[vmem] *...  2.8 us
    reduce_or x1, other arithmetic, sea_cells(): return jnp.any(matches, axis=1).astype(jnp.float32)  2.31 us
    unnamed x13, local copies, waits for them, and re-layouts  1.54 us
  transfers between devices with their start and end apart: 3, of which 2 were waited for; matrix products, arithmetic and copies ran while one was open for 7% of the time, Pallas kernels for 0%

profile of v8, /device:TPU:193, one launch (start us, length us, event | category | flops | bytes accessed | tf_op | source)
XLA Modules:
  0.0 70.6 jit_solution(4508335788339653780)
XLA Ops:
  0.0 0.8 %copy.25 = s32[32,1,192]{2,0,1:T(8,128)S(1)} copy(s32[32,1,192]{2,1,0:T(1,128)} %param.13) | data formatting | bytes 49152
  0.8 0.7 %iota_compare_fusion.1 = pred[32,192]{1,0:T(8,128)(4,1)S(1)} fusion(s32[32]{0:T(128)} %bitcast.30), kind=kLoop, calls=%fused_computation.5 | loop fusion | flops 6144 | bytes 6272 | tf_op jit(solution)/shard_map/lt | solution.py:46
  1.5 0.1 broadcast_add_fusion
  1.6 0.2 and_reduce_fusion
  1.8 0.7 %copy.19 = f32[32,2,2]{2,1,0:T(2,128)} copy(f32[32,2,2]{0,2,1:T(2,128)S(1)} %convert_element_type.26) | data formatting | bytes 1024 | tf_op jit(solution)/shard_map/convert_element_type | solution.py:40
  2.5 2.8 %shard_map.85 = (f32[64,128]{1,0:T(8,128)}, f32[64,128]{1,0:T(8,128)}) custom-call(f32[36,64,128]{2,1,0:T(8,128)} %spec_ref.3, f32[64,2]{1,0:T(8,128)} %bitcast.27, f32[64,128]{1,0:T(8,128)} %depth_ref.3), custom_call_target="tpu_custom_call" | custom-call | tf_op jit(solution)/shard_map/pallas_call | solution.py:282
  5.3 3.9 %collective-permute-start = (f32[64,128]{1,0:T(8,128)}, f32[64,128]{1,0:T(8,128)S(1)}, u32[]{:S(2)}, u32[]{:S(2)}) collective-permute-start(f32[64,128]{1,0:T(8,128)} %get-tuple-element.7), channel_id=1, source_target_pairs={{0,1},{1,2},{2,3},{3,4},{4,5},{5,6},{6,7},{7,8},{8,9},{9,10},{10,1... | collective-permute-start | bytes 98312 | tf_op jit(solution)/shard_map/ppermute | solution.py:206
  9.2 0.0 collective-permute-start.1
  9.2 2.3 %fusion.1 = pred[32,256]{1,0:T(8,128)(4,1)S(1)} fusion(s32[32,192]{1,0:T(8,128)S(1)} %bitcast.26, pred[32,192]{1,0:T(8,128)(4,1)S(1)} %iota_compare_fusion.1), kind=kLoop, calls=%fused_computation.2 | loop fusion | flops 4710400 | bytes 38912 | tf_op jit(solution)/shard_map/reduce_or | solution.py:48
  11.6 0.6 pad_maximum_fusion.coef_ref
  12.2 0.6 reshape.257.mask_ref
  12.8 0.0 collective-permute-done.west_ref
  12.8 0.0 copy-start.1
  12.8 1.1 %collective-permute-done.1.east_ref = f32[64,128]{1,0:T(8,128)S(1)} collective-permute-done((f32[64,128]{1,0:T(8,128)}, f32[64,128]{1,0:T(8,128)S(1)}, u32[]{:S(2)}, u32[]{:S(2)}) %collective-permute-start.1) | collective-permute-done | bytes 32800 | tf_op jit(solution)/shard_map/ppermute | solution.py:207
  13.9 0.0 copy-done.1
  13.9 0.0 copy-start.2
  13.9 0.6 copy-done.2
  14.6 4.6 %shard_map.86 = f32[64,40,128]{2,1,0:T(8,128)} custom-call(f32[2,36]{1,0:T(2,128)} %pad_maximum_fusion.coef_ref, f32[36,64,128]{2,1,0:T(8,128)} %spec_ref.3, f32[64,128]{1,0:T(8,128)} %reshape.257.mask_ref, f32[64,128]{1,0:T(8,128)} %depth_ref.3, f32[64,128]{1,0:T(8,128)} %turn_ref.1, f32[64,128]{1,0:T(8,128)} %copy-done.1, f32[64,128]{1,0:T(8,128)} %copy-done.2), custom_call_target="tpu_custom_call" | custom-call | tf_op jit(solution)/shard_map/pallas_call | solution.py:293
  19.2 0.0 copy-start.3
  19.2 0.0 copy-start.4
  19.2 9.8 %all-to-all-start = ((f32[64,40,128]{2,1,0:T(8,128)}), f32[64,40,128]{2,1,0:T(8,128)S(1)}, u32[]{:S(2)}, u32[]{:S(2)}) async-start(f32[64,40,128]{2,1,0:T(8,128)} %shard_map.86), calls=%async_computation | async-start | bytes 2621440 | tf_op jit(solution)/shard_map/all_to_all | solution.py:322
  29.0 0.0 copy-done.3
  29.0 0.1 reshape_squeeze.6
  29.1 0.1 copy.22
  29.2 0.1 reshape_squeeze.7
  29.3 0.1 copy.23
  29.4 0.0 copy-done.4
  29.4 0.1 reshape.256
  29.6 0.6 pad_add_fusion.table_ref
  30.1 31.9 %all-to-all-done.points_ref = f32[64,40,128]{2,1,0:T(8,128)S(1)} async-done(((f32[64,40,128]{2,1,0:T(8,128)}), f32[64,40,128]{2,1,0:T(8,128)S(1)}, u32[]{:S(2)}, u32[]{:S(2)}) %all-to-all-start) | async-done | bytes 1310752 | tf_op jit(solution)/shard_map/all_to_all | solution.py:322
  62.1 0.0 copy-start
  62.1 1.3 %broadcast_in_dim.2.drift_ref = f32[32,40,128]{2,1,0:T(8,128)} broadcast(f32[32,40]{1,0:T(8,128)S(1)} %pad.4), dimensions={0,1} | broadcast | bytes 660480 | tf_op jit(solution)/shard_map/broadcast_in_dim | solution.py:191
  63.4 0.0 copy-done
  63.4 7.2 %shard_map.87 = f32[1152,2,128]{2,1,0:T(2,128)} custom-call(s32[4,32]{1,0:T(4,128)} %pad_add_fusion.table_ref, f32[64,40,128]{2,1,0:T(8,128)} %copy-done, f32[32,40,128]{2,1,0:T(8,128)} %broadcast_in_dim.2.drift_ref), custom_call_target="tpu_custom_call" | custom-call | tf_op jit(solution)/shard_map/pallas_call | solution.py:194
  (7 shorter events, 0.1 us)
Async XLA Ops:
  5.3 7.5 %collective-permute-start = (f32[64,128]{1,0:T(8,128)}, f32[64,128]{1,0:T(8,128)S(1)}, u32[]{:S(2)}, u32[]{:S(2)}) collective-permute-start(f32[64,128]{1,0:T(8,128)} %get-tuple-element.7), channel_id=1, source_target_pairs={{0,1},{1,2},{2,3},{3,4},{4,5},{5,6},{6,7},{7,8},{8,9},{9,10},{10,1... | collective-permute-start | bytes 98312 | tf_op jit(solution)/shard_map/ppermute | solution.py:206
  9.2 4.8 %collective-permute-start.1 = (f32[64,128]{1,0:T(8,128)}, f32[64,128]{1,0:T(8,128)S(1)}, u32[]{:S(2)}, u32[]{:S(2)}) collective-permute-start(f32[64,128]{1,0:T(8,128)} %get-tuple-element.8), channel_id=1, source_target_pairs={{1,0},{2,1},{3,2},{4,3},{5,4},{6,5},{7,6},{8,7},{9,8},{10,9},{11,1... | collective-permute-start | bytes 98312 | tf_op jit(solution)/shard_map/ppermute | solution.py:207
  12.8 1.1 %copy-start.1 = (f32[64,128]{1,0:T(8,128)}, f32[64,128]{1,0:T(8,128)S(1)}, u32[]{:S(2)}) copy-start(f32[64,128]{1,0:T(8,128)S(1)} %collective-permute-done.west_ref) | copy-start | bytes 98308
  13.9 0.6 copy-start.2
  19.2 9.8 %copy-start.3 = (s32[2,1152]{1,0:T(2,128)S(1)}, s32[2,1152]{1,0:T(2,128)}, u32[]{:S(2)}) copy-start(s32[2,1152]{1,0:T(2,128)} %param.12) | copy-start | bytes 27652
  19.2 10.2 %copy-start.4 = (f32[1152]{0:T(1024)S(1)}, f32[1152]{0:T(1024)}, u32[]{:S(2)}) copy-start(f32[1152]{0:T(1024)} %param.11) | copy-start | bytes 13828
  19.2 42.9 %all-to-all-start = ((f32[64,40,128]{2,1,0:T(8,128)}), f32[64,40,128]{2,1,0:T(8,128)S(1)}, u32[]{:S(2)}, u32[]{:S(2)}) async-start(f32[64,40,128]{2,1,0:T(8,128)} %shard_map.86), calls=%async_computation | async-start | bytes 2621440 | tf_op jit(solution)/shard_map/all_to_all | solution.py:322
  62.1 1.3 %copy-start = (f32[64,40,128]{2,1,0:T(8,128)}, f32[64,40,128]{2,1,0:T(8,128)S(1)}, u32[]{:S(2)}) copy-start(f32[64,40,128]{2,1,0:T(8,128)S(1)} %all-to-all-done.points_ref) | copy-start | bytes 3932164

commit v9 on v8

--- a/solution.py
+++ b/solution.py
@@ -129,9 +129,24 @@
     return jnp.where(d + k < ND, ahead, wrapped)
 
 
-def settle_kernel(table_ref, points_ref, drift_ref, out_ref, shifted_ref, quartet_ref, source_ref):
+def settle_kernel(
+    table_ref, blocks_ref, drift_ref, out_ref, points_ref, shifted_ref, quartet_ref, source_ref
+):
     n_freq = drift_ref.shape[0]
-    sub_rows = points_ref.shape[0] // n_freq
+    sub_rows = blocks_ref.shape[1] // ND
+    for r in range(sub_rows):
+        start = r * ND // 8 * 8
+        offset = r * ND - start
+
+        def align(f, carry):
+            block = blocks_ref[f, pl.ds(start, PAD_DIR), :]
+            if offset:
+                block = pltpu.roll(block, PAD_DIR - offset, 0)
+            points_ref[f * sub_rows + r] = block
+            return carry
+
+        lax.fori_loop(0, n_freq, align, 0, unroll=True)
+
     for r in range(sub_rows):
 
         def advect(f, carry):
@@ -182,8 +197,8 @@
 
 
 def settle(points, drift, partners):
-    n_rows, _, grid_cols = points.shape
-    sub_rows = n_rows // NF
+    _, block_rows, grid_cols = points.shape
+    sub_rows = block_rows // ND
     up_ids = partners[0].reshape(NF, ND)[:, 0]
     down_ids = partners[1].reshape(NF, ND)[:, 0]
     table = jnp.stack([up_ids // ND, down_ids // ND, up_ids % ND, ND - down_ids % ND])
@@ -196,7 +211,7 @@
         out_shape=jax.ShapeDtypeStruct((NF * ND, sub_rows, grid_cols), jnp.float32),
         in_specs=[pl.BlockSpec(memory_space=pltpu.SMEM), vmem, vmem],
         out_specs=vmem,
-        scratch_shapes=[block, block, block],
+        scratch_shapes=[pltpu.VMEM((NF * sub_rows, PAD_DIR, grid_cols), jnp.float32), block, block, block],
     )(table, points, rates)
     return out
 
@@ -208,7 +223,9 @@
     return from_west, from_east
 
 
-def propagate_kernel(coef_ref, spec_ref, mask_ref, depth_ref, turn_ref, west_ref, east_ref, out_ref, spaced_ref):
+def propagate_kernel(
+    coef_ref, spec_ref, mask_ref, depth_ref, turn_ref, west_ref, east_ref, out_ref, spaced_ref, plane_ref
+):
     channels, grid_rows, grid_cols = spec_ref.shape
     mask = mask_ref[...]
     depth = depth_ref[...]
@@ -246,19 +263,22 @@
             + from_north
         )
         spaced_ref[d] = updated * mask
-    out_ref[:, channels:, :] = jnp.zeros((grid_rows, PAD_DIR - channels, grid_cols), jnp.float32)
+    blocks = out_ref.shape[0]
+    sub_rows = out_ref.shape[1] // channels
     turning = turn_ref[...]
     turn_plus = jnp.maximum(turning, 0.0)
     behind = jnp.maximum(-turning, 0.0)
     turn_abs = jnp.abs(turning)
     for d in range(channels):
         here = spaced_ref[d]
-        out_ref[:, d, :] = (
+        plane_ref[...] = (
             here
             - turn_abs * here
             + turn_plus * spaced_ref[(d - 1) % channels]
             + behind * spaced_ref[(d + 1) % channels]
         )
+        for r in range(sub_rows):
+            out_ref[:, r * channels + d, :] = plane_ref[pl.ds(r, blocks, stride=sub_rows), :]
 
 
 def edges_kernel(spec_ref, mask_ref, depth_ref, first_ref, last_ref):
@@ -287,15 +307,18 @@
     )(spectrum, edge_mask, depth)
 
 
-def propagate(spectrum, depth, sea_mask, turning, from_west, from_east, coef):
+def propagate(spectrum, depth, sea_mask, turning, from_west, from_east, coef, blocks):
     channels, grid_rows, grid_cols = spectrum.shape
     vmem = pl.BlockSpec(memory_space=pltpu.VMEM)
     return pl.pallas_call(
         propagate_kernel,
-        out_shape=jax.ShapeDtypeStruct((grid_rows, PAD_DIR, grid_cols), jnp.float32),
+        out_shape=jax.ShapeDtypeStruct((blocks, grid_rows // blocks * channels, grid_cols), jnp.float32),
         in_specs=[pl.BlockSpec(memory_space=pltpu.SMEM)] + [vmem] * 6,
         out_specs=vmem,
-        scratch_shapes=[pltpu.VMEM(spectrum.shape, jnp.float32)],
+        scratch_shapes=[
+            pltpu.VMEM(spectrum.shape, jnp.float32),
+            pltpu.VMEM((grid_rows, grid_cols), jnp.float32),
+        ],
     )(coef, spectrum, sea_mask, depth, turning, from_west, from_east)
 
 
@@ -318,7 +341,9 @@
     cosines = jnp.tile(jnp.cos(angles), local_freq)
     sine_part = jnp.tile(jnp.sin(angles), local_freq)
     coef = jnp.stack([speeds * cosines, speeds * sine_part])
-    turned = propagate(spectrum, depth_speed, sea_mask, turning, from_west, from_east, coef)
+    turned = propagate(
+        spectrum, depth_speed, sea_mask, turning, from_west, from_east, coef, n_spec
+    )
     points = lax.all_to_all(turned, "spec", split_axis=0, concat_axis=0, tiled=True)
     return settle(points, drift, partners)
 

time: 71 us -> 68.7 us (0.968)
  waiting for transfers between devices: 33.1 us -> 30.4 us
    all_to_all x1, waiting for transfers between devices: 31.9 us -> 29.3 us  [shards(): lax.all_to_all(turned, 'spec', split_axis=0, concat_axis=0, tiled=True)]
where the time goes in v9:
time: 68.7 us; the launch traced here: 68.2 us
  waiting for transfers between devices  30.4 us (44%)
  Pallas kernels  15 us (22%)
  starting transfers between devices  13.7 us (20%)
  other arithmetic  4.58 us (7%)
  local copies, waits for them, and re-layouts  4.46 us (6%)
    all_to_all x1, waiting for transfers between devices, shards(): lax.all_to_all(turned, 'spec', split_axis=0, concat_axis=0, tiled=True)  29.3 us
    all_to_all x1, starting transfers between devices, shards(): lax.all_to_all(turned, 'spec', split_axis=0, concat_axis=0, tiled=True)  9.8 us
    pallas_call x1, Pallas kernels, settle(): pl.pallas_call(settle_kernel, out_shape=jax.ShapeDtypeStruct((NF * ND, su...  7.24 us
    pallas_call x1, Pallas kernels, propagate(): pl.pallas_call(propagate_kernel, out_shape=jax.ShapeDtypeStruct((blocks,...  5 us
    ppermute x1, starting transfers between devices, neighbours(): lax.ppermute(edges_last, 'tile', [(i, (i + 1) % count) for i in range(cou...  3.86 us
    pallas_call x1, Pallas kernels, edges(): pl.pallas_call(edges_kernel, out_shape=(plane, plane), in_specs=[vmem] *...  2.8 us
    reduce_or x1, other arithmetic, sea_cells(): return jnp.any(matches, axis=1).astype(jnp.float32)  2.31 us
    unnamed x13, local copies, waits for them, and re-layouts  1.54 us
  transfers between devices with their start and end apart: 3, of which 2 were waited for; matrix products, arithmetic and copies ran while one was open for 7% of the time, Pallas kernels for 0%

profile of v9, /device:TPU:193, one launch (start us, length us, event | category | flops | bytes accessed | tf_op | source)
XLA Modules:
  0.0 68.2 jit_solution(3788456350648010785)
XLA Ops:
  0.0 0.8 %copy.25 = s32[32,1,192]{2,0,1:T(8,128)S(1)} copy(s32[32,1,192]{2,1,0:T(1,128)} %param.13) | data formatting | bytes 49152
  0.8 0.7 %iota_compare_fusion.1 = pred[32,192]{1,0:T(8,128)(4,1)S(1)} fusion(s32[32]{0:T(128)} %bitcast.30), kind=kLoop, calls=%fused_computation.5 | loop fusion | flops 6144 | bytes 6272 | tf_op jit(solution)/shard_map/lt | solution.py:46
  1.5 0.1 broadcast_add_fusion
  1.6 0.2 and_reduce_fusion
  1.8 0.7 %copy.19 = f32[32,2,2]{2,1,0:T(2,128)} copy(f32[32,2,2]{0,2,1:T(2,128)S(1)} %convert_element_type.26) | data formatting | bytes 1024 | tf_op jit(solution)/shard_map/convert_element_type | solution.py:40
  2.5 2.8 %shard_map.85 = (f32[64,128]{1,0:T(8,128)}, f32[64,128]{1,0:T(8,128)}) custom-call(f32[36,64,128]{2,1,0:T(8,128)} %spec_ref.3, f32[64,2]{1,0:T(8,128)} %bitcast.27, f32[64,128]{1,0:T(8,128)} %depth_ref.3), custom_call_target="tpu_custom_call" | custom-call | tf_op jit(solution)/shard_map/pallas_call | solution.py:302
  5.3 3.9 %collective-permute-start = (f32[64,128]{1,0:T(8,128)}, f32[64,128]{1,0:T(8,128)S(1)}, u32[]{:S(2)}, u32[]{:S(2)}) collective-permute-start(f32[64,128]{1,0:T(8,128)} %get-tuple-element.7), channel_id=1, source_target_pairs={{0,1},{1,2},{2,3},{3,4},{4,5},{5,6},{6,7},{7,8},{8,9},{9,10},{10,1... | collective-permute-start | bytes 98312 | tf_op jit(solution)/shard_map/ppermute | solution.py:221
  9.2 0.0 collective-permute-start.1
  9.2 2.3 %fusion.1 = pred[32,256]{1,0:T(8,128)(4,1)S(1)} fusion(s32[32,192]{1,0:T(8,128)S(1)} %bitcast.26, pred[32,192]{1,0:T(8,128)(4,1)S(1)} %iota_compare_fusion.1), kind=kLoop, calls=%fused_computation.2 | loop fusion | flops 4710400 | bytes 38912 | tf_op jit(solution)/shard_map/reduce_or | solution.py:48
  11.6 0.6 pad_maximum_fusion.coef_ref
  12.2 0.6 reshape.257.mask_ref
  12.8 0.0 collective-permute-done.west_ref
  12.8 0.0 copy-start.1
  12.8 1.1 %collective-permute-done.1.east_ref = f32[64,128]{1,0:T(8,128)S(1)} collective-permute-done((f32[64,128]{1,0:T(8,128)}, f32[64,128]{1,0:T(8,128)S(1)}, u32[]{:S(2)}, u32[]{:S(2)}) %collective-permute-start.1) | collective-permute-done | bytes 32800 | tf_op jit(solution)/shard_map/ppermute | solution.py:222
  13.9 0.0 copy-done.1
  13.9 0.0 copy-start.2
  13.9 0.6 copy-done.2
  14.5 5.0 %shard_map.86 = f32[32,72,128]{2,1,0:T(8,128)} custom-call(f32[2,36]{1,0:T(2,128)} %pad_maximum_fusion.coef_ref, f32[36,64,128]{2,1,0:T(8,128)} %spec_ref.3, f32[64,128]{1,0:T(8,128)} %reshape.257.mask_ref, f32[64,128]{1,0:T(8,128)} %depth_ref.3, f32[64,128]{1,0:T(8,128)} %turn_ref.1, f32[64,128]{1,0:T(8,128)} %copy-done.1, f32[64,128]{1,0:T(8,128)} %copy-done.2), custom_call_target="tpu_custom_call" | custom-call | tf_op jit(solution)/shard_map/pallas_call | solution.py:313
  19.5 0.0 copy-start.3
  19.5 0.0 copy-start.4
  19.6 9.8 %all-to-all-start = ((f32[32,72,128]{2,1,0:T(8,128)}), f32[32,72,128]{2,1,0:T(8,128)S(1)}, u32[]{:S(2)}, u32[]{:S(2)}) async-start(f32[32,72,128]{2,1,0:T(8,128)} %shard_map.86), calls=%async_computation | async-start | bytes 2359296 | tf_op jit(solution)/shard_map/all_to_all | solution.py:347
  29.4 0.0 copy-done.3
  29.4 0.1 reshape_squeeze.6
  29.5 0.1 copy.22
  29.6 0.1 reshape_squeeze.7
  29.7 0.1 copy.23
  29.8 0.0 copy-done.4
  29.8 0.1 reshape.256
  29.9 0.6 pad_add_fusion.table_ref
  30.5 29.3 %all-to-all-done.blocks_ref = f32[32,72,128]{2,1,0:T(8,128)S(1)} async-done(((f32[32,72,128]{2,1,0:T(8,128)}), f32[32,72,128]{2,1,0:T(8,128)S(1)}, u32[]{:S(2)}, u32[]{:S(2)}) %all-to-all-start) | async-done | bytes 1179680 | tf_op jit(solution)/shard_map/all_to_all | solution.py:347
  59.8 0.0 copy-start
  59.8 1.3 %broadcast_in_dim.2.drift_ref = f32[32,40,128]{2,1,0:T(8,128)} broadcast(f32[32,40]{1,0:T(8,128)S(1)} %pad.4), dimensions={0,1} | broadcast | bytes 660480 | tf_op jit(solution)/shard_map/broadcast_in_dim | solution.py:206
  61.0 0.0 copy-done
  61.0 7.2 %shard_map.87 = f32[1152,2,128]{2,1,0:T(2,128)} custom-call(s32[4,32]{1,0:T(4,128)} %pad_add_fusion.table_ref, f32[32,72,128]{2,1,0:T(8,128)} %copy-done, f32[32,40,128]{2,1,0:T(8,128)} %broadcast_in_dim.2.drift_ref), custom_call_target="tpu_custom_call" | custom-call | tf_op jit(solution)/shard_map/pallas_call | solution.py:209
  (7 shorter events, 0.1 us)
Async XLA Ops:
  5.3 7.5 %collective-permute-start = (f32[64,128]{1,0:T(8,128)}, f32[64,128]{1,0:T(8,128)S(1)}, u32[]{:S(2)}, u32[]{:S(2)}) collective-permute-start(f32[64,128]{1,0:T(8,128)} %get-tuple-element.7), channel_id=1, source_target_pairs={{0,1},{1,2},{2,3},{3,4},{4,5},{5,6},{6,7},{7,8},{8,9},{9,10},{10,1... | collective-permute-start | bytes 98312 | tf_op jit(solution)/shard_map/ppermute | solution.py:221
  9.2 4.8 %collective-permute-start.1 = (f32[64,128]{1,0:T(8,128)}, f32[64,128]{1,0:T(8,128)S(1)}, u32[]{:S(2)}, u32[]{:S(2)}) collective-permute-start(f32[64,128]{1,0:T(8,128)} %get-tuple-element.8), channel_id=1, source_target_pairs={{1,0},{2,1},{3,2},{4,3},{5,4},{6,5},{7,6},{8,7},{9,8},{10,9},{11,1... | collective-permute-start | bytes 98312 | tf_op jit(solution)/shard_map/ppermute | solution.py:222
  12.8 1.1 %copy-start.1 = (f32[64,128]{1,0:T(8,128)}, f32[64,128]{1,0:T(8,128)S(1)}, u32[]{:S(2)}) copy-start(f32[64,128]{1,0:T(8,128)S(1)} %collective-permute-done.west_ref) | copy-start | bytes 98308
  13.9 0.6 copy-start.2
  19.5 9.8 %copy-start.3 = (s32[2,1152]{1,0:T(2,128)S(1)}, s32[2,1152]{1,0:T(2,128)}, u32[]{:S(2)}) copy-start(s32[2,1152]{1,0:T(2,128)} %param.12) | copy-start | bytes 27652
  19.5 10.2 %copy-start.4 = (f32[1152]{0:T(1024)S(1)}, f32[1152]{0:T(1024)}, u32[]{:S(2)}) copy-start(f32[1152]{0:T(1024)} %param.11) | copy-start | bytes 13828
  19.6 40.2 %all-to-all-start = ((f32[32,72,128]{2,1,0:T(8,128)}), f32[32,72,128]{2,1,0:T(8,128)S(1)}, u32[]{:S(2)}, u32[]{:S(2)}) async-start(f32[32,72,128]{2,1,0:T(8,128)} %shard_map.86), calls=%async_computation | async-start | bytes 2359296 | tf_op jit(solution)/shard_map/all_to_all | solution.py:347
  59.8 1.3 %copy-start = (f32[32,72,128]{2,1,0:T(8,128)}, f32[32,72,128]{2,1,0:T(8,128)S(1)}, u32[]{:S(2)}) copy-start(f32[32,72,128]{2,1,0:T(8,128)S(1)} %all-to-all-done.blocks_ref) | copy-start | bytes 3538948

commit v10 on v9

--- a/solution.py
+++ b/solution.py
@@ -132,7 +132,7 @@
 def settle_kernel(
     table_ref, blocks_ref, drift_ref, out_ref, points_ref, shifted_ref, quartet_ref, source_ref
 ):
-    n_freq = drift_ref.shape[0]
+    n_freq = blocks_ref.shape[0]
     sub_rows = blocks_ref.shape[1] // ND
     for r in range(sub_rows):
         start = r * ND // 8 * 8
@@ -149,24 +149,18 @@
 
     for r in range(sub_rows):
 
-        def advect(f, carry):
+        for f in range(n_freq):
             here = points_ref[f * sub_rows + r]
-            rate = drift_ref[f]
-            below = jnp.maximum(f - 1, 0)
-            above = jnp.minimum(f + 1, n_freq - 1)
-            from_below = jnp.where(
-                f > 0, jnp.maximum(drift_ref[below], 0.0) * points_ref[below * sub_rows + r], 0.0
-            )
-            from_above = jnp.where(
-                f < n_freq - 1,
-                jnp.maximum(-drift_ref[above], 0.0) * points_ref[above * sub_rows + r],
-                0.0,
-            )
-            shifted_ref[f] = here - jnp.abs(rate) * here + from_below + from_above
+            rate = drift_ref[:, f : f + 1]
+            shifted = here - jnp.abs(rate) * here
+            if f > 0:
+                below = points_ref[(f - 1) * sub_rows + r]
+                shifted = shifted + jnp.maximum(drift_ref[:, f - 1 : f], 0.0) * below
+            if f < n_freq - 1:
+                above = points_ref[(f + 1) * sub_rows + r]
+                shifted = shifted + jnp.maximum(-drift_ref[:, f + 1 : f + 2], 0.0) * above
+            shifted_ref[f] = shifted
             source_ref[f] = jnp.zeros_like(here)
-            return carry
-
-        lax.fori_loop(0, n_freq, advect, 0, unroll=True)
 
         def interact(f, carry):
             up_freq = table_ref[0, f]
@@ -202,8 +196,7 @@
     up_ids = partners[0].reshape(NF, ND)[:, 0]
     down_ids = partners[1].reshape(NF, ND)[:, 0]
     table = jnp.stack([up_ids // ND, down_ids // ND, up_ids % ND, ND - down_ids % ND])
-    rates = jnp.pad(drift.reshape(NF, ND), ((0, 0), (0, PAD_DIR - ND)))
-    rates = jnp.broadcast_to(rates[:, :, None], (NF, PAD_DIR, grid_cols))
+    rates = jnp.pad(drift.reshape(NF, ND).T, ((0, PAD_DIR - ND), (0, grid_cols - NF)))
     vmem = pl.BlockSpec(memory_space=pltpu.VMEM)
     block = pltpu.VMEM((NF, PAD_DIR, grid_cols), jnp.float32)
     out = pl.pallas_call(

time: 68.7 us -> 68.8 us (level)
  the two profiles are of different devices: /device:TPU:193 before, /device:TPU:201 now
where the time goes in v10:
time: 68.8 us; the launch traced here: 68.4 us
  waiting for transfers between devices  29.8 us (43%)
  Pallas kernels  15.4 us (22%)
  starting transfers between devices  13.6 us (20%)
  local copies, waits for them, and re-layouts  4.93 us (7%)
  other arithmetic  4.6 us (7%)
    all_to_all x1, waiting for transfers between devices, shards(): lax.all_to_all(turned, 'spec', split_axis=0, concat_axis=0, tiled=True)  28.6 us
    all_to_all x1, starting transfers between devices, shards(): lax.all_to_all(turned, 'spec', split_axis=0, concat_axis=0, tiled=True)  9.74 us
    pallas_call x1, Pallas kernels, settle(): pl.pallas_call(settle_kernel, out_shape=jax.ShapeDtypeStruct((NF * ND, su...  7.6 us
    pallas_call x1, Pallas kernels, propagate(): pl.pallas_call(propagate_kernel, out_shape=jax.ShapeDtypeStruct((blocks,...  5 us
    ppermute x1, starting transfers between devices, neighbours(): lax.ppermute(edges_last, 'tile', [(i, (i + 1) % count) for i in range(cou...  3.86 us
    pallas_call x1, Pallas kernels, edges(): pl.pallas_call(edges_kernel, out_shape=(plane, plane), in_specs=[vmem] *...  2.8 us
    unnamed x13, local copies, waits for them, and re-layouts  2.55 us
    reduce_or x1, other arithmetic, sea_cells(): return jnp.any(matches, axis=1).astype(jnp.float32)  2.31 us
  transfers between devices with their start and end apart: 3, of which 2 were waited for; matrix products, arithmetic and copies ran while one was open for 8% of the time, Pallas kernels for 0%

profile of v10, /device:TPU:201, one launch (start us, length us, event | category | flops | bytes accessed | tf_op | source)
XLA Modules:
  0.0 68.4 jit_solution(1269484928411715584)
XLA Ops:
  0.0 0.8 %copy.27 = s32[32,1,192]{2,0,1:T(8,128)S(1)} copy(s32[32,1,192]{2,1,0:T(1,128)} %param.13) | data formatting | bytes 49152
  0.8 0.7 %iota_compare_fusion.1 = pred[32,192]{1,0:T(8,128)(4,1)S(1)} fusion(s32[32]{0:T(128)} %bitcast.32), kind=kLoop, calls=%fused_computation.5 | loop fusion | flops 6144 | bytes 6272 | tf_op jit(solution)/shard_map/lt | solution.py:46
  1.5 0.1 broadcast_add_fusion
  1.6 0.2 and_reduce_fusion
  1.8 0.7 %copy.21 = f32[32,2,2]{2,1,0:T(2,128)} copy(f32[32,2,2]{0,2,1:T(2,128)S(1)} %convert_element_type.26) | data formatting | bytes 1024 | tf_op jit(solution)/shard_map/convert_element_type | solution.py:40
  2.5 2.8 %shard_map.85 = (f32[64,128]{1,0:T(8,128)}, f32[64,128]{1,0:T(8,128)}) custom-call(f32[36,64,128]{2,1,0:T(8,128)} %spec_ref.3, f32[64,2]{1,0:T(8,128)} %bitcast.28, f32[64,128]{1,0:T(8,128)} %depth_ref.3), custom_call_target="tpu_custom_call" | custom-call | tf_op jit(solution)/shard_map/pallas_call | solution.py:295
  5.3 3.9 %collective-permute-start = (f32[64,128]{1,0:T(8,128)}, f32[64,128]{1,0:T(8,128)S(1)}, u32[]{:S(2)}, u32[]{:S(2)}) collective-permute-start(f32[64,128]{1,0:T(8,128)} %get-tuple-element.7), channel_id=1, source_target_pairs={{0,1},{1,2},{2,3},{3,4},{4,5},{5,6},{6,7},{7,8},{8,9},{9,10},{10,1... | collective-permute-start | bytes 98312 | tf_op jit(solution)/shard_map/ppermute | solution.py:214
  9.2 0.0 collective-permute-start.1
  9.2 2.3 %fusion.1 = pred[32,256]{1,0:T(8,128)(4,1)S(1)} fusion(s32[32,192]{1,0:T(8,128)S(1)} %bitcast.27, pred[32,192]{1,0:T(8,128)(4,1)S(1)} %iota_compare_fusion.1), kind=kLoop, calls=%fused_computation.2 | loop fusion | flops 4710400 | bytes 38912 | tf_op jit(solution)/shard_map/reduce_or | solution.py:48
  11.6 0.6 pad_maximum_fusion.coef_ref
  12.2 0.6 reshape.256.mask_ref
  12.8 0.0 collective-permute-done.west_ref
  12.8 0.0 copy-start.1
  12.8 1.1 %collective-permute-done.1.east_ref = f32[64,128]{1,0:T(8,128)S(1)} collective-permute-done((f32[64,128]{1,0:T(8,128)}, f32[64,128]{1,0:T(8,128)S(1)}, u32[]{:S(2)}, u32[]{:S(2)}) %collective-permute-start.1) | collective-permute-done | bytes 32800 | tf_op jit(solution)/shard_map/ppermute | solution.py:215
  13.9 0.0 copy-done.1
  13.9 0.0 copy-start.2
  13.9 0.6 copy-done.2
  14.5 5.0 %shard_map.86 = f32[32,72,128]{2,1,0:T(8,128)} custom-call(f32[2,36]{1,0:T(2,128)} %pad_maximum_fusion.coef_ref, f32[36,64,128]{2,1,0:T(8,128)} %spec_ref.3, f32[64,128]{1,0:T(8,128)} %reshape.256.mask_ref, f32[64,128]{1,0:T(8,128)} %depth_ref.3, f32[64,128]{1,0:T(8,128)} %turn_ref.1, f32[64,128]{1,0:T(8,128)} %copy-done.1, f32[64,128]{1,0:T(8,128)} %copy-done.2), custom_call_target="tpu_custom_call" | custom-call | tf_op jit(solution)/shard_map/pallas_call | solution.py:306
  19.5 0.0 copy-start.3
  19.5 0.0 copy-start.4
  19.6 9.7 %all-to-all-start = ((f32[32,72,128]{2,1,0:T(8,128)}), f32[32,72,128]{2,1,0:T(8,128)S(1)}, u32[]{:S(2)}, u32[]{:S(2)}) async-start(f32[32,72,128]{2,1,0:T(8,128)} %shard_map.86), calls=%async_computation | async-start | bytes 2359296 | tf_op jit(solution)/shard_map/all_to_all | solution.py:340
  29.3 0.0 copy-done.3
  29.3 0.1 reshape_squeeze.6
  29.4 0.1 copy.24
  29.5 0.1 reshape_squeeze.7
  29.6 0.1 copy.25
  29.7 0.0 copy-done.4
  29.7 0.1 reshape.255
  29.8 0.1 copy.20
  29.9 0.6 pad.4.drift_ref
  30.6 0.6 pad_add_fusion.table_ref
  31.1 28.6 %all-to-all-done.blocks_ref = f32[32,72,128]{2,1,0:T(8,128)S(1)} async-done(((f32[32,72,128]{2,1,0:T(8,128)}), f32[32,72,128]{2,1,0:T(8,128)S(1)}, u32[]{:S(2)}, u32[]{:S(2)}) %all-to-all-start) | async-done | bytes 1179680 | tf_op jit(solution)/shard_map/all_to_all | solution.py:340
  59.8 0.0 copy-start
  59.8 1.0 %copy-done = f32[32,72,128]{2,1,0:T(8,128)} copy-done((f32[32,72,128]{2,1,0:T(8,128)}, f32[32,72,128]{2,1,0:T(8,128)S(1)}, u32[]{:S(2)}) %copy-start) | copy-done | bytes 1179672
  60.8 7.6 %shard_map.87 = f32[1152,2,128]{2,1,0:T(2,128)} custom-call(s32[4,32]{1,0:T(4,128)} %pad_add_fusion.table_ref, f32[32,72,128]{2,1,0:T(8,128)} %copy-done, f32[40,128]{1,0:T(8,128)} %pad.4.drift_ref), custom_call_target="tpu_custom_call" | custom-call | tf_op jit(solution)/shard_map/pallas_call | solution.py:202
  (6 shorter events, 0.1 us)
Async XLA Ops:
  5.3 7.5 %collective-permute-start = (f32[64,128]{1,0:T(8,128)}, f32[64,128]{1,0:T(8,128)S(1)}, u32[]{:S(2)}, u32[]{:S(2)}) collective-permute-start(f32[64,128]{1,0:T(8,128)} %get-tuple-element.7), channel_id=1, source_target_pairs={{0,1},{1,2},{2,3},{3,4},{4,5},{5,6},{6,7},{7,8},{8,9},{9,10},{10,1... | collective-permute-start | bytes 98312 | tf_op jit(solution)/shard_map/ppermute | solution.py:214
  9.2 4.8 %collective-permute-start.1 = (f32[64,128]{1,0:T(8,128)}, f32[64,128]{1,0:T(8,128)S(1)}, u32[]{:S(2)}, u32[]{:S(2)}) collective-permute-start(f32[64,128]{1,0:T(8,128)} %get-tuple-element.8), channel_id=1, source_target_pairs={{1,0},{2,1},{3,2},{4,3},{5,4},{6,5},{7,6},{8,7},{9,8},{10,9},{11,1... | collective-permute-start | bytes 98312 | tf_op jit(solution)/shard_map/ppermute | solution.py:215
  12.8 1.1 %copy-start.1 = (f32[64,128]{1,0:T(8,128)}, f32[64,128]{1,0:T(8,128)S(1)}, u32[]{:S(2)}) copy-start(f32[64,128]{1,0:T(8,128)S(1)} %collective-permute-done.west_ref) | copy-start | bytes 98308
  13.9 0.6 copy-start.2
  19.5 9.8 %copy-start.3 = (s32[2,1152]{1,0:T(2,128)S(1)}, s32[2,1152]{1,0:T(2,128)}, u32[]{:S(2)}) copy-start(s32[2,1152]{1,0:T(2,128)} %param.12) | copy-start | bytes 27652
  19.5 10.2 %copy-start.4 = (f32[1152]{0:T(1024)S(1)}, f32[1152]{0:T(1024)}, u32[]{:S(2)}) copy-start(f32[1152]{0:T(1024)} %param.11) | copy-start | bytes 13828
  19.6 40.2 %all-to-all-start = ((f32[32,72,128]{2,1,0:T(8,128)}), f32[32,72,128]{2,1,0:T(8,128)S(1)}, u32[]{:S(2)}, u32[]{:S(2)}) async-start(f32[32,72,128]{2,1,0:T(8,128)} %shard_map.86), calls=%async_computation | async-start | bytes 2359296 | tf_op jit(solution)/shard_map/all_to_all | solution.py:340
  59.8 1.0 %copy-start = (f32[32,72,128]{2,1,0:T(8,128)}, f32[32,72,128]{2,1,0:T(8,128)S(1)}, u32[]{:S(2)}) copy-start(f32[32,72,128]{2,1,0:T(8,128)S(1)} %all-to-all-done.blocks_ref) | copy-start | bytes 3538948

commit v11 on v10

--- a/solution.py
+++ b/solution.py
@@ -159,35 +159,40 @@
             if f < n_freq - 1:
                 above = points_ref[(f + 1) * sub_rows + r]
                 shifted = shifted + jnp.maximum(-drift_ref[:, f + 1 : f + 2], 0.0) * above
-            shifted_ref[f] = shifted
-            source_ref[f] = jnp.zeros_like(here)
+            shifted_ref[f * sub_rows + r] = shifted
+            source_ref[f * sub_rows + r] = jnp.zeros_like(here)
 
         def interact(f, carry):
             up_freq = table_ref[0, f]
             down_freq = table_ref[1, f]
             up_turn = table_ref[2, f]
             down_turn = table_ref[3, f]
-            here = shifted_ref[f]
-            plus_values = turn_rows(shifted_ref[up_freq], up_turn)
-            minus_values = turn_rows(shifted_ref[down_freq], ND - down_turn)
+            here = shifted_ref[f * sub_rows + r]
+            plus_values = turn_rows(shifted_ref[up_freq * sub_rows + r], up_turn)
+            minus_values = turn_rows(shifted_ref[down_freq * sub_rows + r], ND - down_turn)
             quartet = (
                 here * here * (plus_values + minus_values)
                 - 2.0 * here * plus_values * minus_values
             )
-            quartet_ref[f] = quartet
-            source_ref[up_freq] = source_ref[up_freq] + turn_rows(quartet, ND - up_turn)
-            source_ref[down_freq] = source_ref[down_freq] + turn_rows(quartet, down_turn)
+            quartet_ref[f * sub_rows + r] = quartet
+            up_at = up_freq * sub_rows + r
+            down_at = down_freq * sub_rows + r
+            source_ref[up_at] = source_ref[up_at] + turn_rows(quartet, ND - up_turn)
+            source_ref[down_at] = source_ref[down_at] + turn_rows(quartet, down_turn)
             return carry
 
         lax.fori_loop(0, n_freq, interact, 0, unroll=True)
 
-        def finish(f, carry):
-            source = source_ref[f] - 2.0 * quartet_ref[f]
-            value = shifted_ref[f] + dia_coeff * source
-            out_ref[pl.ds(f * ND, ND), r, :] = value[:ND]
-            return carry
-
-        lax.fori_loop(0, n_freq, finish, 0, unroll=True)
+    def finish(f, carry):
+        values = []
+        for r in range(sub_rows):
+            at = f * sub_rows + r
+            source = source_ref[at] - 2.0 * quartet_ref[at]
+            values.append((shifted_ref[at] + dia_coeff * source)[:ND])
+        out_ref[pl.ds(f * ND, ND), :, :] = jnp.stack(values, axis=1)
+        return carry
+
+    lax.fori_loop(0, n_freq, finish, 0, unroll=True)
 
 
 def settle(points, drift, partners):
@@ -198,13 +203,13 @@
     table = jnp.stack([up_ids // ND, down_ids // ND, up_ids % ND, ND - down_ids % ND])
     rates = jnp.pad(drift.reshape(NF, ND).T, ((0, PAD_DIR - ND), (0, grid_cols - NF)))
     vmem = pl.BlockSpec(memory_space=pltpu.VMEM)
-    block = pltpu.VMEM((NF, PAD_DIR, grid_cols), jnp.float32)
+    block = pltpu.VMEM((NF * sub_rows, PAD_DIR, grid_cols), jnp.float32)
     out = pl.pallas_call(
         settle_kernel,
         out_shape=jax.ShapeDtypeStruct((NF * ND, sub_rows, grid_cols), jnp.float32),
         in_specs=[pl.BlockSpec(memory_space=pltpu.SMEM), vmem, vmem],
         out_specs=vmem,
-        scratch_shapes=[pltpu.VMEM((NF * sub_rows, PAD_DIR, grid_cols), jnp.float32), block, block, block],
+        scratch_shapes=[block, block, block, block],
     )(table, points, rates)
     return out
 

time: 68.8 us -> 68.9 us (level)
  the two profiles are of different devices: /device:TPU:201 before, /device:TPU:193 now
where the time goes in v11:
time: 68.9 us; the launch traced here: 68.5 us
  waiting for transfers between devices  29.7 us (43%)
  Pallas kernels  15.5 us (22%)
  starting transfers between devices  13.7 us (20%)
  local copies, waits for them, and re-layouts  4.93 us (7%)
  other arithmetic  4.6 us (7%)
    all_to_all x1, waiting for transfers between devices, shards(): lax.all_to_all(turned, 'spec', split_axis=0, concat_axis=0, tiled=True)  28.5 us
    all_to_all x1, starting transfers between devices, shards(): lax.all_to_all(turned, 'spec', split_axis=0, concat_axis=0, tiled=True)  9.8 us
    pallas_call x1, Pallas kernels, settle(): pl.pallas_call(settle_kernel, out_shape=jax.ShapeDtypeStruct((NF * ND, su...  7.74 us
    pallas_call x1, Pallas kernels, propagate(): pl.pallas_call(propagate_kernel, out_shape=jax.ShapeDtypeStruct((blocks,...  5 us
    ppermute x1, starting transfers between devices, neighbours(): lax.ppermute(edges_last, 'tile', [(i, (i + 1) % count) for i in range(cou...  3.86 us
    pallas_call x1, Pallas kernels, edges(): pl.pallas_call(edges_kernel, out_shape=(plane, plane), in_specs=[vmem] *...  2.8 us
    unnamed x13, local copies, waits for them, and re-layouts  2.55 us
    reduce_or x1, other arithmetic, sea_cells(): return jnp.any(matches, axis=1).astype(jnp.float32)  2.31 us
  transfers between devices with their start and end apart: 3, of which 2 were waited for; matrix products, arithmetic and copies ran while one was open for 8% of the time, Pallas kernels for 0%

profile of v11, /device:TPU:193, one launch (start us, length us, event | category | flops | bytes accessed | tf_op | source)
XLA Modules:
  0.0 68.5 jit_solution(3970799847080678379)
XLA Ops:
  0.0 0.8 %copy.27 = s32[32,1,192]{2,0,1:T(8,128)S(1)} copy(s32[32,1,192]{2,1,0:T(1,128)} %param.13) | data formatting | bytes 49152
  0.8 0.7 %iota_compare_fusion.1 = pred[32,192]{1,0:T(8,128)(4,1)S(1)} fusion(s32[32]{0:T(128)} %bitcast.32), kind=kLoop, calls=%fused_computation.5 | loop fusion | flops 6144 | bytes 6272 | tf_op jit(solution)/shard_map/lt | solution.py:46
  1.5 0.1 broadcast_add_fusion
  1.6 0.2 and_reduce_fusion
  1.8 0.7 %copy.21 = f32[32,2,2]{2,1,0:T(2,128)} copy(f32[32,2,2]{0,2,1:T(2,128)S(1)} %convert_element_type.26) | data formatting | bytes 1024 | tf_op jit(solution)/shard_map/convert_element_type | solution.py:40
  2.5 2.8 %shard_map.85 = (f32[64,128]{1,0:T(8,128)}, f32[64,128]{1,0:T(8,128)}) custom-call(f32[36,64,128]{2,1,0:T(8,128)} %spec_ref.3, f32[64,2]{1,0:T(8,128)} %bitcast.28, f32[64,128]{1,0:T(8,128)} %depth_ref.3), custom_call_target="tpu_custom_call" | custom-call | tf_op jit(solution)/shard_map/pallas_call | solution.py:300
  5.3 3.9 %collective-permute-start = (f32[64,128]{1,0:T(8,128)}, f32[64,128]{1,0:T(8,128)S(1)}, u32[]{:S(2)}, u32[]{:S(2)}) collective-permute-start(f32[64,128]{1,0:T(8,128)} %get-tuple-element.7), channel_id=1, source_target_pairs={{0,1},{1,2},{2,3},{3,4},{4,5},{5,6},{6,7},{7,8},{8,9},{9,10},{10,1... | collective-permute-start | bytes 98312 | tf_op jit(solution)/shard_map/ppermute | solution.py:219
  9.2 0.0 collective-permute-start.1
  9.2 2.3 %fusion.1 = pred[32,256]{1,0:T(8,128)(4,1)S(1)} fusion(s32[32,192]{1,0:T(8,128)S(1)} %bitcast.27, pred[32,192]{1,0:T(8,128)(4,1)S(1)} %iota_compare_fusion.1), kind=kLoop, calls=%fused_computation.2 | loop fusion | flops 4710400 | bytes 38912 | tf_op jit(solution)/shard_map/reduce_or | solution.py:48
  11.6 0.6 pad_maximum_fusion.coef_ref
  12.2 0.6 reshape.256.mask_ref
  12.8 0.0 collective-permute-done.west_ref
  12.8 0.0 copy-start.1
  12.8 1.1 %collective-permute-done.1.east_ref = f32[64,128]{1,0:T(8,128)S(1)} collective-permute-done((f32[64,128]{1,0:T(8,128)}, f32[64,128]{1,0:T(8,128)S(1)}, u32[]{:S(2)}, u32[]{:S(2)}) %collective-permute-start.1) | collective-permute-done | bytes 32800 | tf_op jit(solution)/shard_map/ppermute | solution.py:220
  13.9 0.0 copy-done.1
  13.9 0.0 copy-start.2
  13.9 0.6 copy-done.2
  14.5 5.0 %shard_map.86 = f32[32,72,128]{2,1,0:T(8,128)} custom-call(f32[2,36]{1,0:T(2,128)} %pad_maximum_fusion.coef_ref, f32[36,64,128]{2,1,0:T(8,128)} %spec_ref.3, f32[64,128]{1,0:T(8,128)} %reshape.256.mask_ref, f32[64,128]{1,0:T(8,128)} %depth_ref.3, f32[64,128]{1,0:T(8,128)} %turn_ref.1, f32[64,128]{1,0:T(8,128)} %copy-done.1, f32[64,128]{1,0:T(8,128)} %copy-done.2), custom_call_target="tpu_custom_call" | custom-call | tf_op jit(solution)/shard_map/pallas_call | solution.py:311
  19.5 0.0 copy-start.3
  19.5 0.0 copy-start.4
  19.6 9.8 %all-to-all-start = ((f32[32,72,128]{2,1,0:T(8,128)}), f32[32,72,128]{2,1,0:T(8,128)S(1)}, u32[]{:S(2)}, u32[]{:S(2)}) async-start(f32[32,72,128]{2,1,0:T(8,128)} %shard_map.86), calls=%async_computation | async-start | bytes 2359296 | tf_op jit(solution)/shard_map/all_to_all | solution.py:345
  29.4 0.0 copy-done.3
  29.4 0.1 reshape_squeeze.6
  29.5 0.1 copy.24
  29.6 0.1 reshape_squeeze.7
  29.7 0.1 copy.25
  29.8 0.0 copy-done.4
  29.8 0.1 reshape.255
  29.9 0.1 copy.20
  30.0 0.6 pad.4.drift_ref
  30.6 0.6 pad_add_fusion.table_ref
  31.2 28.5 %all-to-all-done.blocks_ref = f32[32,72,128]{2,1,0:T(8,128)S(1)} async-done(((f32[32,72,128]{2,1,0:T(8,128)}), f32[32,72,128]{2,1,0:T(8,128)S(1)}, u32[]{:S(2)}, u32[]{:S(2)}) %all-to-all-start) | async-done | bytes 1179680 | tf_op jit(solution)/shard_map/all_to_all | solution.py:345
  59.8 0.0 copy-start
  59.8 1.0 %copy-done = f32[32,72,128]{2,1,0:T(8,128)} copy-done((f32[32,72,128]{2,1,0:T(8,128)}, f32[32,72,128]{2,1,0:T(8,128)S(1)}, u32[]{:S(2)}) %copy-start) | copy-done | bytes 1179672
  60.8 7.7 %shard_map.87 = f32[1152,2,128]{2,1,0:T(2,128)} custom-call(s32[4,32]{1,0:T(4,128)} %pad_add_fusion.table_ref, f32[32,72,128]{2,1,0:T(8,128)} %copy-done, f32[40,128]{1,0:T(8,128)} %pad.4.drift_ref), custom_call_target="tpu_custom_call" | custom-call | tf_op jit(solution)/shard_map/pallas_call | solution.py:207
  (6 shorter events, 0.1 us)
Async XLA Ops:
  5.3 7.5 %collective-permute-start = (f32[64,128]{1,0:T(8,128)}, f32[64,128]{1,0:T(8,128)S(1)}, u32[]{:S(2)}, u32[]{:S(2)}) collective-permute-start(f32[64,128]{1,0:T(8,128)} %get-tuple-element.7), channel_id=1, source_target_pairs={{0,1},{1,2},{2,3},{3,4},{4,5},{5,6},{6,7},{7,8},{8,9},{9,10},{10,1... | collective-permute-start | bytes 98312 | tf_op jit(solution)/shard_map/ppermute | solution.py:219
  9.2 4.8 %collective-permute-start.1 = (f32[64,128]{1,0:T(8,128)}, f32[64,128]{1,0:T(8,128)S(1)}, u32[]{:S(2)}, u32[]{:S(2)}) collective-permute-start(f32[64,128]{1,0:T(8,128)} %get-tuple-element.8), channel_id=1, source_target_pairs={{1,0},{2,1},{3,2},{4,3},{5,4},{6,5},{7,6},{8,7},{9,8},{10,9},{11,1... | collective-permute-start | bytes 98312 | tf_op jit(solution)/shard_map/ppermute | solution.py:220
  12.8 1.1 %copy-start.1 = (f32[64,128]{1,0:T(8,128)}, f32[64,128]{1,0:T(8,128)S(1)}, u32[]{:S(2)}) copy-start(f32[64,128]{1,0:T(8,128)S(1)} %collective-permute-done.west_ref) | copy-start | bytes 98308
  13.9 0.6 copy-start.2
  19.5 9.8 %copy-start.3 = (s32[2,1152]{1,0:T(2,128)S(1)}, s32[2,1152]{1,0:T(2,128)}, u32[]{:S(2)}) copy-start(s32[2,1152]{1,0:T(2,128)} %param.12) | copy-start | bytes 27652
  19.5 10.2 %copy-start.4 = (f32[1152]{0:T(1024)S(1)}, f32[1152]{0:T(1024)}, u32[]{:S(2)}) copy-start(f32[1152]{0:T(1024)} %param.11) | copy-start | bytes 13828
  19.6 40.2 %all-to-all-start = ((f32[32,72,128]{2,1,0:T(8,128)}), f32[32,72,128]{2,1,0:T(8,128)S(1)}, u32[]{:S(2)}, u32[]{:S(2)}) async-start(f32[32,72,128]{2,1,0:T(8,128)} %shard_map.86), calls=%async_computation | async-start | bytes 2359296 | tf_op jit(solution)/shard_map/all_to_all | solution.py:345
  59.8 1.0 %copy-start = (f32[32,72,128]{2,1,0:T(8,128)}, f32[32,72,128]{2,1,0:T(8,128)S(1)}, u32[]{:S(2)}) copy-start(f32[32,72,128]{2,1,0:T(8,128)S(1)} %all-to-all-done.blocks_ref) | copy-start | bytes 3538948

commit v12 on v11

--- a/solution.py
+++ b/solution.py
@@ -130,7 +130,7 @@
 
 
 def settle_kernel(
-    table_ref, blocks_ref, drift_ref, out_ref, points_ref, shifted_ref, quartet_ref, source_ref
+    table_ref, blocks_ref, drift_ref, out_ref, points_ref, shifted_ref, quartet_ref, *source_refs
 ):
     n_freq = blocks_ref.shape[0]
     sub_rows = blocks_ref.shape[1] // ND
@@ -148,7 +148,6 @@
         lax.fori_loop(0, n_freq, align, 0, unroll=True)
 
     for r in range(sub_rows):
-
         for f in range(n_freq):
             here = points_ref[f * sub_rows + r]
             rate = drift_ref[:, f : f + 1]
@@ -160,13 +159,17 @@
                 above = points_ref[(f + 1) * sub_rows + r]
                 shifted = shifted + jnp.maximum(-drift_ref[:, f + 1 : f + 2], 0.0) * above
             shifted_ref[f * sub_rows + r] = shifted
-            source_ref[f * sub_rows + r] = jnp.zeros_like(here)
-
-        def interact(f, carry):
-            up_freq = table_ref[0, f]
-            down_freq = table_ref[1, f]
-            up_turn = table_ref[2, f]
-            down_turn = table_ref[3, f]
+            for source_ref in source_refs:
+                source_ref[f * sub_rows + r] = jnp.zeros_like(here)
+
+    def interact(f, carry):
+        up_freq = table_ref[0, f]
+        down_freq = table_ref[1, f]
+        up_turn = table_ref[2, f]
+        down_turn = table_ref[3, f]
+        for r in range(sub_rows):
+            up_ref = source_refs[2 * r]
+            down_ref = source_refs[2 * r + 1]
             here = shifted_ref[f * sub_rows + r]
             plus_values = turn_rows(shifted_ref[up_freq * sub_rows + r], up_turn)
             minus_values = turn_rows(shifted_ref[down_freq * sub_rows + r], ND - down_turn)
@@ -177,17 +180,17 @@
             quartet_ref[f * sub_rows + r] = quartet
             up_at = up_freq * sub_rows + r
             down_at = down_freq * sub_rows + r
-            source_ref[up_at] = source_ref[up_at] + turn_rows(quartet, ND - up_turn)
-            source_ref[down_at] = source_ref[down_at] + turn_rows(quartet, down_turn)
-            return carry
-
-        lax.fori_loop(0, n_freq, interact, 0, unroll=True)
+            up_ref[up_at] = up_ref[up_at] + turn_rows(quartet, ND - up_turn)
+            down_ref[down_at] = down_ref[down_at] + turn_rows(quartet, down_turn)
+        return carry
+
+    lax.fori_loop(0, n_freq, interact, 0, unroll=True)
 
     def finish(f, carry):
         values = []
         for r in range(sub_rows):
             at = f * sub_rows + r
-            source = source_ref[at] - 2.0 * quartet_ref[at]
+            source = source_refs[2 * r][at] + source_refs[2 * r + 1][at] - 2.0 * quartet_ref[at]
             values.append((shifted_ref[at] + dia_coeff * source)[:ND])
         out_ref[pl.ds(f * ND, ND), :, :] = jnp.stack(values, axis=1)
         return carry
@@ -209,7 +212,7 @@
         out_shape=jax.ShapeDtypeStruct((NF * ND, sub_rows, grid_cols), jnp.float32),
         in_specs=[pl.BlockSpec(memory_space=pltpu.SMEM), vmem, vmem],
         out_specs=vmem,
-        scratch_shapes=[block, block, block, block],
+        scratch_shapes=[block] * (3 + 2 * sub_rows),
     )(table, points, rates)
     return out
 

time: 68.9 us -> 69.4 us (level)
  the two profiles are of different devices: /device:TPU:193 before, /device:TPU:201 now
where the time goes in v12:
time: 69.4 us; the launch traced here: 69.1 us
  waiting for transfers between devices  29.8 us (43%)
  Pallas kernels  16.1 us (23%)
  starting transfers between devices  13.6 us (20%)
  local copies, waits for them, and re-layouts  4.93 us (7%)
  other arithmetic  4.6 us (7%)
    all_to_all x1, waiting for transfers between devices, shards(): lax.all_to_all(turned, 'spec', split_axis=0, concat_axis=0, tiled=True)  28.6 us
    all_to_all x1, starting transfers between devices, shards(): lax.all_to_all(turned, 'spec', split_axis=0, concat_axis=0, tiled=True)  9.74 us
    pallas_call x1, Pallas kernels, settle(): pl.pallas_call(settle_kernel, out_shape=jax.ShapeDtypeStruct((NF * ND, su...  8.27 us
    pallas_call x1, Pallas kernels, propagate(): pl.pallas_call(propagate_kernel, out_shape=jax.ShapeDtypeStruct((blocks,...  5 us
    ppermute x1, starting transfers between devices, neighbours(): lax.ppermute(edges_last, 'tile', [(i, (i + 1) % count) for i in range(cou...  3.86 us
    pallas_call x1, Pallas kernels, edges(): pl.pallas_call(edges_kernel, out_shape=(plane, plane), in_specs=[vmem] *...  2.8 us
    unnamed x13, local copies, waits for them, and re-layouts  2.55 us
    reduce_or x1, other arithmetic, sea_cells(): return jnp.any(matches, axis=1).astype(jnp.float32)  2.31 us
  transfers between devices with their start and end apart: 3, of which 2 were waited for; matrix products, arithmetic and copies ran while one was open for 8% of the time, Pallas kernels for 0%

profile of v12, /device:TPU:201, one launch (start us, length us, event | category | flops | bytes accessed | tf_op | source)
XLA Modules:
  0.0 69.1 jit_solution(13133871133379574176)
XLA Ops:
  0.0 0.8 %copy.27 = s32[32,1,192]{2,0,1:T(8,128)S(1)} copy(s32[32,1,192]{2,1,0:T(1,128)} %param.13) | data formatting | bytes 49152
  0.8 0.7 %iota_compare_fusion.1 = pred[32,192]{1,0:T(8,128)(4,1)S(1)} fusion(s32[32]{0:T(128)} %bitcast.32), kind=kLoop, calls=%fused_computation.5 | loop fusion | flops 6144 | bytes 6272 | tf_op jit(solution)/shard_map/lt | solution.py:46
  1.5 0.1 broadcast_add_fusion
  1.6 0.2 and_reduce_fusion
  1.8 0.7 %copy.21 = f32[32,2,2]{2,1,0:T(2,128)} copy(f32[32,2,2]{0,2,1:T(2,128)S(1)} %convert_element_type.26) | data formatting | bytes 1024 | tf_op jit(solution)/shard_map/convert_element_type | solution.py:40
  2.5 2.8 %shard_map.85 = (f32[64,128]{1,0:T(8,128)}, f32[64,128]{1,0:T(8,128)}) custom-call(f32[36,64,128]{2,1,0:T(8,128)} %spec_ref.3, f32[64,2]{1,0:T(8,128)} %bitcast.28, f32[64,128]{1,0:T(8,128)} %depth_ref.3), custom_call_target="tpu_custom_call" | custom-call | tf_op jit(solution)/shard_map/pallas_call | solution.py:303
  5.3 3.9 %collective-permute-start = (f32[64,128]{1,0:T(8,128)}, f32[64,128]{1,0:T(8,128)S(1)}, u32[]{:S(2)}, u32[]{:S(2)}) collective-permute-start(f32[64,128]{1,0:T(8,128)} %get-tuple-element.7), channel_id=1, source_target_pairs={{0,1},{1,2},{2,3},{3,4},{4,5},{5,6},{6,7},{7,8},{8,9},{9,10},{10,1... | collective-permute-start | bytes 98312 | tf_op jit(solution)/shard_map/ppermute | solution.py:222
  9.2 0.0 collective-permute-start.1
  9.2 2.3 %fusion.1 = pred[32,256]{1,0:T(8,128)(4,1)S(1)} fusion(s32[32,192]{1,0:T(8,128)S(1)} %bitcast.27, pred[32,192]{1,0:T(8,128)(4,1)S(1)} %iota_compare_fusion.1), kind=kLoop, calls=%fused_computation.2 | loop fusion | flops 4710400 | bytes 38912 | tf_op jit(solution)/shard_map/reduce_or | solution.py:48
  11.6 0.6 pad_maximum_fusion.coef_ref
  12.2 0.6 reshape.256.mask_ref
  12.8 0.0 collective-permute-done.west_ref
  12.8 0.0 copy-start.1
  12.8 1.1 %collective-permute-done.1.east_ref = f32[64,128]{1,0:T(8,128)S(1)} collective-permute-done((f32[64,128]{1,0:T(8,128)}, f32[64,128]{1,0:T(8,128)S(1)}, u32[]{:S(2)}, u32[]{:S(2)}) %collective-permute-start.1) | collective-permute-done | bytes 32800 | tf_op jit(solution)/shard_map/ppermute | solution.py:223
  13.9 0.0 copy-done.1
  13.9 0.0 copy-start.2
  13.9 0.6 copy-done.2
  14.5 5.0 %shard_map.86 = f32[32,72,128]{2,1,0:T(8,128)} custom-call(f32[2,36]{1,0:T(2,128)} %pad_maximum_fusion.coef_ref, f32[36,64,128]{2,1,0:T(8,128)} %spec_ref.3, f32[64,128]{1,0:T(8,128)} %reshape.256.mask_ref, f32[64,128]{1,0:T(8,128)} %depth_ref.3, f32[64,128]{1,0:T(8,128)} %turn_ref.1, f32[64,128]{1,0:T(8,128)} %copy-done.1, f32[64,128]{1,0:T(8,128)} %copy-done.2), custom_call_target="tpu_custom_call" | custom-call | tf_op jit(solution)/shard_map/pallas_call | solution.py:314
  19.5 0.0 copy-start.3
  19.5 0.0 copy-start.4
  19.6 9.7 %all-to-all-start = ((f32[32,72,128]{2,1,0:T(8,128)}), f32[32,72,128]{2,1,0:T(8,128)S(1)}, u32[]{:S(2)}, u32[]{:S(2)}) async-start(f32[32,72,128]{2,1,0:T(8,128)} %shard_map.86), calls=%async_computation | async-start | bytes 2359296 | tf_op jit(solution)/shard_map/all_to_all | solution.py:348
  29.3 0.0 copy-done.3
  29.3 0.1 reshape_squeeze.6
  29.4 0.1 copy.24
  29.5 0.1 reshape_squeeze.7
  29.6 0.1 copy.25
  29.7 0.0 copy-done.4
  29.7 0.1 reshape.255
  29.8 0.1 copy.20
  29.9 0.6 pad.4.drift_ref
  30.6 0.6 pad_add_fusion.table_ref
  31.1 28.6 %all-to-all-done.blocks_ref = f32[32,72,128]{2,1,0:T(8,128)S(1)} async-done(((f32[32,72,128]{2,1,0:T(8,128)}), f32[32,72,128]{2,1,0:T(8,128)S(1)}, u32[]{:S(2)}, u32[]{:S(2)}) %all-to-all-start) | async-done | bytes 1179680 | tf_op jit(solution)/shard_map/all_to_all | solution.py:348
  59.8 0.0 copy-start
  59.8 1.0 %copy-done = f32[32,72,128]{2,1,0:T(8,128)} copy-done((f32[32,72,128]{2,1,0:T(8,128)}, f32[32,72,128]{2,1,0:T(8,128)S(1)}, u32[]{:S(2)}) %copy-start) | copy-done | bytes 1179672
  60.8 8.3 %shard_map.87 = f32[1152,2,128]{2,1,0:T(2,128)} custom-call(s32[4,32]{1,0:T(4,128)} %pad_add_fusion.table_ref, f32[32,72,128]{2,1,0:T(8,128)} %copy-done, f32[40,128]{1,0:T(8,128)} %pad.4.drift_ref), custom_call_target="tpu_custom_call" | custom-call | tf_op jit(solution)/shard_map/pallas_call | solution.py:210
  (6 shorter events, 0.1 us)
Async XLA Ops:
  5.3 7.5 %collective-permute-start = (f32[64,128]{1,0:T(8,128)}, f32[64,128]{1,0:T(8,128)S(1)}, u32[]{:S(2)}, u32[]{:S(2)}) collective-permute-start(f32[64,128]{1,0:T(8,128)} %get-tuple-element.7), channel_id=1, source_target_pairs={{0,1},{1,2},{2,3},{3,4},{4,5},{5,6},{6,7},{7,8},{8,9},{9,10},{10,1... | collective-permute-start | bytes 98312 | tf_op jit(solution)/shard_map/ppermute | solution.py:222
  9.2 4.8 %collective-permute-start.1 = (f32[64,128]{1,0:T(8,128)}, f32[64,128]{1,0:T(8,128)S(1)}, u32[]{:S(2)}, u32[]{:S(2)}) collective-permute-start(f32[64,128]{1,0:T(8,128)} %get-tuple-element.8), channel_id=1, source_target_pairs={{1,0},{2,1},{3,2},{4,3},{5,4},{6,5},{7,6},{8,7},{9,8},{10,9},{11,1... | collective-permute-start | bytes 98312 | tf_op jit(solution)/shard_map/ppermute | solution.py:223
  12.8 1.1 %copy-start.1 = (f32[64,128]{1,0:T(8,128)}, f32[64,128]{1,0:T(8,128)S(1)}, u32[]{:S(2)}) copy-start(f32[64,128]{1,0:T(8,128)S(1)} %collective-permute-done.west_ref) | copy-start | bytes 98308
  13.9 0.6 copy-start.2
  19.5 9.8 %copy-start.3 = (s32[2,1152]{1,0:T(2,128)S(1)}, s32[2,1152]{1,0:T(2,128)}, u32[]{:S(2)}) copy-start(s32[2,1152]{1,0:T(2,128)} %param.12) | copy-start | bytes 27652
  19.5 10.2 %copy-start.4 = (f32[1152]{0:T(1024)S(1)}, f32[1152]{0:T(1024)}, u32[]{:S(2)}) copy-start(f32[1152]{0:T(1024)} %param.11) | copy-start | bytes 13828
  19.6 40.2 %all-to-all-start = ((f32[32,72,128]{2,1,0:T(8,128)}), f32[32,72,128]{2,1,0:T(8,128)S(1)}, u32[]{:S(2)}, u32[]{:S(2)}) async-start(f32[32,72,128]{2,1,0:T(8,128)} %shard_map.86), calls=%async_computation | async-start | bytes 2359296 | tf_op jit(solution)/shard_map/all_to_all | solution.py:348
  59.8 1.0 %copy-start = (f32[32,72,128]{2,1,0:T(8,128)}, f32[32,72,128]{2,1,0:T(8,128)S(1)}, u32[]{:S(2)}) copy-start(f32[32,72,128]{2,1,0:T(8,128)S(1)} %all-to-all-done.blocks_ref) | copy-start | bytes 3538948

commit v13 on v9

--- a/solution.py
+++ b/solution.py
@@ -328,10 +328,11 @@
     sub_rows = grid_rows // n_spec
     per_block = sub_rows * grid_cols
     sea_list = sea_slots[:, 0, :]
-    sea_mask = sea_cells(sea_list, sea_counts[:, 0], per_block).reshape(grid_rows, grid_cols)
     edge_mask = edge_cells(sea_list, sea_counts[:, 0], sub_rows, grid_cols)
     edges_first, edges_last = edges(spectrum, edge_mask, depth_speed)
     from_west, from_east = neighbours(edges_first, edges_last)
+    from_west, from_east, sea_list = lax.optimization_barrier((from_west, from_east, sea_list))
+    sea_mask = sea_cells(sea_list, sea_counts[:, 0], per_block).reshape(grid_rows, grid_cols)
     local_freq = channels // ND
     freq_ids = (
         lax.axis_index("spec") * local_freq + jnp.arange(local_freq, dtype=jnp.int32)

time: 68.7 us -> 70 us (1.019)
  the two profiles are of different devices: /device:TPU:193 before, /device:TPU:8 now
where the time goes in v13:
time: 70 us; the launch traced here: 69.6 us
  waiting for transfers between devices  27.2 us (39%)
  starting transfers between devices  18.8 us (27%)
  Pallas kernels  15 us (21%)
  other arithmetic  4.58 us (7%)
  local copies, waits for them, and re-layouts  3.85 us (6%)
    all_to_all x1, waiting for transfers between devices, shards(): lax.all_to_all(turned, 'spec', split_axis=0, concat_axis=0, tiled=True)  26 us
    all_to_all x1, starting transfers between devices, shards(): lax.all_to_all(turned, 'spec', split_axis=0, concat_axis=0, tiled=True)  10.3 us
    ppermute x1, starting transfers between devices, neighbours(): lax.ppermute(edges_first, 'tile', [((i + 1) % count, i) for i in range(co...  8.48 us
    pallas_call x1, Pallas kernels, settle(): pl.pallas_call(settle_kernel, out_shape=jax.ShapeDtypeStruct((NF * ND, su...  7.24 us
    pallas_call x1, Pallas kernels, propagate(): pl.pallas_call(propagate_kernel, out_shape=jax.ShapeDtypeStruct((blocks,...  5 us
    pallas_call x1, Pallas kernels, edges(): pl.pallas_call(edges_kernel, out_shape=(plane, plane), in_specs=[vmem] *...  2.8 us
    reduce_or x1, other arithmetic, sea_cells(): return jnp.any(matches, axis=1).astype(jnp.float32)  2.31 us
  transfers between devices with their start and end apart: 3, of which 3 were waited for; matrix products, arithmetic and copies ran while one was open for 2% of the time, Pallas kernels for 0%

profile of v13, /device:TPU:8, one launch (start us, length us, event | category | flops | bytes accessed | tf_op | source)
XLA Modules:
  0.0 69.6 jit_solution(15946867486282180676)
XLA Ops:
  0.0 0.8 %copy.25 = s32[32,1,192]{2,0,1:T(8,128)S(1)} copy(s32[32,1,192]{2,1,0:T(1,128)} %param.13) | data formatting | bytes 49152
  0.8 0.7 %iota_compare_fusion.1 = pred[32,192]{1,0:T(8,128)(4,1)S(1)} fusion(s32[32]{0:T(128)} %bitcast.30), kind=kLoop, calls=%fused_computation.5 | loop fusion | flops 6144 | bytes 6272 | tf_op jit(solution)/shard_map/lt | solution.py:36
  1.5 0.1 broadcast_add_fusion
  1.6 0.2 and_reduce_fusion
  1.8 0.7 %copy.19 = f32[32,2,2]{2,1,0:T(2,128)} copy(f32[32,2,2]{0,2,1:T(2,128)S(1)} %convert_element_type.25) | data formatting | bytes 1024 | tf_op jit(solution)/shard_map/convert_element_type | solution.py:40
  2.5 2.8 %shard_map.82 = (f32[64,128]{1,0:T(8,128)}, f32[64,128]{1,0:T(8,128)}) custom-call(f32[36,64,128]{2,1,0:T(8,128)} %spec_ref.3, f32[64,2]{1,0:T(8,128)} %bitcast.27, f32[64,128]{1,0:T(8,128)} %depth_ref.3), custom_call_target="tpu_custom_call" | custom-call | tf_op jit(solution)/shard_map/pallas_call | solution.py:302
  5.3 0.0 collective-permute-start
  5.3 8.5 %collective-permute-start.1 = (f32[64,128]{1,0:T(8,128)}, f32[64,128]{1,0:T(8,128)S(1)}, u32[]{:S(2)}, u32[]{:S(2)}) collective-permute-start(f32[64,128]{1,0:T(8,128)} %get-tuple-element.11), channel_id=1, source_target_pairs={{1,0},{2,1},{3,2},{4,3},{5,4},{6,5},{7,6},{8,7},{9,8},{10,9},{11,1... | collective-permute-start | bytes 98312 | tf_op jit(solution)/shard_map/ppermute | solution.py:222
  13.9 0.6 pad_maximum_fusion.coef_ref
  14.5 1.1 %collective-permute-done.west_ref = f32[64,128]{1,0:T(8,128)S(1)} collective-permute-done((f32[64,128]{1,0:T(8,128)}, f32[64,128]{1,0:T(8,128)S(1)}, u32[]{:S(2)}, u32[]{:S(2)}) %collective-permute-start) | collective-permute-done | bytes 32800 | tf_op jit(solution)/shard_map/ppermute | solution.py:221
  15.6 0.0 copy-start.1
  15.6 0.1 collective-permute-done.1.east_ref
  15.7 0.0 copy-start.2
  15.7 2.3 %fusion.1 = pred[32,256]{1,0:T(8,128)(4,1)S(1)} fusion(s32[32,192]{1,0:T(8,128)S(1)} %bitcast.26, pred[32,192]{1,0:T(8,128)(4,1)S(1)} %iota_compare_fusion.1), kind=kLoop, calls=%fused_computation.2 | loop fusion | flops 4710400 | bytes 38912 | tf_op jit(solution)/shard_map/reduce_or | solution.py:48
  18.0 0.6 reshape.258.mask_ref
  18.6 0.0 copy-done.1
  18.6 0.0 copy-done.2
  18.7 5.0 %shard_map.83 = f32[32,72,128]{2,1,0:T(8,128)} custom-call(f32[2,36]{1,0:T(2,128)} %pad_maximum_fusion.coef_ref, f32[36,64,128]{2,1,0:T(8,128)} %spec_ref.3, f32[64,128]{1,0:T(8,128)} %reshape.258.mask_ref, f32[64,128]{1,0:T(8,128)} %depth_ref.3, f32[64,128]{1,0:T(8,128)} %turn_ref.1, f32[64,128]{1,0:T(8,128)} %copy-done.1, f32[64,128]{1,0:T(8,128)} %copy-done.2), custom_call_target="tpu_custom_call" | custom-call | tf_op jit(solution)/shard_map/pallas_call | solution.py:313
  23.7 0.0 copy-start.3
  23.7 0.0 copy-start.4
  23.7 10.3 %all-to-all-start = ((f32[32,72,128]{2,1,0:T(8,128)}), f32[32,72,128]{2,1,0:T(8,128)S(1)}, u32[]{:S(2)}, u32[]{:S(2)}) async-start(f32[32,72,128]{2,1,0:T(8,128)} %shard_map.83), calls=%async_computation | async-start | bytes 2359296 | tf_op jit(solution)/shard_map/all_to_all | solution.py:348
  34.0 0.0 copy-done.3
  34.0 0.1 reshape_squeeze.6
  34.1 0.1 copy.22
  34.2 0.1 reshape_squeeze.7
  34.3 0.1 copy.23
  34.4 0.0 copy-done.4
  34.4 0.1 reshape.256
  34.5 0.6 pad_add_fusion.table_ref
  35.1 26.0 %all-to-all-done.blocks_ref = f32[32,72,128]{2,1,0:T(8,128)S(1)} async-done(((f32[32,72,128]{2,1,0:T(8,128)}), f32[32,72,128]{2,1,0:T(8,128)S(1)}, u32[]{:S(2)}, u32[]{:S(2)}) %all-to-all-start) | async-done | bytes 1179680 | tf_op jit(solution)/shard_map/all_to_all | solution.py:348
  61.1 0.0 copy-start
  61.1 1.3 %broadcast_in_dim.2.drift_ref = f32[32,40,128]{2,1,0:T(8,128)} broadcast(f32[32,40]{1,0:T(8,128)S(1)} %pad.4), dimensions={0,1} | broadcast | bytes 660480 | tf_op jit(solution)/shard_map/broadcast_in_dim | solution.py:206
  62.4 0.0 copy-done
  62.4 7.2 %shard_map.84 = f32[1152,2,128]{2,1,0:T(2,128)} custom-call(s32[4,32]{1,0:T(4,128)} %pad_add_fusion.table_ref, f32[32,72,128]{2,1,0:T(8,128)} %copy-done, f32[32,40,128]{2,1,0:T(8,128)} %broadcast_in_dim.2.drift_ref), custom_call_target="tpu_custom_call" | custom-call | tf_op jit(solution)/shard_map/pallas_call | solution.py:209
  (7 shorter events, 0.1 us)
Async XLA Ops:
  5.3 10.3 %collective-permute-start = (f32[64,128]{1,0:T(8,128)}, f32[64,128]{1,0:T(8,128)S(1)}, u32[]{:S(2)}, u32[]{:S(2)}) collective-permute-start(f32[64,128]{1,0:T(8,128)} %get-tuple-element.10), channel_id=1, source_target_pairs={{0,1},{1,2},{2,3},{3,4},{4,5},{5,6},{6,7},{7,8},{8,9},{9,10},{10,1... | collective-permute-start | bytes 98312 | tf_op jit(solution)/shard_map/ppermute | solution.py:221
  5.3 10.4 %collective-permute-start.1 = (f32[64,128]{1,0:T(8,128)}, f32[64,128]{1,0:T(8,128)S(1)}, u32[]{:S(2)}, u32[]{:S(2)}) collective-permute-start(f32[64,128]{1,0:T(8,128)} %get-tuple-element.11), channel_id=1, source_target_pairs={{1,0},{2,1},{3,2},{4,3},{5,4},{6,5},{7,6},{8,7},{9,8},{10,9},{11,1... | collective-permute-start | bytes 98312 | tf_op jit(solution)/shard_map/ppermute | solution.py:222
  15.6 3.0 %copy-start.1 = (f32[64,128]{1,0:T(8,128)}, f32[64,128]{1,0:T(8,128)S(1)}, u32[]{:S(2)}) copy-start(f32[64,128]{1,0:T(8,128)S(1)} %collective-permute-done.west_ref) | copy-start | bytes 98308
  15.7 2.9 %copy-start.2 = (f32[64,128]{1,0:T(8,128)}, f32[64,128]{1,0:T(8,128)S(1)}, u32[]{:S(2)}) copy-start(f32[64,128]{1,0:T(8,128)S(1)} %collective-permute-done.1.east_ref) | copy-start | bytes 98308
  23.7 10.3 %copy-start.3 = (s32[2,1152]{1,0:T(2,128)S(1)}, s32[2,1152]{1,0:T(2,128)}, u32[]{:S(2)}) copy-start(s32[2,1152]{1,0:T(2,128)} %param.12) | copy-start | bytes 27652
  23.7 10.7 %copy-start.4 = (f32[1152]{0:T(1024)S(1)}, f32[1152]{0:T(1024)}, u32[]{:S(2)}) copy-start(f32[1152]{0:T(1024)} %param.11) | copy-start | bytes 13828
  23.7 37.5 %all-to-all-start = ((f32[32,72,128]{2,1,0:T(8,128)}), f32[32,72,128]{2,1,0:T(8,128)S(1)}, u32[]{:S(2)}, u32[]{:S(2)}) async-start(f32[32,72,128]{2,1,0:T(8,128)} %shard_map.83), calls=%async_computation | async-start | bytes 2359296 | tf_op jit(solution)/shard_map/all_to_all | solution.py:348
  61.1 1.3 %copy-start = (f32[32,72,128]{2,1,0:T(8,128)}, f32[32,72,128]{2,1,0:T(8,128)S(1)}, u32[]{:S(2)}) copy-start(f32[32,72,128]{2,1,0:T(8,128)S(1)} %all-to-all-done.blocks_ref) | copy-start | bytes 3538948

commit v14 on v9

--- a/solution.py
+++ b/solution.py
@@ -38,6 +38,16 @@
     cells = rows + jnp.array([0, grid_cols - 1], dtype=jnp.int32)[None, :]
     matches = (sea_list[:, None, None, :] == cells[None, :, :, None]) & is_live[:, None, None, :]
     return jnp.any(matches, axis=3).astype(jnp.float32).reshape(-1, 2)
+
+
+def sea_rows(sea_list, sea_total, sub_rows, grid_cols):
+    slot_rank = jnp.arange(sea_list.shape[1], dtype=jnp.int32)
+    live = jnp.where(slot_rank[None, :] < sea_total[:, None], sea_list, -1)
+    live = jnp.repeat(live, sub_rows, axis=0)
+    row_start = (jnp.arange(live.shape[0], dtype=jnp.int32) % sub_rows) * grid_cols
+    cols = jnp.arange(grid_cols, dtype=jnp.int32)
+    matches = (live - row_start[:, None])[:, :, None] == cols[None, None, :]
+    return jnp.any(matches & (live >= 0)[:, :, None], axis=1).astype(jnp.float32)
 
 
 def sea_cells(sea_list, sea_total, per_block):
@@ -328,7 +338,7 @@
     sub_rows = grid_rows // n_spec
     per_block = sub_rows * grid_cols
     sea_list = sea_slots[:, 0, :]
-    sea_mask = sea_cells(sea_list, sea_counts[:, 0], per_block).reshape(grid_rows, grid_cols)
+    sea_mask = sea_rows(sea_list, sea_counts[:, 0], sub_rows, grid_cols)
     edge_mask = edge_cells(sea_list, sea_counts[:, 0], sub_rows, grid_cols)
     edges_first, edges_last = edges(spectrum, edge_mask, depth_speed)
     from_west, from_east = neighbours(edges_first, edges_last)

time: 68.7 us -> 71.3 us (1.038)
  other arithmetic: 4.58 us -> 7.76 us
    reduce_or x1, other arithmetic: 2.31 us -> 4.67 us  [sea_rows(): jnp.any(matches & (live >= 0)[:, :, None], axis=1).astype(jnp.float32)]
    ppermute x1, waiting for transfers between devices: 1.13 us -> 0.01 us  [neighbours(): lax.ppermute(edges_first, 'tile', [((i + 1) % count, i) for i in range(co...]
    unnamed x13 -> x17, local copies, waits for them, and re-layouts: 1.54 us -> 2.14 us
  transfers between devices with their start and end apart: 3 -> 3, of which waited for: 2 -> 1; matrix products, arithmetic and copies ran while one was open for 7% -> 10% of each run, Pallas kernels for 0% -> 0%
where the time goes in v14:
time: 71.3 us; the launch traced here: 70.8 us
  waiting for transfers between devices  29.7 us (42%)
  Pallas kernels  15 us (21%)
  starting transfers between devices  13.7 us (19%)
  other arithmetic  7.76 us (11%)
  local copies, waits for them, and re-layouts  4.52 us (6%)
    all_to_all x1, waiting for transfers between devices, shards(): lax.all_to_all(turned, 'spec', split_axis=0, concat_axis=0, tiled=True)  29.7 us
    all_to_all x1, starting transfers between devices, shards(): lax.all_to_all(turned, 'spec', split_axis=0, concat_axis=0, tiled=True)  9.8 us
    pallas_call x1, Pallas kernels, settle(): pl.pallas_call(settle_kernel, out_shape=jax.ShapeDtypeStruct((NF * ND, su...  7.24 us
    pallas_call x1, Pallas kernels, propagate(): pl.pallas_call(propagate_kernel, out_shape=jax.ShapeDtypeStruct((blocks,...  5 us
    reduce_or x1, other arithmetic, sea_rows(): jnp.any(matches & (live >= 0)[:, :, None], axis=1).astype(jnp.float32)  4.67 us
    ppermute x1, starting transfers between devices, neighbours(): lax.ppermute(edges_last, 'tile', [(i, (i + 1) % count) for i in range(cou...  3.86 us
    pallas_call x1, Pallas kernels, edges(): pl.pallas_call(edges_kernel, out_shape=(plane, plane), in_specs=[vmem] *...  2.81 us
    unnamed x17, local copies, waits for them, and re-layouts  2.14 us
  transfers between devices with their start and end apart: 3, of which 1 were waited for; matrix products, arithmetic and copies ran while one was open for 10% of the time, Pallas kernels for 0%

profile of v14, /device:TPU:193, one launch (start us, length us, event | category | flops | bytes accessed | tf_op | source)
XLA Modules:
  0.0 70.8 jit_solution(14424353370377898497)
XLA Ops:
  0.0 0.0 copy-start.6
  0.0 0.0 copy-start.1
  0.0 0.8 %iota_compare_fusion.1 = pred[32,192]{1,0:T(8,128)(4,1)S(1)} fusion(s32[32]{0:T(128)} %bitcast.31), kind=kLoop, calls=%fused_computation.7 | loop fusion | flops 6144 | bytes 6272 | tf_op jit(solution)/shard_map/lt | solution.py:45
  0.8 0.8 %copy.27 = s32[32,1,192]{2,0,1:T(8,128)S(1)} copy(s32[32,1,192]{2,1,0:T(1,128)} %param.13) | data formatting | bytes 49152
  1.6 0.1 broadcast_add_fusion
  1.6 0.2 and_reduce_fusion
  1.9 0.7 %copy.19 = f32[32,2,2]{2,1,0:T(2,128)} copy(f32[32,2,2]{0,2,1:T(2,128)S(1)} %convert_element_type.20) | data formatting | bytes 1024 | tf_op jit(solution)/shard_map/convert_element_type | solution.py:40
  2.6 2.8 %shard_map.82 = (f32[64,128]{1,0:T(8,128)}, f32[64,128]{1,0:T(8,128)}) custom-call(f32[36,64,128]{2,1,0:T(8,128)} %spec_ref.3, f32[64,2]{1,0:T(8,128)} %bitcast.27, f32[64,128]{1,0:T(8,128)} %depth_ref.3), custom_call_target="tpu_custom_call" | custom-call | tf_op jit(solution)/shard_map/pallas_call | solution.py:312
  5.4 3.9 %collective-permute-start = (f32[64,128]{1,0:T(8,128)}, f32[64,128]{1,0:T(8,128)S(1)}, u32[]{:S(2)}, u32[]{:S(2)}) collective-permute-start(f32[64,128]{1,0:T(8,128)} %get-tuple-element.7), channel_id=1, source_target_pairs={{0,1},{1,2},{2,3},{3,4},{4,5},{5,6},{6,7},{7,8},{8,9},{9,10},{10,1... | collective-permute-start | bytes 98312 | tf_op jit(solution)/shard_map/ppermute | solution.py:231
  9.3 0.0 collective-permute-start.1
  9.3 0.0 copy-done.6
  9.3 0.0 copy-done.1
  9.3 0.1 broadcast_select_fusion
  9.4 0.1 broadcast_subtract_fusion
  9.6 4.7 %fusion.1 = pred[64,128]{1,0:T(8,128)(4,1)S(1)} fusion(s32[64,192]{1,0:T(8,128)S(1)} %broadcast_subtract_fusion, pred[64,192]{1,0:T(8,128)(4,1)S(1)} %broadcast_compare_fusion), kind=kLoop, calls=%fused_computation.2 | loop fusion | flops 4710400 | bytes 69632 | tf_op jit(solution)/shard_map/reduce_or | solution.py:50
  14.3 0.6 pad_maximum_fusion.coef_ref
  14.9 0.6 convert_element_type.17.mask_ref
  15.5 0.0 collective-permute-done.west_ref
  15.5 0.0 copy-start.2
  15.5 0.0 collective-permute-done.1.east_ref
  15.5 0.6 copy-done.2
  16.1 0.0 copy-start.3
  16.1 0.6 copy-done.3
  16.7 5.0 %shard_map.83 = f32[32,72,128]{2,1,0:T(8,128)} custom-call(f32[2,36]{1,0:T(2,128)} %pad_maximum_fusion.coef_ref, f32[36,64,128]{2,1,0:T(8,128)} %spec_ref.3, f32[64,128]{1,0:T(8,128)} %convert_element_type.17.mask_ref, f32[64,128]{1,0:T(8,128)} %depth_ref.3, f32[64,128]{1,0:T(8,128)} %turn_ref.1, f32[64,128]{1,0:T(8,128)} %copy-done.2, f32[64,128]{1,0:T(8,128)} %copy-done.3), custom_call_target="tpu_custom_call" | custom-call | tf_op jit(solution)/shard_map/pallas_call | solution.py:323
  21.7 0.0 copy-start.4
  21.7 0.0 copy-start.5
  21.7 9.8 %all-to-all-start = ((f32[32,72,128]{2,1,0:T(8,128)}), f32[32,72,128]{2,1,0:T(8,128)S(1)}, u32[]{:S(2)}, u32[]{:S(2)}) async-start(f32[32,72,128]{2,1,0:T(8,128)} %shard_map.83), calls=%async_computation | async-start | bytes 2359296 | tf_op jit(solution)/shard_map/all_to_all | solution.py:357
  31.5 0.0 copy-done.4
  31.5 0.1 reshape_squeeze.6
  31.6 0.1 copy.22
  31.7 0.1 reshape_squeeze.7
  31.8 0.1 copy.23
  31.9 0.0 copy-done.5
  31.9 0.1 reshape.267
  32.1 0.6 pad_add_fusion.table_ref
  32.7 29.7 %all-to-all-done.blocks_ref = f32[32,72,128]{2,1,0:T(8,128)S(1)} async-done(((f32[32,72,128]{2,1,0:T(8,128)}), f32[32,72,128]{2,1,0:T(8,128)S(1)}, u32[]{:S(2)}, u32[]{:S(2)}) %all-to-all-start) | async-done | bytes 1179680 | tf_op jit(solution)/shard_map/all_to_all | solution.py:357
  62.3 0.0 copy-start
  62.3 1.3 %broadcast_in_dim.10.drift_ref = f32[32,40,128]{2,1,0:T(8,128)} broadcast(f32[32,40]{1,0:T(8,128)S(1)} %pad.4), dimensions={0,1} | broadcast | bytes 660480 | tf_op jit(solution)/shard_map/broadcast_in_dim | solution.py:216
  63.6 0.0 copy-done
  63.6 7.2 %shard_map.84 = f32[1152,2,128]{2,1,0:T(2,128)} custom-call(s32[4,32]{1,0:T(4,128)} %pad_add_fusion.table_ref, f32[32,72,128]{2,1,0:T(8,128)} %copy-done, f32[32,40,128]{2,1,0:T(8,128)} %broadcast_in_dim.10.drift_ref), custom_call_target="tpu_custom_call" | custom-call | tf_op jit(solution)/shard_map/pallas_call | solution.py:219
  (10 shorter events, 0.2 us)
Async XLA Ops:
  0.0 9.3 %copy-start.6 = (s32[32,1]{0,1:T(1,128)S(1)}, s32[32,1]{0,1:T(1,128)}, u32[]{:S(2)}) copy-start(s32[32,1]{0,1:T(1,128)} %param.14) | copy-start | bytes 388
  0.0 9.3 %copy-start.1 = (s32[32,1,192]{2,1,0:T(1,128)S(1)}, s32[32,1,192]{2,1,0:T(1,128)}, u32[]{:S(2)}) copy-start(s32[32,1,192]{2,1,0:T(1,128)} %param.13) | copy-start | bytes 73732
  5.4 10.1 %collective-permute-start = (f32[64,128]{1,0:T(8,128)}, f32[64,128]{1,0:T(8,128)S(1)}, u32[]{:S(2)}, u32[]{:S(2)}) collective-permute-start(f32[64,128]{1,0:T(8,128)} %get-tuple-element.7), channel_id=1, source_target_pairs={{0,1},{1,2},{2,3},{3,4},{4,5},{5,6},{6,7},{7,8},{8,9},{9,10},{10,1... | collective-permute-start | bytes 98312 | tf_op jit(solution)/shard_map/ppermute | solution.py:231
  9.3 6.2 %collective-permute-start.1 = (f32[64,128]{1,0:T(8,128)}, f32[64,128]{1,0:T(8,128)S(1)}, u32[]{:S(2)}, u32[]{:S(2)}) collective-permute-start(f32[64,128]{1,0:T(8,128)} %get-tuple-element.8), channel_id=1, source_target_pairs={{1,0},{2,1},{3,2},{4,3},{5,4},{6,5},{7,6},{8,7},{9,8},{10,9},{11,1... | collective-permute-start | bytes 98312 | tf_op jit(solution)/shard_map/ppermute | solution.py:232
  15.5 0.6 copy-start.2
  16.1 0.6 copy-start.3
  21.7 9.8 %copy-start.4 = (s32[2,1152]{1,0:T(2,128)S(1)}, s32[2,1152]{1,0:T(2,128)}, u32[]{:S(2)}) copy-start(s32[2,1152]{1,0:T(2,128)} %param.12) | copy-start | bytes 27652
  21.7 10.2 %copy-start.5 = (f32[1152]{0:T(1024)S(1)}, f32[1152]{0:T(1024)}, u32[]{:S(2)}) copy-start(f32[1152]{0:T(1024)} %param.11) | copy-start | bytes 13828
  21.7 40.6 %all-to-all-start = ((f32[32,72,128]{2,1,0:T(8,128)}), f32[32,72,128]{2,1,0:T(8,128)S(1)}, u32[]{:S(2)}, u32[]{:S(2)}) async-start(f32[32,72,128]{2,1,0:T(8,128)} %shard_map.83), calls=%async_computation | async-start | bytes 2359296 | tf_op jit(solution)/shard_map/all_to_all | solution.py:357
  62.3 1.3 %copy-start = (f32[32,72,128]{2,1,0:T(8,128)}, f32[32,72,128]{2,1,0:T(8,128)S(1)}, u32[]{:S(2)}) copy-start(f32[32,72,128]{2,1,0:T(8,128)S(1)} %all-to-all-done.blocks_ref) | copy-start | bytes 3538948

commit v15 on v9

--- a/solution.py
+++ b/solution.py
@@ -122,11 +122,10 @@
     return out
 
 
-def turn_rows(x, k):
-    d = lax.broadcasted_iota(jnp.int32, x.shape, 0)
+def turn_rows(x, k, rows):
     ahead = pltpu.roll(x, PAD_DIR - k, 0)
     wrapped = pltpu.roll(x, ND - k, 0)
-    return jnp.where(d + k < ND, ahead, wrapped)
+    return jnp.where(rows < ND - k, ahead, wrapped)
 
 
 def settle_kernel(
@@ -134,6 +133,7 @@
 ):
     n_freq = drift_ref.shape[0]
     sub_rows = blocks_ref.shape[1] // ND
+    rows = lax.broadcasted_iota(jnp.int32, (PAD_DIR, blocks_ref.shape[2]), 0)
     for r in range(sub_rows):
         start = r * ND // 8 * 8
         offset = r * ND - start
@@ -174,15 +174,15 @@
             up_turn = table_ref[2, f]
             down_turn = table_ref[3, f]
             here = shifted_ref[f]
-            plus_values = turn_rows(shifted_ref[up_freq], up_turn)
-            minus_values = turn_rows(shifted_ref[down_freq], ND - down_turn)
+            plus_values = turn_rows(shifted_ref[up_freq], up_turn, rows)
+            minus_values = turn_rows(shifted_ref[down_freq], ND - down_turn, rows)
             quartet = (
                 here * here * (plus_values + minus_values)
                 - 2.0 * here * plus_values * minus_values
             )
             quartet_ref[f] = quartet
-            source_ref[up_freq] = source_ref[up_freq] + turn_rows(quartet, ND - up_turn)
-            source_ref[down_freq] = source_ref[down_freq] + turn_rows(quartet, down_turn)
+            source_ref[up_freq] = source_ref[up_freq] + turn_rows(quartet, ND - up_turn, rows)
+            source_ref[down_freq] = source_ref[down_freq] + turn_rows(quartet, down_turn, rows)
             return carry
 
         lax.fori_loop(0, n_freq, interact, 0, unroll=True)

time: 68.7 us -> 68.5 us (level)
  no operation moved by 1% of the time
where the time goes in v15:
time: 68.5 us; the launch traced here: 68.1 us
  waiting for transfers between devices  30.4 us (44%)
  Pallas kernels  14.8 us (22%)
  starting transfers between devices  13.7 us (20%)
  other arithmetic  4.58 us (7%)
  local copies, waits for them, and re-layouts  4.46 us (7%)
    all_to_all x1, waiting for transfers between devices, shards(): lax.all_to_all(turned, 'spec', split_axis=0, concat_axis=0, tiled=True)  29.3 us
    all_to_all x1, starting transfers between devices, shards(): lax.all_to_all(turned, 'spec', split_axis=0, concat_axis=0, tiled=True)  9.8 us
    pallas_call x1, Pallas kernels, settle(): pl.pallas_call(settle_kernel, out_shape=jax.ShapeDtypeStruct((NF * ND, su...  7.05 us
    pallas_call x1, Pallas kernels, propagate(): pl.pallas_call(propagate_kernel, out_shape=jax.ShapeDtypeStruct((blocks,...  5 us
    ppermute x1, starting transfers between devices, neighbours(): lax.ppermute(edges_last, 'tile', [(i, (i + 1) % count) for i in range(cou...  3.86 us
    pallas_call x1, Pallas kernels, edges(): pl.pallas_call(edges_kernel, out_shape=(plane, plane), in_specs=[vmem] *...  2.8 us
    reduce_or x1, other arithmetic, sea_cells(): return jnp.any(matches, axis=1).astype(jnp.float32)  2.31 us
    unnamed x13, local copies, waits for them, and re-layouts  1.54 us
  transfers between devices with their start and end apart: 3, of which 2 were waited for; matrix products, arithmetic and copies ran while one was open for 7% of the time, Pallas kernels for 0%

profile of v15, /device:TPU:193, one launch (start us, length us, event | category | flops | bytes accessed | tf_op | source)
XLA Modules:
  0.0 68.1 jit_solution(13674402368426922812)
XLA Ops:
  0.0 0.8 %copy.25 = s32[32,1,192]{2,0,1:T(8,128)S(1)} copy(s32[32,1,192]{2,1,0:T(1,128)} %param.13) | data formatting | bytes 49152
  0.8 0.7 %iota_compare_fusion.1 = pred[32,192]{1,0:T(8,128)(4,1)S(1)} fusion(s32[32]{0:T(128)} %bitcast.30), kind=kLoop, calls=%fused_computation.5 | loop fusion | flops 6144 | bytes 6272 | tf_op jit(solution)/shard_map/lt | solution.py:46
  1.5 0.1 broadcast_add_fusion
  1.6 0.2 and_reduce_fusion
  1.8 0.7 %copy.19 = f32[32,2,2]{2,1,0:T(2,128)} copy(f32[32,2,2]{0,2,1:T(2,128)S(1)} %convert_element_type.26) | data formatting | bytes 1024 | tf_op jit(solution)/shard_map/convert_element_type | solution.py:40
  2.5 2.8 %shard_map.85 = (f32[64,128]{1,0:T(8,128)}, f32[64,128]{1,0:T(8,128)}) custom-call(f32[36,64,128]{2,1,0:T(8,128)} %spec_ref.3, f32[64,2]{1,0:T(8,128)} %bitcast.27, f32[64,128]{1,0:T(8,128)} %depth_ref.3), custom_call_target="tpu_custom_call" | custom-call | tf_op jit(solution)/shard_map/pallas_call | solution.py:302
  5.3 3.9 %collective-permute-start = (f32[64,128]{1,0:T(8,128)}, f32[64,128]{1,0:T(8,128)S(1)}, u32[]{:S(2)}, u32[]{:S(2)}) collective-permute-start(f32[64,128]{1,0:T(8,128)} %get-tuple-element.7), channel_id=1, source_target_pairs={{0,1},{1,2},{2,3},{3,4},{4,5},{5,6},{6,7},{7,8},{8,9},{9,10},{10,1... | collective-permute-start | bytes 98312 | tf_op jit(solution)/shard_map/ppermute | solution.py:221
  9.2 0.0 collective-permute-start.1
  9.2 2.3 %fusion.1 = pred[32,256]{1,0:T(8,128)(4,1)S(1)} fusion(s32[32,192]{1,0:T(8,128)S(1)} %bitcast.26, pred[32,192]{1,0:T(8,128)(4,1)S(1)} %iota_compare_fusion.1), kind=kLoop, calls=%fused_computation.2 | loop fusion | flops 4710400 | bytes 38912 | tf_op jit(solution)/shard_map/reduce_or | solution.py:48
  11.6 0.6 pad_maximum_fusion.coef_ref
  12.2 0.6 reshape.257.mask_ref
  12.8 0.0 collective-permute-done.west_ref
  12.8 0.0 copy-start.1
  12.8 1.1 %collective-permute-done.1.east_ref = f32[64,128]{1,0:T(8,128)S(1)} collective-permute-done((f32[64,128]{1,0:T(8,128)}, f32[64,128]{1,0:T(8,128)S(1)}, u32[]{:S(2)}, u32[]{:S(2)}) %collective-permute-start.1) | collective-permute-done | bytes 32800 | tf_op jit(solution)/shard_map/ppermute | solution.py:222
  13.9 0.0 copy-done.1
  13.9 0.0 copy-start.2
  13.9 0.6 copy-done.2
  14.5 5.0 %shard_map.86 = f32[32,72,128]{2,1,0:T(8,128)} custom-call(f32[2,36]{1,0:T(2,128)} %pad_maximum_fusion.coef_ref, f32[36,64,128]{2,1,0:T(8,128)} %spec_ref.3, f32[64,128]{1,0:T(8,128)} %reshape.257.mask_ref, f32[64,128]{1,0:T(8,128)} %depth_ref.3, f32[64,128]{1,0:T(8,128)} %turn_ref.1, f32[64,128]{1,0:T(8,128)} %copy-done.1, f32[64,128]{1,0:T(8,128)} %copy-done.2), custom_call_target="tpu_custom_call" | custom-call | tf_op jit(solution)/shard_map/pallas_call | solution.py:313
  19.5 0.0 copy-start.3
  19.5 0.0 copy-start.4
  19.6 9.8 %all-to-all-start = ((f32[32,72,128]{2,1,0:T(8,128)}), f32[32,72,128]{2,1,0:T(8,128)S(1)}, u32[]{:S(2)}, u32[]{:S(2)}) async-start(f32[32,72,128]{2,1,0:T(8,128)} %shard_map.86), calls=%async_computation | async-start | bytes 2359296 | tf_op jit(solution)/shard_map/all_to_all | solution.py:347
  29.4 0.0 copy-done.3
  29.4 0.1 reshape_squeeze.6
  29.5 0.1 copy.22
  29.6 0.1 reshape_squeeze.7
  29.7 0.1 copy.23
  29.8 0.0 copy-done.4
  29.8 0.1 reshape.256
  29.9 0.6 pad_add_fusion.table_ref
  30.5 29.3 %all-to-all-done.blocks_ref = f32[32,72,128]{2,1,0:T(8,128)S(1)} async-done(((f32[32,72,128]{2,1,0:T(8,128)}), f32[32,72,128]{2,1,0:T(8,128)S(1)}, u32[]{:S(2)}, u32[]{:S(2)}) %all-to-all-start) | async-done | bytes 1179680 | tf_op jit(solution)/shard_map/all_to_all | solution.py:347
  59.8 0.0 copy-start
  59.8 1.3 %broadcast_in_dim.2.drift_ref = f32[32,40,128]{2,1,0:T(8,128)} broadcast(f32[32,40]{1,0:T(8,128)S(1)} %pad.4), dimensions={0,1} | broadcast | bytes 660480 | tf_op jit(solution)/shard_map/broadcast_in_dim | solution.py:206
  61.0 0.0 copy-done
  61.0 7.0 %shard_map.87 = f32[1152,2,128]{2,1,0:T(2,128)} custom-call(s32[4,32]{1,0:T(4,128)} %pad_add_fusion.table_ref, f32[32,72,128]{2,1,0:T(8,128)} %copy-done, f32[32,40,128]{2,1,0:T(8,128)} %broadcast_in_dim.2.drift_ref), custom_call_target="tpu_custom_call" | custom-call | tf_op jit(solution)/shard_map/pallas_call | solution.py:209
  (7 shorter events, 0.1 us)
Async XLA Ops:
  5.3 7.5 %collective-permute-start = (f32[64,128]{1,0:T(8,128)}, f32[64,128]{1,0:T(8,128)S(1)}, u32[]{:S(2)}, u32[]{:S(2)}) collective-permute-start(f32[64,128]{1,0:T(8,128)} %get-tuple-element.7), channel_id=1, source_target_pairs={{0,1},{1,2},{2,3},{3,4},{4,5},{5,6},{6,7},{7,8},{8,9},{9,10},{10,1... | collective-permute-start | bytes 98312 | tf_op jit(solution)/shard_map/ppermute | solution.py:221
  9.2 4.8 %collective-permute-start.1 = (f32[64,128]{1,0:T(8,128)}, f32[64,128]{1,0:T(8,128)S(1)}, u32[]{:S(2)}, u32[]{:S(2)}) collective-permute-start(f32[64,128]{1,0:T(8,128)} %get-tuple-element.8), channel_id=1, source_target_pairs={{1,0},{2,1},{3,2},{4,3},{5,4},{6,5},{7,6},{8,7},{9,8},{10,9},{11,1... | collective-permute-start | bytes 98312 | tf_op jit(solution)/shard_map/ppermute | solution.py:222
  12.8 1.1 %copy-start.1 = (f32[64,128]{1,0:T(8,128)}, f32[64,128]{1,0:T(8,128)S(1)}, u32[]{:S(2)}) copy-start(f32[64,128]{1,0:T(8,128)S(1)} %collective-permute-done.west_ref) | copy-start | bytes 98308
  13.9 0.6 copy-start.2
  19.5 9.8 %copy-start.3 = (s32[2,1152]{1,0:T(2,128)S(1)}, s32[2,1152]{1,0:T(2,128)}, u32[]{:S(2)}) copy-start(s32[2,1152]{1,0:T(2,128)} %param.12) | copy-start | bytes 27652
  19.5 10.2 %copy-start.4 = (f32[1152]{0:T(1024)S(1)}, f32[1152]{0:T(1024)}, u32[]{:S(2)}) copy-start(f32[1152]{0:T(1024)} %param.11) | copy-start | bytes 13828
  19.6 40.2 %all-to-all-start = ((f32[32,72,128]{2,1,0:T(8,128)}), f32[32,72,128]{2,1,0:T(8,128)S(1)}, u32[]{:S(2)}, u32[]{:S(2)}) async-start(f32[32,72,128]{2,1,0:T(8,128)} %shard_map.86), calls=%async_computation | async-start | bytes 2359296 | tf_op jit(solution)/shard_map/all_to_all | solution.py:347
  59.8 1.3 %copy-start = (f32[32,72,128]{2,1,0:T(8,128)}, f32[32,72,128]{2,1,0:T(8,128)S(1)}, u32[]{:S(2)}) copy-start(f32[32,72,128]{2,1,0:T(8,128)S(1)} %all-to-all-done.blocks_ref) | copy-start | bytes 3538948
